TPU v7x, 256 devices: a whole 4x4x8 slice. The times are simulated.
256 devices in a mesh: req: 64 (over z_hi, x, y, core), tp: 4 (over z_lo).
Axes of the slice: x: 4, y: 4, z: 8 (z_hi: 2, z_lo: 4; z = z_hi * 4 + z_lo), core: 2. Of those that a mesh axis runs over, the one named last changes fastest.
Arguments:
- layer_in: bfloat16 [8192, 2048], P('req'), may hold values from -15 to 15
- q_nope: bfloat16 [8192, 2048], P('req', 'tp'), may hold values from -6 to 6
- q_pe: bfloat16 [8192, 1024], P('req', 'tp'), may hold values from -100 to 100
- kv_cache: bfloat16 [128, 1024, 576], P('req'), may hold values from -6 to 6
- lengths: int32 [128], P('req'), may hold values from 2 to 1024, as said below
- parents: int32 [128, 64], P('req'), may hold values from 0 to 62, as said below
- accepted: int32 [128], P('req'), may hold values from 0 to 63
- kv_a: bfloat16 [2048, 576], P(None, 'tp'), may hold values from -0.125 to 0.125
- kv_gain: float32 [512], replicated, may hold values from 0.1 to 1.9
- w_uk: bfloat16 [2048, 512], P('tp'), may hold values from -0.5 to 0.5
- w_uv: bfloat16 [512, 2048], P(None, 'tp'), may hold values from -0.25 to 0.25
- o_proj: bfloat16 [2048, 2048], P('tp'), may hold values from -0.125 to 0.125
- post_gain: float32 [2048], replicated, may hold values from 0.1 to 1.9
- routes: int32 [8192, 6], P('req'), may hold values from 0 to 63, all different within a row; in each aligned block of 128 rows (0 to 127, 128 to 255, ...) at most 16 rows name the same one
- gates: bfloat16 [8192, 6], P('req'), may hold values from 0.14941406 to 0.59765625
- w_gate: bfloat16 [64, 2048, 1408], P('req', None, 'tp'), may hold values from -0.125 to 0.125
- w_up: bfloat16 [64, 2048, 1408], P('req', None, 'tp'), may hold values from -0.125 to 0.125
- w_down: bfloat16 [64, 1408, 2048], P('req', 'tp'), may hold values from -0.15625 to 0.15625
Outputs:
- layer_out: bfloat16 [8192, 2048], P('req', 'tp')
- accepted_rows: bfloat16 [128, 64, 576], P('req')
Inputs may be any that keep to these rules, and one draw needn't show every extreme that they name: `lengths`: at least one request of every draw has 1024 live slots. parents[r, 0] = 0; for i >= 1, parents[r, i] lies from i - 4 to i - 1. `routes`: the 6 experts of a token differ; within each aligned block of 128 rows (the tokens of one device) no expert is named more than 16 times.
All inputs are finite; a program needn't handle non-finite values.
Results may differ from a plain program's by a relative error of at most 0.012.
Values may be sent and summed in bfloat16 or wider, within the bound.
No kernel may reach another device: no remote copies, remote signals or barrier semaphores. Data moves between devices by JAX's collectives and lax.ppermute only.
A program may use at most 128 MiB of HBM per device.

v0:
```python
import jax
import jax.numpy as jnp
from jax import lax
from jax.sharding import PartitionSpec as P

D = 2048
NOPE = 128
ROPE = 64
VDIM = 128
LATENT = 512


epsilon = 1e-06


def ancestors(parent_row):
    tree_size = parent_row.shape[0]
    indices = jnp.arange(tree_size, dtype=jnp.int32)
    link = (
        (parent_row[:, None] == indices[None, :]) | (indices[:, None] == indices[None, :])
    ).astype(jnp.float32)
    for repeat_index in range(tree_size.bit_length()):
        link = jnp.minimum(jnp.dot(link, link, precision=lax.Precision.HIGHEST), 1.0)
    return link


def rotate(vector, positions):
    half_width = vector.shape[-1] // 2
    frequency = 10000.0 ** (-jnp.arange(half_width, dtype=jnp.float32) / half_width)
    angles = positions[:, None] * frequency[None, :]
    first_half = vector[:, :half_width]
    second_half = vector[:, half_width:]
    return jnp.concatenate(
        [
            first_half * jnp.cos(angles) - second_half * jnp.sin(angles),
            first_half * jnp.sin(angles) + second_half * jnp.cos(angles),
        ],
        -1,
    )


def make_rows(compressed, kv_gain, positions):
    latent_raw = compressed[:, :LATENT].astype(jnp.float32)
    new_latent = (
        latent_raw
        * lax.rsqrt(jnp.mean(latent_raw * latent_raw, -1, keepdims=True) + epsilon)
        * kv_gain
    ).astype(jnp.bfloat16)
    new_rotary = rotate(compressed[:, LATENT:].astype(jnp.float32), positions).astype(jnp.bfloat16)
    return jnp.concatenate([new_latent, new_rotary], -1)


def compact(ancestry, depths, node_index, row_set):
    tree_size = ancestry.shape[0]
    chain_mask = jnp.take(ancestry, node_index, axis=0)
    selector = (depths[None, :] == jnp.arange(tree_size, dtype=jnp.float32)[:, None]).astype(
        jnp.float32
    ) * chain_mask[None, :]
    return jnp.dot(
        selector.astype(jnp.bfloat16), row_set, preferred_element_type=jnp.float32
    ).astype(jnp.bfloat16)


def attend_request(q_rows, cache_r, length, new_r, mask_rows):
    score_scale = (NOPE + ROPE) ** (-0.5)
    cache_slots = cache_r.shape[0]
    block_size = min(cache_slots, 512)
    block_total = cache_slots // block_size
    offsets = jnp.arange(block_size, dtype=jnp.int32)
    tree_scores = jnp.dot(q_rows, new_r.T, preferred_element_type=jnp.float32) * score_scale
    tree_scores = jnp.where(mask_rows, tree_scores, -jnp.inf)

    def block_scores(block_index):
        key_block = lax.dynamic_slice_in_dim(cache_r, block_index * block_size, block_size, 0)
        scores = jnp.dot(q_rows, key_block.T, preferred_element_type=jnp.float32) * score_scale
        valid = block_index * block_size + offsets < length
        return (jnp.where(valid[None, :], scores, -jnp.inf), key_block)

    def raise_max(block_index, row_max):
        scores, key_block = block_scores(block_index)
        return jnp.maximum(row_max, jnp.max(scores, -1))

    row_max = lax.fori_loop(0, block_total, raise_max, jnp.max(tree_scores, -1))
    tree_exps = jnp.exp(tree_scores - row_max[:, None])
    start_totals = jnp.sum(tree_exps, -1)
    start_sums = jnp.dot(
        tree_exps.astype(jnp.bfloat16), new_r[:, :LATENT], preferred_element_type=jnp.float32
    )

    def accumulate(block_index, carry):
        totals, weighted = carry
        scores, key_block = block_scores(block_index)
        exps = jnp.exp(scores - row_max[:, None])
        weighted = weighted + jnp.dot(
            exps.astype(jnp.bfloat16), key_block[:, :LATENT], preferred_element_type=jnp.float32
        )
        return (totals + jnp.sum(exps, -1), weighted)

    totals, weighted = lax.fori_loop(0, block_total, accumulate, (start_totals, start_sums))
    return (weighted / totals[:, None]).astype(jnp.bfloat16)


def attend_dense(q_rows, cache, lengths, new_rows, mask_rows):
    score_scale = (NOPE + ROPE) ** (-0.5)
    cache_slots = cache.shape[1]
    cache_scores = (
        jnp.einsum("rqk,rck->rqc", q_rows, cache, preferred_element_type=jnp.float32) * score_scale
    )
    valid = jnp.arange(cache_slots, dtype=jnp.int32)[None, :] < lengths[:, None]
    cache_scores = jnp.where(valid[:, None, :], cache_scores, -jnp.inf)
    tree_scores = (
        jnp.einsum("rqk,ruk->rqu", q_rows, new_rows, preferred_element_type=jnp.float32)
        * score_scale
    )
    tree_scores = jnp.where(mask_rows, tree_scores, -jnp.inf)
    row_max = jnp.maximum(jnp.max(cache_scores, -1), jnp.max(tree_scores, -1))
    cache_exps = jnp.exp(cache_scores - row_max[..., None])
    tree_exps = jnp.exp(tree_scores - row_max[..., None])
    totals = jnp.sum(cache_exps, -1) + jnp.sum(tree_exps, -1)
    summed = jnp.einsum(
        "rqc,rck->rqk", cache_exps.astype(jnp.bfloat16), cache, preferred_element_type=jnp.float32
    )
    summed = summed + jnp.einsum(
        "rqu,ruk->rqk", tree_exps.astype(jnp.bfloat16), new_rows, preferred_element_type=jnp.float32
    )
    return (summed[..., :LATENT] / totals[..., None]).astype(jnp.bfloat16)


def route_tables(routes, gates, experts_all, capacity):
    tok_rows, top_count = routes.shape
    flat_ids = routes.reshape(-1)
    pair_count = flat_ids.shape[0]
    hit_table = (flat_ids[:, None] == jnp.arange(experts_all, dtype=jnp.int32)[None, :]).astype(
        jnp.bfloat16
    )
    earlier = (
        jnp.arange(pair_count, dtype=jnp.int32)[:, None]
        > jnp.arange(pair_count, dtype=jnp.int32)[None, :]
    ).astype(jnp.bfloat16)
    before = jnp.dot(earlier, hit_table, preferred_element_type=jnp.float32)
    slot_rank = jnp.sum(before * hit_table.astype(jnp.float32), -1).astype(jnp.int32)
    slot_index = flat_ids * capacity + slot_rank
    places = (
        slot_index[:, None] == jnp.arange(experts_all * capacity, dtype=jnp.int32)[None, :]
    ).reshape(tok_rows, top_count, -1)
    pick_table = jnp.any(places, 1).astype(jnp.bfloat16)
    weights = jnp.sum(jnp.where(places, gates[:, :, None], jnp.zeros((), jnp.bfloat16)), 1)
    return (pick_table, weights)


def run_expert(row_set, w_gate, w_up, w_down):
    local_experts = w_gate.shape[0]
    sources = row_set.shape[0] // local_experts
    grouped = row_set.reshape(sources, local_experts, row_set.shape[1], row_set.shape[2])
    gate_act = jnp.einsum("secd,edf->secf", grouped, w_gate, preferred_element_type=jnp.float32)
    up_act = jnp.einsum("secd,edf->secf", grouped, w_up, preferred_element_type=jnp.float32)
    hidden = (jax.nn.silu(gate_act) * up_act).astype(jnp.bfloat16)
    partial_value = jnp.einsum("secf,efd->secd", hidden, w_down, preferred_element_type=jnp.float32)
    return partial_value.reshape(sources * local_experts, row_set.shape[1], -1)


def on_device(
    layer_in,
    q_nope,
    q_pe,
    kv_cache,
    lengths,
    parents,
    accepted,
    kv_a,
    kv_gain,
    w_uk,
    w_uv,
    o_proj,
    post_gain,
    routes,
    gates,
    w_gate,
    w_up,
    w_down,
):
    tok_rows = layer_in.shape[0]
    local_requests, tree_size = parents.shape
    local_heads = q_nope.shape[1] // NOPE
    compressed_part = jnp.dot(layer_in, kv_a, preferred_element_type=jnp.float32).astype(
        jnp.bfloat16
    )
    compressed = lax.all_gather(compressed_part, "tp", axis=1, tiled=True)
    ancestry = jax.vmap(ancestors)(parents)
    depths = jnp.sum(ancestry, -1) - 1.0
    positions = (lengths.astype(jnp.float32)[:, None] + depths).reshape(-1)
    new_rows = make_rows(compressed, kv_gain, positions)
    rows_by_request = new_rows.reshape(local_requests, tree_size, -1)
    accepted_rows = jax.vmap(compact)(ancestry, depths, accepted, rows_by_request)
    query_latent = jnp.einsum(
        "thn,hnl->thl",
        q_nope.reshape(tok_rows, local_heads, NOPE),
        w_uk.reshape(local_heads, NOPE, LATENT),
        preferred_element_type=jnp.float32,
    ).astype(jnp.bfloat16)
    queries = jnp.concatenate([query_latent, q_pe.reshape(tok_rows, local_heads, ROPE)], -1)
    q_rows = queries.reshape(local_requests, tree_size * local_heads, -1)
    mask_rows = jnp.repeat(ancestry > 0, local_heads, axis=1)
    latent_out = attend_dense(q_rows, kv_cache, lengths, rows_by_request, mask_rows)
    latent_out = latent_out.reshape(tok_rows, local_heads, LATENT)
    head_out = jnp.einsum(
        "thl,lhv->thv",
        latent_out,
        w_uv.reshape(LATENT, local_heads, VDIM),
        preferred_element_type=jnp.float32,
    ).astype(jnp.bfloat16)
    experts_all = w_gate.shape[0] * lax.axis_size("req")
    top_count = routes.shape[1]
    capacity = 4 * tok_rows * top_count // (3 * experts_all)
    pick_table, weights = route_tables(routes, gates, experts_all, capacity)
    tp_size = lax.axis_size("tp")
    tp_index = lax.axis_index("tp")
    quarter = D // tp_size
    attention_parts = jnp.einsum(
        "tk,kqf->qtf",
        head_out.reshape(tok_rows, local_heads * VDIM),
        o_proj.reshape(o_proj.shape[0], tp_size, quarter),
        preferred_element_type=jnp.float32,
    )
    attention_quarter = lax.psum_scatter(attention_parts, "tp", scatter_dimension=0, tiled=True)
    attention_quarter = attention_quarter.reshape(tok_rows, quarter)
    hidden_quarter = lax.dynamic_slice_in_dim(layer_in, tp_index * quarter, quarter, 1)
    residual_quarter = hidden_quarter.astype(jnp.float32) + attention_quarter
    square_sum = lax.psum(jnp.sum(residual_quarter * residual_quarter, -1, keepdims=True), "tp")
    gain_quarter = lax.dynamic_slice_in_dim(post_gain, tp_index * quarter, quarter, 0)
    normed_quarter = (
        residual_quarter * lax.rsqrt(square_sum / D + epsilon) * gain_quarter
    ).astype(jnp.bfloat16)
    parity = tp_index % 2
    upper = tp_index // 2
    across = [(t, t ^ 2) for t in range(tp_size)]
    beside = [(t, t ^ 1) for t in range(tp_size)]
    other_quarter = lax.ppermute(normed_quarter, "tp", across)
    half_rows = jnp.where(
        upper == 0,
        jnp.concatenate([normed_quarter, other_quarter], 1),
        jnp.concatenate([other_quarter, normed_quarter], 1),
    )
    outgoing = lax.dot_general(
        pick_table, half_rows, (((0,), (0,)), ((), ())), preferred_element_type=jnp.float32
    ).astype(jnp.bfloat16)
    outgoing = outgoing.reshape(experts_all, capacity, 2 * quarter)

    def features(block, first):
        return lax.dynamic_slice_in_dim(block, first * quarter, quarter, block.ndim - 1)

    chunks = 1
    slot_step = capacity // chunks
    weights_by_slot = weights.reshape(tok_rows, experts_all, capacity)
    routed_half = jnp.zeros((tok_rows, 2 * quarter), jnp.float32)
    for chunk in range(chunks):
        slots = slice(chunk * slot_step, (chunk + 1) * slot_step)
        own_rows = lax.all_to_all(outgoing[:, slots], "req", split_axis=0, concat_axis=0, tiled=True)
        partner_rows = lax.ppermute(own_rows, "tp", beside)
        low_own, high_own = own_rows[..., :quarter], own_rows[..., quarter:]
        low_partner, high_partner = partner_rows[..., :quarter], partner_rows[..., quarter:]
        row_set = jnp.where(
            parity == 0,
            jnp.concatenate([low_own, low_partner, high_own, high_partner], -1),
            jnp.concatenate([low_partner, low_own, high_partner, high_own], -1),
        )
        gate_act = jnp.einsum("scf,fh->sch", row_set, w_gate[0], preferred_element_type=jnp.float32)
        up_act = jnp.einsum("scf,fh->sch", row_set, w_up[0], preferred_element_type=jnp.float32)
        expert_hidden = (jax.nn.silu(gate_act) * up_act).astype(jnp.bfloat16)
        value = jnp.einsum(
            "sch,hf->scf", expert_hidden, w_down[0], preferred_element_type=jnp.float32
        )
        partner_value = jnp.concatenate(
            [features(value, 1 - parity), features(value, 3 - parity)], -1
        ).astype(jnp.bfloat16)
        arrived_value = lax.ppermute(partner_value, "tp", beside)
        own_value = jnp.concatenate([features(value, parity), features(value, parity + 2)], -1)
        pair_value = (own_value + arrived_value.astype(jnp.float32)).astype(jnp.bfloat16)
        shares = lax.all_to_all(pair_value, "req", split_axis=0, concat_axis=0, tiled=True)
        routed_half = routed_half + jnp.dot(
            weights_by_slot[:, :, slots].reshape(tok_rows, experts_all * slot_step),
            shares.reshape(experts_all * slot_step, 2 * quarter),
            preferred_element_type=jnp.float32,
        )
    keep = features(routed_half, upper)
    give = features(routed_half, 1 - upper)
    routed = keep + lax.ppermute(give, "tp", across)
    layer_out = (residual_quarter + routed).astype(jnp.bfloat16)
    return (layer_out, accepted_rows)


def solution(mesh):
    return jax.shard_map(
        on_device,
        mesh=mesh,
        in_specs=(
            P("req", None),
            P("req", "tp"),
            P("req", "tp"),
            P("req", None, None),
            P("req"),
            P("req", None),
            P("req"),
            P(None, "tp"),
            P(),
            P("tp", None),
            P(None, "tp"),
            P("tp", None),
            P(),
            P("req", None),
            P("req", None),
            P("req", None, "tp"),
            P("req", None, "tp"),
            P("req", "tp", None),
        ),
        out_specs=(P("req", "tp"), P("req", None, None)),
        check_vma=False,
    )
```

profile of v0, /device:TPU:1, one launch (start us, length us, event | category | flops | bytes accessed | tf_op | source)
XLA Modules:
  0.0 367.1 jit_solution(7415623347455324733)
XLA Ops:
  7.3 1.7 convolution_convert_fusion.4
  9.0 13.4 %all_gather.3 = bf16[128,576]{0,1:T(8,128)(2,1)S(1)} all-gather(bf16[128,144]{0,1:T(8,128)(2,1)S(1)} %convolution_convert_fusion.4), channel_id=1, replica_groups=mesh['req'=64,'tp'=4] {'tp'}, dimensions={1}, use_global_device_ids=true | all-gather | bytes 184320 | tf_op jit(solution)/shard_map/all_gather | solution.py:188
  22.5 0.7 convert_element_type.94
  23.2 0.7 iota_compare_fusion.12
  23.9 1.0 convolution_minimum_fusion.6
  24.9 0.2 convolution_minimum_fusion.5
  25.1 0.2 convolution_minimum_fusion.4
  25.3 0.2 convolution_minimum_fusion.3
  25.5 0.2 convolution_minimum_fusion.2
  25.7 0.2 convolution_minimum_fusion.1
  25.9 0.3 fusion.79
  26.3 0.1 fusion.38
  26.5 0.1 fusion.66
  26.6 0.8 copy.73
  27.5 0.7 copy.74
  28.3 0.3 fusion.21
  28.6 0.4 copy.68
  29.0 0.1 concatenate.33
  29.1 1.0 copy.69
  30.1 0.1 concatenate.34
  30.3 1.4 fusion.80
  31.8 2.2 fusion.7
  34.1 0.4 fusion.51
  34.4 0.6 fusion.8
  35.0 1.1 fusion.25
  36.1 0.2 fusion.28
  36.3 0.9 reshape.161
  37.2 1.3 copy.84
  38.5 1.4 convolution_convert_fusion.3
  39.9 3.1 fusion.16
  43.1 0.1 eq.86
  43.3 0.4 fusion.24
  43.7 0.1 convert_element_type.103
  43.9 0.8 dynamic_slice.25
  44.7 34.5 %reduce-scatter.2.cloned.1.call-done = f32[1,128,512]{2,1,0:T(8,128)} async-done(((f32[4,128,512]{2,1,0:T(8,128)}), f32[1,128,512]{2,1,0:T(8,128)}) %reduce-scatter.2.cloned.1.call-update) | async-done | bytes 262160 | tf_op jit(solution)/shard_map/reduce_scatter | solution.py:225
  79.2 1.1 multiply_reduce_fusion
  80.2 7.4 %psum.7 = f32[128,1]{0,1:T(1,128)S(1)} all-reduce(f32[128,1]{0,1:T(1,128)S(1)} %bitcast.93), channel_id=1, replica_groups=mesh['req'=64,'tp'=4] {'tp'}, use_global_device_ids=true, to_apply=%region_11.12 | all-reduce | flops 128 | bytes 1024 | tf_op jit(solution)/shard_map/psum | solution.py:229
  87.7 1.0 multiply_convert_fusion.1
  88.8 0.5 fusion.1
  89.3 5.6 %collective-permute-done = bf16[128,512]{1,0:T(8,128)(2,1)S(1)} collective-permute-done((bf16[128,512]{1,0:T(8,128)(2,1)S(1)}, bf16[128,512]{1,0:T(8,128)(2,1)S(1)}, u32[]{:S(2)}, u32[]{:S(2)}) %collective-permute-start) | collective-permute-done | bytes 131104 | tf_op jit(solution)/shard_map/ppermute | solution.py:238
  94.9 0.8 convolution_convert_fusion
  95.7 66.9 %all_to_all.10 = bf16[64,16,1024]{2,1,0:T(8,128)(2,1)} all-to-all(bf16[64,16,1024]{2,1,0:T(8,128)(2,1)S(1)} %bitcast.84), channel_id=1, replica_groups=mesh['req'=64,'tp'=4] {'req'}, dimensions={0} | all-to-all | bytes 4194304 | tf_op jit(solution)/shard_map/all_to_all | solution.py:258
  162.6 1.7 fusion.77
  164.3 45.5 %collective-permute-done.1 = bf16[64,16,1024]{2,1,0:T(8,128)(2,1)} collective-permute-done((bf16[64,16,1024]{2,1,0:T(8,128)(2,1)}, bf16[64,16,1024]{2,1,0:T(8,128)(2,1)}, u32[]{:S(2)}, u32[]{:S(2)}) %collective-permute-start.1) | collective-permute-done | bytes 2097184 | tf_op jit(solution)/shard_map/ppermute | solution.py:259
  209.8 1.7 fusion.78
  211.6 1.0 copy-done.6
  212.5 0.4 copy-done.7
  212.9 3.4 fusion.14
  216.3 10.3 %fusion.11 = f32[64,16,2048]{2,1,0:T(8,128)} fusion(bf16[1,352,2048]{2,1,0:T(8,128)(2,1)} %param.35, f32[64,16,352]{2,1,0:T(8,128)} %fusion.14, bf16[1,2048,352]{1,2,0:T(8,128)(2,1)} %param.34, bf16[64,16,512]{2,1,0:T(8,128)(2,1)} %copy-done.7, bf16[64,16,512]{2,1,0:T(8,128)(2,1)} %copy-done.5, bf16[64,16,512]{2,1,0:T(8,128)(2,1)} %copy-done.6, ...), kind=kOutput, calls=%fused_computation.23 | convolution fusion | flops 2990604288 | bytes 16908288 | tf_op jit(solution)/shard_map/sch,hf->scf/dot_general | solution.py:270
  226.6 2.6 dynamic-slice_convert_fusion.1
  229.2 1.6 pad_maximum_fusion
  230.8 2.7 constant_dynamic-slice_fusion.2
  233.5 43.7 %collective-permute-done.2 = bf16[64,16,1024]{2,1,0:T(8,128)(2,1)} collective-permute-done((bf16[64,16,1024]{2,1,0:T(8,128)(2,1)}, bf16[64,16,1024]{2,1,0:T(8,128)(2,1)}, u32[]{:S(2)}, u32[]{:S(2)}) %collective-permute-start.2) | collective-permute-done | bytes 2097184 | tf_op jit(solution)/shard_map/ppermute | solution.py:276
  277.1 3.9 %fusion = bf16[64,16,1024]{2,1,0:T(8,128)(2,1)} fusion(f32[64,16,512]{2,1,0:T(8,128)S(1)} %get-tuple-element.5, f32[64,16,512]{2,1,0:T(8,128)S(1)} %get-tuple-element.4, bf16[64,16,1024]{2,1,0:T(8,128)(2,1)} %collective-permute-done.2), kind=kLoop, calls=%fused_computation.3 | loop fusion | flops 4194304 | bytes 8388608 | tf_op jit(solution)/shard_map/convert_element_type | solution.py:278
  281.0 8.3 %all-to-all-start.1 = ((bf16[64,16,1024]{2,1,0:T(8,128)(2,1)}), bf16[64,16,1024]{2,1,0:T(8,128)(2,1)}, u32[]{:S(2)}, u32[]{:S(2)}) async-start(bf16[64,16,1024]{2,1,0:T(8,128)(2,1)} %fusion), calls=%async_computation.2 | async-start | bytes 4194304 | tf_op jit(solution)/shard_map/all_to_all | solution.py:279
  289.3 0.6 gather_fusion
  289.9 1.1 fusion.10
  291.0 45.6 %all-to-all-done.1 = bf16[64,16,1024]{2,1,0:T(8,128)(2,1)} async-done(((bf16[64,16,1024]{2,1,0:T(8,128)(2,1)}), bf16[64,16,1024]{2,1,0:T(8,128)(2,1)}, u32[]{:S(2)}, u32[]{:S(2)}) %all-to-all-start.1) | async-done | bytes 2097184 | tf_op jit(solution)/shard_map/all_to_all | solution.py:279
  336.6 2.1 fusion.81
  338.8 0.7 constant_dynamic-slice_fusion
  339.5 6.7 %collective-permute-start.3 = (f32[128,512]{1,0:T(8,128)}, f32[128,512]{1,0:T(8,128)}, u32[]{:S(2)}, u32[]{:S(2)}) collective-permute-start(f32[128,512]{1,0:T(8,128)} %constant_dynamic-slice_fusion), channel_id=1, source_target_pairs={{0,2},{1,3},{2,0},{3,1},{4,6},{5,7},{6,4},{7,5},{8,10},{9,11},{10,... | collective-permute-start | bytes 786440 | tf_op jit(solution)/shard_map/ppermute | solution.py:287
  346.3 0.8 convolution_convert_fusion.2
  347.1 11.4 %collective-permute-done.3 = f32[128,512]{1,0:T(8,128)} collective-permute-done((f32[128,512]{1,0:T(8,128)}, f32[128,512]{1,0:T(8,128)}, u32[]{:S(2)}, u32[]{:S(2)}) %collective-permute-start.3) | collective-permute-done | bytes 262176 | tf_op jit(solution)/shard_map/ppermute | solution.py:287
  358.5 1.7 add_convert_fusion
  (57 shorter events, 1.0 us)
Async XLA Ops:
  7.2 24.6 %copy-start = (bf16[2,1024,576]{1,2,0:T(8,128)(2,1)S(1)}, bf16[2,1024,576]{1,2,0:T(8,128)(2,1)}, u32[]{:S(2)}) copy-start(bf16[2,1024,576]{1,2,0:T(8,128)(2,1)} %param.21) | copy-start | bytes 7077892
  7.2 19.1 %copy-start.12 = (f32[512]{0:T(512)S(1)}, f32[512]{0:T(512)}, u32[]{:S(2)}) copy-start(f32[512]{0:T(512)} %param.26) | copy-start | bytes 6148
  7.2 21.1 %copy-start.8 = (bf16[512,512]{1,0:T(8,128)(2,1)S(1)}, bf16[512,512]{1,0:T(8,128)(2,1)}, u32[]{:S(2)}) copy-start(bf16[512,512]{1,0:T(8,128)(2,1)} %param.27) | copy-start | bytes 1572868
  7.2 21.1 %copy-start.9 = (bf16[128,512]{1,0:T(8,128)(2,1)S(1)}, bf16[128,512]{1,0:T(8,128)(2,1)}, u32[]{:S(2)}) copy-start(bf16[128,512]{1,0:T(8,128)(2,1)} %param.19) | copy-start | bytes 393220
  7.2 71.9 %reduce-scatter.2.cloned.1.call-start = ((), (), s32[]{:S(2)}) async-start(), calls=%async_computation.3 | async-start | bytes 1310720 | tf_op jit(solution)/shard_map/reduce_scatter | solution.py:225
  28.3 1.8 copy-start.10
  31.7 2.3 copy-start.3
  39.8 3.2 copy-start.11
  39.9 39.3 %copy-start.2 = (bf16[128,2048]{1,0:T(8,128)(2,1)S(1)}, bf16[128,2048]{1,0:T(8,128)(2,1)}, u32[]{:S(2)}) copy-start(bf16[128,2048]{1,0:T(8,128)(2,1)} %param.18) | copy-start | bytes 1572868
  88.7 6.2 %collective-permute-start = (bf16[128,512]{1,0:T(8,128)(2,1)S(1)}, bf16[128,512]{1,0:T(8,128)(2,1)S(1)}, u32[]{:S(2)}, u32[]{:S(2)}) collective-permute-start(bf16[128,512]{1,0:T(8,128)(2,1)S(1)} %multiply_convert_fusion.1), channel_id=1, source_target_pairs={{0,2},{1,3},{2,0},{3,1},{4,6},{5,7},{6,4},{7,5},{8,10},{9,11},{10,... | collective-permute-start | bytes 393224 | tf_op jit(solution)/shard_map/ppermute | solution.py:238
  162.6 47.2 %collective-permute-start.1 = (bf16[64,16,1024]{2,1,0:T(8,128)(2,1)}, bf16[64,16,1024]{2,1,0:T(8,128)(2,1)}, u32[]{:S(2)}, u32[]{:S(2)}) collective-permute-start(bf16[64,16,1024]{2,1,0:T(8,128)(2,1)} %all_to_all.10), channel_id=1, source_target_pairs={{0,1},{1,0},{2,3},{3,2},{4,5},{5,4},{6,7},{7,6},{8,9},{9,8},{10,11... | collective-permute-start | bytes 6291464 | tf_op jit(solution)/shard_map/ppermute | solution.py:259
  164.3 47.2 %copy-start.4 = (bf16[64,16,512]{2,1,0:T(8,128)(2,1)}, bf16[64,16,512]{2,1,0:T(8,128)(2,1)S(1)}, u32[]{:S(2)}) copy-start(bf16[64,16,512]{2,1,0:T(8,128)(2,1)S(1)} %get-tuple-element.6) | copy-start | bytes 3145732
  164.3 47.2 %copy-start.5 = (bf16[64,16,512]{2,1,0:T(8,128)(2,1)}, bf16[64,16,512]{2,1,0:T(8,128)(2,1)S(1)}, u32[]{:S(2)}) copy-start(bf16[64,16,512]{2,1,0:T(8,128)(2,1)S(1)} %get-tuple-element.7) | copy-start | bytes 3145732
  164.3 48.6 %copy-start.14 = (bf16[1,2048,352]{1,2,0:T(8,128)(2,1)S(1)}, bf16[1,2048,352]{1,2,0:T(8,128)(2,1)}, u32[]{:S(2)}) copy-start(bf16[1,2048,352]{1,2,0:T(8,128)(2,1)} %param.33) | copy-start | bytes 4325380
  211.5 1.0 copy-start.6
  211.5 1.4 copy-start.7
  230.8 46.4 %collective-permute-start.2 = (bf16[64,16,1024]{2,1,0:T(8,128)(2,1)}, bf16[64,16,1024]{2,1,0:T(8,128)(2,1)}, u32[]{:S(2)}, u32[]{:S(2)}) collective-permute-start(bf16[64,16,1024]{2,1,0:T(8,128)(2,1)} %pad_maximum_fusion), channel_id=1, source_target_pairs={{0,1},{1,0},{2,3},{3,2},{4,5},{5,4},{6,7},{7,6},{8,9},{9,8},{10,11... | collective-permute-start | bytes 6291464 | tf_op jit(solution)/shard_map/ppermute | solution.py:276
  281.0 8.3 %copy-start.15 = (s32[2]{0:T(128)S(1)}, s32[2]{0:T(128)}, u32[]{:S(2)}) copy-start(s32[2]{0:T(128)} %param.24) | copy-start | bytes 28
  281.0 8.9 %copy-start.13 = (bf16[128,6]{0,1:T(8,128)(2,1)S(1)}, bf16[128,6]{0,1:T(8,128)(2,1)}, u32[]{:S(2)}) copy-start(bf16[128,6]{0,1:T(8,128)(2,1)} %param.32) | copy-start | bytes 4612
  281.0 55.6 %all-to-all-start.1 = ((bf16[64,16,1024]{2,1,0:T(8,128)(2,1)}), bf16[64,16,1024]{2,1,0:T(8,128)(2,1)}, u32[]{:S(2)}, u32[]{:S(2)}) async-start(bf16[64,16,1024]{2,1,0:T(8,128)(2,1)} %fusion), calls=%async_computation.2 | async-start | bytes 4194304 | tf_op jit(solution)/shard_map/all_to_all | solution.py:279
  289.3 69.2 %copy-start.1 = (f32[1,128,512]{2,1,0:T(8,128)S(1)}, f32[1,128,512]{2,1,0:T(8,128)}, u32[]{:S(2)}) copy-start(f32[1,128,512]{2,1,0:T(8,128)} %reduce-scatter.2.cloned.1.call-done) | copy-start | bytes 786436
  339.5 19.0 %collective-permute-start.3 = (f32[128,512]{1,0:T(8,128)}, f32[128,512]{1,0:T(8,128)}, u32[]{:S(2)}, u32[]{:S(2)}) collective-permute-start(f32[128,512]{1,0:T(8,128)} %constant_dynamic-slice_fusion), channel_id=1, source_target_pairs={{0,2},{1,3},{2,0},{3,1},{4,6},{5,7},{6,4},{7,5},{8,10},{9,11},{10,... | collective-permute-start | bytes 786440 | tf_op jit(solution)/shard_map/ppermute | solution.py:287
Sparse Core Ops, SparseCore 0:
  43.1 35.9 reduce-scatter.1
where the time goes:
time: 368 us; the launch traced here: 367 us
  waiting for transfers between devices  186 us (51%)
  blocking collectives  87.8 us (24%)
  matrix products  31.5 us (9%)
  local copies, waits for them, and re-layouts  18.2 us (5%)
  starting transfers between devices  15.1 us (4%)
  between operations  14.5 us (4%)
  other arithmetic  13.7 us (4%)
    all_to_all x1, blocking collectives, on_device(): lax.all_to_all(outgoing[:, slots], 'req', split_axis=0, concat_axis=0, ti...  66.9 us
    all_to_all x1, waiting for transfers between devices, on_device(): lax.all_to_all(pair_value, 'req', split_axis=0, concat_axis=0, tiled=True)  45.6 us
    ppermute x1, waiting for transfers between devices, on_device(): partner_rows = lax.ppermute(own_rows, 'tp', beside)  45.5 us
    ppermute x1, waiting for transfers between devices, on_device(): arrived_value = lax.ppermute(partner_value, 'tp', beside)  43.7 us
    reduce_scatter x1, waiting for transfers between devices, on_device(): lax.psum_scatter(attention_parts, 'tp', scatter_dimension=0, tiled=True)  34.5 us
    all_gather x1, blocking collectives, on_device(): compressed = lax.all_gather(compressed_part, 'tp', axis=1, tiled=True)  13.4 us
    ppermute x1, waiting for transfers between devices, on_device(): routed = keep + lax.ppermute(give, 'tp', across)  11.4 us
    dot_general x1, matrix products, on_device(): jnp.einsum('sch,hf->scf', expert_hidden, w_down[0], preferred_element_typ...  10.3 us
  transfers between devices with their start and end apart: 6, of which 6 were waited for; matrix products, arithmetic and copies ran while one was open for 2% of the time, Pallas kernels for 0%

commit v1 on v0

--- a/solution.py
+++ b/solution.py
@@ -186,6 +186,22 @@
         jnp.bfloat16
     )
     compressed = lax.all_gather(compressed_part, "tp", axis=1, tiled=True)
+    tp_size = lax.axis_size("tp")
+    tp_index = lax.axis_index("tp")
+    quarter = D // tp_size
+    parity = tp_index % 2
+    beside = [(t, t ^ 1) for t in range(tp_size)]
+
+    def features(block, first):
+        return lax.dynamic_slice_in_dim(block, first * quarter, quarter, block.ndim - 1)
+
+    down_local = w_down[0]
+    down_own = jnp.concatenate([features(down_local, parity), features(down_local, parity + 2)], -1)
+    down_given = jnp.concatenate(
+        [features(down_local, 1 - parity), features(down_local, 3 - parity)], -1
+    )
+    down_partner = lax.ppermute(down_given, "tp", beside)
+    down_partner, compressed = lax.optimization_barrier((down_partner, compressed))
     ancestry = jax.vmap(ancestors)(parents)
     depths = jnp.sum(ancestry, -1) - 1.0
     positions = (lengths.astype(jnp.float32)[:, None] + depths).reshape(-1)
@@ -213,9 +229,6 @@
     top_count = routes.shape[1]
     capacity = 4 * tok_rows * top_count // (3 * experts_all)
     pick_table, weights = route_tables(routes, gates, experts_all, capacity)
-    tp_size = lax.axis_size("tp")
-    tp_index = lax.axis_index("tp")
-    quarter = D // tp_size
     attention_parts = jnp.einsum(
         "tk,kqf->qtf",
         head_out.reshape(tok_rows, local_heads * VDIM),
@@ -231,10 +244,8 @@
     normed_quarter = (
         residual_quarter * lax.rsqrt(square_sum / D + epsilon) * gain_quarter
     ).astype(jnp.bfloat16)
-    parity = tp_index % 2
     upper = tp_index // 2
     across = [(t, t ^ 2) for t in range(tp_size)]
-    beside = [(t, t ^ 1) for t in range(tp_size)]
     other_quarter = lax.ppermute(normed_quarter, "tp", across)
     half_rows = jnp.where(
         upper == 0,
@@ -245,9 +256,6 @@
         pick_table, half_rows, (((0,), (0,)), ((), ())), preferred_element_type=jnp.float32
     ).astype(jnp.bfloat16)
     outgoing = outgoing.reshape(experts_all, capacity, 2 * quarter)
-
-    def features(block, first):
-        return lax.dynamic_slice_in_dim(block, first * quarter, quarter, block.ndim - 1)
 
     chunks = 1
     slot_step = capacity // chunks
@@ -267,15 +275,13 @@
         gate_act = jnp.einsum("scf,fh->sch", row_set, w_gate[0], preferred_element_type=jnp.float32)
         up_act = jnp.einsum("scf,fh->sch", row_set, w_up[0], preferred_element_type=jnp.float32)
         expert_hidden = (jax.nn.silu(gate_act) * up_act).astype(jnp.bfloat16)
-        value = jnp.einsum(
-            "sch,hf->scf", expert_hidden, w_down[0], preferred_element_type=jnp.float32
-        )
-        partner_value = jnp.concatenate(
-            [features(value, 1 - parity), features(value, 3 - parity)], -1
+        partner_hidden = lax.ppermute(expert_hidden, "tp", beside)
+        pair_value = (
+            jnp.einsum("sch,hf->scf", expert_hidden, down_own, preferred_element_type=jnp.float32)
+            + jnp.einsum(
+                "sch,hf->scf", partner_hidden, down_partner, preferred_element_type=jnp.float32
+            )
         ).astype(jnp.bfloat16)
-        arrived_value = lax.ppermute(partner_value, "tp", beside)
-        own_value = jnp.concatenate([features(value, parity), features(value, parity + 2)], -1)
-        pair_value = (own_value + arrived_value.astype(jnp.float32)).astype(jnp.bfloat16)
         shares = lax.all_to_all(pair_value, "req", split_axis=0, concat_axis=0, tiled=True)
         routed_half = routed_half + jnp.dot(
             weights_by_slot[:, :, slots].reshape(tok_rows, experts_all * slot_step),

time: 368 us -> 334 us (0.908)
  waiting for transfers between devices: 186 us -> 158 us
  matrix products: 31.5 us -> 27 us
  other arithmetic: 13.7 us -> 9.5 us
    ppermute x1 -> x2, waiting for transfers between devices: 43.7 us -> 16.7 us  [the longest x1 16.6 us: on_device(): partner_hidden = lax.ppermute(expert_hidden, 'tp', beside)]
    convert_element_type x1 -> x0, other arithmetic: 3.86 us -> none  [on_device(): (own_value + arrived_value.astype(jnp.float32)).astype(jnp.bfloat16)]
    dot_general x1 -> x3, matrix products: 10.3 us -> 7.52 us  [the longest x1 3.7 us: on_device(): jnp.einsum('sch,hf->scf', partner_hidden, down_partner, preferred_element...]
  transfers between devices with their start and end apart: 6 -> 7, of which waited for: 6 -> 6; matrix products, arithmetic and copies ran while one was open for 2% -> 6% of each run, Pallas kernels for 0% -> 0%
where the time goes in v1:
time: 334 us; the launch traced here: 333 us
  waiting for transfers between devices  158 us (47%)
  blocking collectives  89 us (27%)
  matrix products  27 us (8%)
  starting transfers between devices  17.8 us (5%)
  local copies, waits for them, and re-layouts  16.7 us (5%)
  between operations  14.6 us (4%)
  other arithmetic  9.5 us (3%)
    all_to_all x1, blocking collectives, on_device(): lax.all_to_all(outgoing[:, slots], 'req', split_axis=0, concat_axis=0, ti...  66.9 us
    ppermute x1, waiting for transfers between devices, on_device(): partner_rows = lax.ppermute(own_rows, 'tp', beside)  45.5 us
    all_to_all x1, waiting for transfers between devices, on_device(): lax.all_to_all(pair_value, 'req', split_axis=0, concat_axis=0, tiled=True)  44.6 us
    reduce_scatter x1, waiting for transfers between devices, on_device(): lax.psum_scatter(attention_parts, 'tp', scatter_dimension=0, tiled=True)  34.5 us
    ppermute x1, waiting for transfers between devices, on_device(): partner_hidden = lax.ppermute(expert_hidden, 'tp', beside)  16.6 us
    all_gather x1, blocking collectives, on_device(): compressed = lax.all_gather(compressed_part, 'tp', axis=1, tiled=True)  14.7 us
    ppermute x1, waiting for transfers between devices, on_device(): routed = keep + lax.ppermute(give, 'tp', across)  11.4 us
    all_to_all x1, starting transfers between devices, on_device(): lax.all_to_all(pair_value, 'req', split_axis=0, concat_axis=0, tiled=True)  8.3 us
  transfers between devices with their start and end apart: 7, of which 6 were waited for; matrix products, arithmetic and copies ran while one was open for 6% of the time, Pallas kernels for 0%

profile of v1, /device:TPU:1, one launch (start us, length us, event | category | flops | bytes accessed | tf_op | source)
XLA Modules:
  0.0 332.9 jit_solution(11059970846262623483)
XLA Ops:
  7.3 2.5 dynamic-slice_bitcast_fusion.1
  9.7 1.0 pad_maximum_fusion
  10.7 2.5 collective-permute-start
  13.2 0.2 convolution_minimum_fusion.6
  13.4 0.2 convolution_minimum_fusion.5
  13.6 0.2 convolution_minimum_fusion.4
  13.8 0.2 convolution_minimum_fusion.3
  14.0 0.2 convolution_minimum_fusion.2
  14.2 0.2 convolution_minimum_fusion.1
  14.4 0.3 fusion.77
  15.0 0.7 copy.74
  15.7 0.3 fusion.16
  16.0 0.4 copy.68
  16.4 0.1 concatenate.32
  16.5 1.0 copy.69
  17.6 1.0 concatenate.33
  18.6 0.7 copy.70
  19.3 2.1 copy.84
  21.4 1.4 convolution_convert_fusion.4
  22.8 14.7 %all_gather.3 = bf16[128,576]{0,1:T(8,128)(2,1)S(1)} all-gather(bf16[128,144]{0,1:T(8,128)(2,1)S(1)} %convolution_convert_fusion.4), channel_id=1, replica_groups=mesh['req'=64,'tp'=4] {'tp'}, dimensions={1}, use_global_device_ids=true | all-gather | bytes 184320 | tf_op jit(solution)/shard_map/all_gather | solution.py:188
  37.6 2.4 fusion.6
  40.2 0.1 fusion.36
  40.3 0.1 fusion.64
  40.5 0.2 copy.73
  40.6 1.4 fusion.78
  42.1 2.1 fusion.7
  44.2 1.1 fusion.20
  45.4 0.4 fusion.49
  45.8 0.2 fusion.23
  46.0 0.9 reshape.165
  46.9 1.5 convolution_convert_fusion.3
  48.5 3.1 fusion.13
  51.6 0.1 copy.79
  51.7 0.1 eq.86
  51.9 0.4 fusion.19
  52.3 0.1 convert_element_type.99
  52.5 0.8 dynamic_slice.37
  53.3 34.5 %reduce-scatter.2.cloned.1.call-done = f32[1,128,512]{2,1,0:T(8,128)} async-done(((f32[4,128,512]{2,1,0:T(8,128)}), f32[1,128,512]{2,1,0:T(8,128)}) %reduce-scatter.2.cloned.1.call-update) | async-done | bytes 262160 | tf_op jit(solution)/shard_map/reduce_scatter | solution.py:238
  87.7 1.1 multiply_reduce_fusion
  88.8 7.4 %psum.7 = f32[128,1]{0,1:T(1,128)S(1)} all-reduce(f32[128,1]{0,1:T(1,128)S(1)} %bitcast.103), channel_id=1, replica_groups=mesh['req'=64,'tp'=4] {'tp'}, use_global_device_ids=true, to_apply=%region_11.12 | all-reduce | flops 128 | bytes 1024 | tf_op jit(solution)/shard_map/psum | solution.py:242
  96.2 1.0 multiply_convert_fusion.1
  97.4 0.5 fusion
  97.8 5.6 %collective-permute-done.1 = bf16[128,512]{1,0:T(8,128)(2,1)S(1)} collective-permute-done((bf16[128,512]{1,0:T(8,128)(2,1)S(1)}, bf16[128,512]{1,0:T(8,128)(2,1)S(1)}, u32[]{:S(2)}, u32[]{:S(2)}) %collective-permute-start.1) | collective-permute-done | bytes 131104 | tf_op jit(solution)/shard_map/ppermute | solution.py:249
  103.5 0.7 convolution_convert_fusion
  104.2 66.9 %all_to_all.10 = bf16[64,16,1024]{2,1,0:T(8,128)(2,1)} all-to-all(bf16[64,16,1024]{2,1,0:T(8,128)(2,1)S(1)} %bitcast.94), channel_id=1, replica_groups=mesh['req'=64,'tp'=4] {'req'}, dimensions={0} | all-to-all | bytes 4194304 | tf_op jit(solution)/shard_map/all_to_all | solution.py:266
  171.1 1.7 fusion.75
  172.9 45.5 %collective-permute-done.2 = bf16[64,16,1024]{2,1,0:T(8,128)(2,1)} collective-permute-done((bf16[64,16,1024]{2,1,0:T(8,128)(2,1)}, bf16[64,16,1024]{2,1,0:T(8,128)(2,1)}, u32[]{:S(2)}, u32[]{:S(2)}) %collective-permute-start.2) | collective-permute-done | bytes 2097184 | tf_op jit(solution)/shard_map/ppermute | solution.py:267
  218.4 1.7 fusion.76
  220.1 2.3 fusion.11
  222.5 2.6 multiply_convert_fusion
  225.1 0.1 collective-permute-start.3
  225.2 1.2 fusion.28
  226.5 16.6 %collective-permute-done.3 = bf16[64,16,352]{2,1,0:T(8,128)(2,1)S(1)} collective-permute-done((bf16[64,16,352]{2,1,0:T(8,128)(2,1)S(1)}, bf16[64,16,352]{2,1,0:T(8,128)(2,1)S(1)}, u32[]{:S(2)}, u32[]{:S(2)}) %collective-permute-start.3) | collective-permute-done | bytes 720928 | tf_op jit(solution)/shard_map/ppermute | solution.py:278
  243.1 3.7 %add_convert_fusion = bf16[64,16,1024]{2,1,0:T(8,128)(2,1)} fusion(f32[64,16,1024]{2,1,0:T(8,128)S(1)} %fusion.28, bf16[64,16,352]{2,1,0:T(8,128)(2,1)S(1)} %collective-permute-done.3, bf16[352,1024]{1,0:T(8,128)(2,1)} %collective-permute-done), kind=kOutput, calls=%fused_computation.2 | convolution fusion | flops 740294656 | bytes 7733248 | tf_op jit(solution)/shard_map/sch,hf->scf/dot_general | solution.py:281
  246.8 8.3 %all-to-all-start.1 = ((bf16[64,16,1024]{2,1,0:T(8,128)(2,1)}), bf16[64,16,1024]{2,1,0:T(8,128)(2,1)}, u32[]{:S(2)}, u32[]{:S(2)}) async-start(bf16[64,16,1024]{2,1,0:T(8,128)(2,1)} %add_convert_fusion), calls=%async_computation.2 | async-start | bytes 4194304 | tf_op jit(solution)/shard_map/all_to_all | solution.py:285
  255.2 1.5 gather_fusion
  256.6 1.1 fusion.9
  257.8 44.6 %all-to-all-done.1 = bf16[64,16,1024]{2,1,0:T(8,128)(2,1)} async-done(((bf16[64,16,1024]{2,1,0:T(8,128)(2,1)}), bf16[64,16,1024]{2,1,0:T(8,128)(2,1)}, u32[]{:S(2)}, u32[]{:S(2)}) %all-to-all-start.1) | async-done | bytes 2097184 | tf_op jit(solution)/shard_map/all_to_all | solution.py:285
  302.3 2.1 fusion.79
  304.5 0.7 constant_dynamic-slice_fusion
  305.2 6.8 %collective-permute-start.4 = (f32[128,512]{1,0:T(8,128)}, f32[128,512]{1,0:T(8,128)}, u32[]{:S(2)}, u32[]{:S(2)}) collective-permute-start(f32[128,512]{1,0:T(8,128)} %constant_dynamic-slice_fusion), channel_id=1, source_target_pairs={{0,2},{1,3},{2,0},{3,1},{4,6},{5,7},{6,4},{7,5},{8,10},{9,11},{10,... | collective-permute-start | bytes 786440 | tf_op jit(solution)/shard_map/ppermute | solution.py:293
  312.1 0.8 convolution_convert_fusion.2
  312.9 11.4 %collective-permute-done.4 = f32[128,512]{1,0:T(8,128)} collective-permute-done((f32[128,512]{1,0:T(8,128)}, f32[128,512]{1,0:T(8,128)}, u32[]{:S(2)}, u32[]{:S(2)}) %collective-permute-start.4) | collective-permute-done | bytes 262176 | tf_op jit(solution)/shard_map/ppermute | solution.py:293
  324.4 1.7 add_convert_fusion.1
  (69 shorter events, 0.9 us)
Async XLA Ops:
  7.2 30.4 %copy-start = (bf16[2,1024,576]{1,2,0:T(8,128)(2,1)S(1)}, bf16[2,1024,576]{1,2,0:T(8,128)(2,1)}, u32[]{:S(2)}) copy-start(bf16[2,1024,576]{1,2,0:T(8,128)(2,1)} %param.21) | copy-start | bytes 7077892
  7.2 80.5 %reduce-scatter.2.cloned.1.call-start = ((), (), s32[]{:S(2)}) async-start(), calls=%async_computation.3 | async-start | bytes 1310720 | tf_op jit(solution)/shard_map/reduce_scatter | solution.py:238
  7.3 5.9 %copy-start.19 = (s32[2,64]{1,0:T(2,128)S(1)}, s32[2,64]{1,0:T(2,128)}, u32[]{:S(2)}) copy-start(s32[2,64]{1,0:T(2,128)} %param.23) | copy-start | bytes 1540
  7.3 7.4 %copy-start.16 = (s32[2]{0:T(128)S(1)}, s32[2]{0:T(128)}, u32[]{:S(2)}) copy-start(s32[2]{0:T(128)} %param.22) | copy-start | bytes 28
  9.7 6.0 %copy-start.7 = (bf16[512,512]{1,0:T(8,128)(2,1)S(1)}, bf16[512,512]{1,0:T(8,128)(2,1)}, u32[]{:S(2)}) copy-start(bf16[512,512]{1,0:T(8,128)(2,1)} %param.27) | copy-start | bytes 1572868
  9.7 6.0 %copy-start.10 = (bf16[128,512]{1,0:T(8,128)(2,1)S(1)}, bf16[128,512]{1,0:T(8,128)(2,1)}, u32[]{:S(2)}) copy-start(bf16[128,512]{1,0:T(8,128)(2,1)} %param.19) | copy-start | bytes 393220
  10.7 29.3 %collective-permute-start = (bf16[352,1024]{1,0:T(8,128)(2,1)}, bf16[352,1024]{1,0:T(8,128)(2,1)}, u32[]{:S(2)}, u32[]{:S(2)}) collective-permute-start(bf16[352,1024]{1,0:T(8,128)(2,1)} %pad_maximum_fusion), channel_id=1, source_target_pairs={{0,1},{1,0},{2,3},{3,2},{4,5},{5,4},{6,7},{7,6},{8,9},{9,8},{10,11... | collective-permute-start | bytes 2162696 | tf_op jit(solution)/shard_map/ppermute | solution.py:203
  14.7 1.3 copy-start.9
  16.5 4.9 %copy-start.3 = (bf16[128,2048]{1,0:T(8,128)(2,1)S(1)}, bf16[128,2048]{1,0:T(8,128)(2,1)}, u32[]{:S(2)}) copy-start(bf16[128,2048]{1,0:T(8,128)(2,1)} %param.18) | copy-start | bytes 1572868
  17.6 20.0 %copy-start.8 = (bf16[2,256,512]{1,2,0:T(8,128)(2,1)S(1)}, bf16[2,256,512]{1,2,0:T(8,128)(2,1)}, u32[]{:S(2)}) copy-start(bf16[2,256,512]{1,2,0:T(8,128)(2,1)} %copy.69) | copy-start | bytes 1572868
  19.3 18.3 %copy-start.11 = (bf16[2,256,64]{1,2,0:T(8,128)(2,1)S(1)}, bf16[2,256,64]{1,2,0:T(8,128)(2,1)}, u32[]{:S(2)}) copy-start(bf16[2,256,64]{1,2,0:T(8,128)(2,1)} %copy.70) | copy-start | bytes 196612
  37.6 2.5 copy-start.14
  37.6 3.0 copy-start.12
  40.6 3.6 %copy-start.2 = (f32[2,256,1024]{2,1,0:T(8,128)S(1)}, f32[2,256,1024]{2,1,0:T(8,128)}, u32[]{:S(2)}) copy-start(f32[2,256,1024]{2,1,0:T(8,128)} %get-tuple-element.21) | copy-start | bytes 6291460
  48.5 3.2 copy-start.13
  48.5 39.3 %copy-start.4 = (bf16[128,2048]{1,0:T(8,128)(2,1)S(1)}, bf16[128,2048]{1,0:T(8,128)(2,1)}, u32[]{:S(2)}) copy-start(bf16[128,2048]{1,0:T(8,128)(2,1)} %param.18) | copy-start | bytes 1572868
  97.3 6.2 %collective-permute-start.1 = (bf16[128,512]{1,0:T(8,128)(2,1)S(1)}, bf16[128,512]{1,0:T(8,128)(2,1)S(1)}, u32[]{:S(2)}, u32[]{:S(2)}) collective-permute-start(bf16[128,512]{1,0:T(8,128)(2,1)S(1)} %multiply_convert_fusion.1), channel_id=1, source_target_pairs={{0,2},{1,3},{2,0},{3,1},{4,6},{5,7},{6,4},{7,5},{8,10},{9,11},{10,... | collective-permute-start | bytes 393224 | tf_op jit(solution)/shard_map/ppermute | solution.py:249
  171.1 47.2 %collective-permute-start.2 = (bf16[64,16,1024]{2,1,0:T(8,128)(2,1)}, bf16[64,16,1024]{2,1,0:T(8,128)(2,1)}, u32[]{:S(2)}, u32[]{:S(2)}) collective-permute-start(bf16[64,16,1024]{2,1,0:T(8,128)(2,1)} %all_to_all.10), channel_id=1, source_target_pairs={{0,1},{1,0},{2,3},{3,2},{4,5},{5,4},{6,7},{7,6},{8,9},{9,8},{10,11... | collective-permute-start | bytes 6291464 | tf_op jit(solution)/shard_map/ppermute | solution.py:267
  172.9 47.2 %copy-start.17 = (bf16[1,2048,352]{1,2,0:T(8,128)(2,1)S(1)}, bf16[1,2048,352]{1,2,0:T(8,128)(2,1)}, u32[]{:S(2)}) copy-start(bf16[1,2048,352]{1,2,0:T(8,128)(2,1)} %param.33) | copy-start | bytes 4325380
  220.1 2.4 copy-start.18
  222.4 2.8 copy-start.5
  222.5 2.8 copy-start.6
  225.1 18.0 %collective-permute-start.3 = (bf16[64,16,352]{2,1,0:T(8,128)(2,1)S(1)}, bf16[64,16,352]{2,1,0:T(8,128)(2,1)S(1)}, u32[]{:S(2)}, u32[]{:S(2)}) collective-permute-start(bf16[64,16,352]{2,1,0:T(8,128)(2,1)S(1)} %multiply_convert_fusion), channel_id=1, source_target_pairs={{0,1},{1,0},{2,3},{3,2},{4,5},{5,4},{6,7},{7,6},{8,9},{9,8},{10,11... | collective-permute-start | bytes 2162696 | tf_op jit(solution)/shard_map/ppermute | solution.py:278
  246.8 8.3 %copy-start.20 = (s32[2]{0:T(128)S(1)}, s32[2]{0:T(128)}, u32[]{:S(2)}) copy-start(s32[2]{0:T(128)} %param.24) | copy-start | bytes 28
  246.8 9.8 %copy-start.15 = (bf16[128,6]{0,1:T(8,128)(2,1)S(1)}, bf16[128,6]{0,1:T(8,128)(2,1)}, u32[]{:S(2)}) copy-start(bf16[128,6]{0,1:T(8,128)(2,1)} %param.32) | copy-start | bytes 4612
  246.8 55.5 %all-to-all-start.1 = ((bf16[64,16,1024]{2,1,0:T(8,128)(2,1)}), bf16[64,16,1024]{2,1,0:T(8,128)(2,1)}, u32[]{:S(2)}, u32[]{:S(2)}) async-start(bf16[64,16,1024]{2,1,0:T(8,128)(2,1)} %add_convert_fusion), calls=%async_computation.2 | async-start | bytes 4194304 | tf_op jit(solution)/shard_map/all_to_all | solution.py:285
  255.1 69.2 %copy-start.1 = (f32[1,128,512]{2,1,0:T(8,128)S(1)}, f32[1,128,512]{2,1,0:T(8,128)}, u32[]{:S(2)}) copy-start(f32[1,128,512]{2,1,0:T(8,128)} %reduce-scatter.2.cloned.1.call-done) | copy-start | bytes 786436
  305.2 19.2 %collective-permute-start.4 = (f32[128,512]{1,0:T(8,128)}, f32[128,512]{1,0:T(8,128)}, u32[]{:S(2)}, u32[]{:S(2)}) collective-permute-start(f32[128,512]{1,0:T(8,128)} %constant_dynamic-slice_fusion), channel_id=1, source_target_pairs={{0,2},{1,3},{2,0},{3,1},{4,6},{5,7},{6,4},{7,5},{8,10},{9,11},{10,... | collective-permute-start | bytes 786440 | tf_op jit(solution)/shard_map/ppermute | solution.py:293
Sparse Core Ops, SparseCore 0:
  51.7 35.9 reduce-scatter.1

commit v2 on v1

--- a/solution.py
+++ b/solution.py
@@ -229,28 +229,28 @@
     top_count = routes.shape[1]
     capacity = 4 * tok_rows * top_count // (3 * experts_all)
     pick_table, weights = route_tables(routes, gates, experts_all, capacity)
-    attention_parts = jnp.einsum(
-        "tk,kqf->qtf",
-        head_out.reshape(tok_rows, local_heads * VDIM),
-        o_proj.reshape(o_proj.shape[0], tp_size, quarter),
-        preferred_element_type=jnp.float32,
-    )
-    attention_quarter = lax.psum_scatter(attention_parts, "tp", scatter_dimension=0, tiled=True)
-    attention_quarter = attention_quarter.reshape(tok_rows, quarter)
-    hidden_quarter = lax.dynamic_slice_in_dim(layer_in, tp_index * quarter, quarter, 1)
-    residual_quarter = hidden_quarter.astype(jnp.float32) + attention_quarter
-    square_sum = lax.psum(jnp.sum(residual_quarter * residual_quarter, -1, keepdims=True), "tp")
-    gain_quarter = lax.dynamic_slice_in_dim(post_gain, tp_index * quarter, quarter, 0)
-    normed_quarter = (
-        residual_quarter * lax.rsqrt(square_sum / D + epsilon) * gain_quarter
-    ).astype(jnp.bfloat16)
     upper = tp_index // 2
     across = [(t, t ^ 2) for t in range(tp_size)]
-    other_quarter = lax.ppermute(normed_quarter, "tp", across)
-    half_rows = jnp.where(
-        upper == 0,
-        jnp.concatenate([normed_quarter, other_quarter], 1),
-        jnp.concatenate([other_quarter, normed_quarter], 1),
+
+    def half_of(block, which):
+        return jnp.concatenate([features(block, which), features(block, which + 2)], -1)
+
+    attention = jnp.dot(
+        head_out.reshape(tok_rows, local_heads * VDIM), o_proj, preferred_element_type=jnp.float32
+    )
+    pair_sum = half_of(attention, parity) + lax.ppermute(
+        half_of(attention, 1 - parity).astype(jnp.bfloat16), "tp", beside
+    ).astype(jnp.float32)
+    attention_half = pair_sum + lax.ppermute(
+        pair_sum.astype(jnp.bfloat16), "tp", across
+    ).astype(jnp.float32)
+    residual_half = half_of(layer_in, parity).astype(jnp.float32) + attention_half
+    half_squares = jnp.sum(residual_half * residual_half, -1, keepdims=True)
+    square_sum = half_squares + lax.ppermute(half_squares, "tp", beside)
+    residual_quarter = features(residual_half, upper)
+    gain_half = half_of(post_gain, parity)
+    half_rows = (residual_half * lax.rsqrt(square_sum / D + epsilon) * gain_half).astype(
+        jnp.bfloat16
     )
     outgoing = lax.dot_general(
         pick_table, half_rows, (((0,), (0,)), ((), ())), preferred_element_type=jnp.float32
@@ -290,7 +290,7 @@
         )
     keep = features(routed_half, upper)
     give = features(routed_half, 1 - upper)
-    routed = keep + lax.ppermute(give, "tp", across)
+    routed = keep + lax.ppermute(give.astype(jnp.bfloat16), "tp", across).astype(jnp.float32)
     layer_out = (residual_quarter + routed).astype(jnp.bfloat16)
     return (layer_out, accepted_rows)
 

time: 334 us -> 285 us (0.85)
  waiting for transfers between devices: 158 us -> 113 us
  starting transfers between devices: 17.8 us -> 40.3 us
  between operations: 14.6 us -> 1.27 us
  blocking collectives: 89 us -> 79.4 us
    reduce_scatter x1 -> x0, waiting for transfers between devices: 34.5 us -> none  [on_device(): lax.psum_scatter(attention_parts, 'tp', scatter_dimension=0, tiled=True)]
    ppermute x2 -> x4, starting transfers between devices: 6.9 us -> 24.1 us  [the longest x1 23.2 us: on_device(): lax.ppermute(give.astype(jnp.bfloat16), 'tp', across).astype(jnp.float32)]
    all_to_all x1, waiting for transfers between devices: 44.6 us -> 31.3 us  [on_device(): lax.all_to_all(pair_value, 'req', split_axis=0, concat_axis=0, tiled=True)]
    psum x1 -> x0, blocking collectives: 7.4 us -> none  [on_device(): lax.psum(jnp.sum(residual_quarter * residual_quarter, -1, keepdims=True),...]
    ppermute x1, starting transfers between devices: 0.01 us -> 5.65 us  [on_device(): partner_rows = lax.ppermute(own_rows, 'tp', beside)]
    ppermute x2 -> x4, waiting for transfers between devices: 17 us -> 21 us  [the longest x1 7.65 us: on_device(): lax.ppermute(pair_sum.astype(jnp.bfloat16), 'tp', across)]
  transfers between devices with their start and end apart: 7 -> 8, of which waited for: 6 -> 7; matrix products, arithmetic and copies ran while one was open for 6% -> 8% of each run, Pallas kernels for 0% -> 0%
where the time goes in v2:
time: 285 us; the launch traced here: 284 us
  waiting for transfers between devices  113 us (40%)
  blocking collectives  79.4 us (28%)
  starting transfers between devices  40.3 us (14%)
  matrix products  24.9 us (9%)
  local copies, waits for them, and re-layouts  19 us (7%)
  other arithmetic  6.72 us (2%)
    all_to_all x1, blocking collectives, on_device(): lax.all_to_all(outgoing[:, slots], 'req', split_axis=0, concat_axis=0, ti...  67.8 us
    ppermute x1, waiting for transfers between devices, on_device(): partner_rows = lax.ppermute(own_rows, 'tp', beside)  44.4 us
    all_to_all x1, waiting for transfers between devices, on_device(): lax.all_to_all(pair_value, 'req', split_axis=0, concat_axis=0, tiled=True)  31.3 us
    ppermute x1, starting transfers between devices, on_device(): lax.ppermute(give.astype(jnp.bfloat16), 'tp', across).astype(jnp.float32)  23.2 us
    ppermute x1, waiting for transfers between devices, on_device(): partner_hidden = lax.ppermute(expert_hidden, 'tp', beside)  15.9 us
    all_gather x1, blocking collectives, on_device(): compressed = lax.all_gather(compressed_part, 'tp', axis=1, tiled=True)  11.5 us
    ppermute x1, waiting for transfers between devices, on_device(): lax.ppermute(pair_sum.astype(jnp.bfloat16), 'tp', across)  7.65 us
    all_to_all x1, starting transfers between devices, on_device(): lax.all_to_all(pair_value, 'req', split_axis=0, concat_axis=0, tiled=True)  6.8 us
  transfers between devices with their start and end apart: 8, of which 7 were waited for; matrix products, arithmetic and copies ran while one was open for 8% of the time, Pallas kernels for 0%

profile of v2, /device:TPU:1, one launch (start us, length us, event | category | flops | bytes accessed | tf_op | source)
XLA Modules:
  0.0 284.1 jit_solution(15346067437031733673)
XLA Ops:
  0.7 2.4 dynamic-slice_bitcast_fusion.1
  3.1 0.9 pad_maximum_fusion
  4.1 2.5 collective-permute-start
  6.6 0.2 convolution_minimum_fusion.6
  6.8 0.2 convolution_minimum_fusion.5
  7.0 0.2 convolution_minimum_fusion.4
  7.2 0.2 convolution_minimum_fusion.3
  7.4 0.2 convolution_minimum_fusion.2
  7.6 0.2 convolution_minimum_fusion.1
  7.8 0.3 fusion.68
  8.3 0.7 copy.68
  9.1 0.3 fusion.10
  9.4 0.4 copy.62
  9.9 1.0 copy.63
  10.9 1.7 concatenate.41
  12.6 1.6 copy.64
  14.2 2.0 copy.75
  16.3 0.7 copy.71
  17.0 1.0 eq.83
  18.0 0.4 fusion.13
  18.4 0.8 convert_element_type.118
  19.2 0.9 copy.72
  20.1 0.3 convolution_convert_fusion.4
  20.4 11.5 %all_gather.3 = bf16[128,576]{0,1:T(8,128)(2,1)S(1)} all-gather(bf16[128,144]{0,1:T(8,128)(2,1)S(1)} %convolution_convert_fusion.4), channel_id=1, replica_groups=mesh['req'=64,'tp'=4] {'tp'}, dimensions={1}, use_global_device_ids=true | all-gather | bytes 184320 | tf_op jit(solution)/shard_map/all_gather | solution.py:188
  31.9 0.7 iota_compare_fusion.12
  32.7 3.5 %fusion.3 = (f32[2,256]{1,0:T(2,128)S(1)}, f32[2,256,1024]{2,1,0:T(8,128)}) fusion(pred[2,1024]{1,0:T(4,128)(4,1)S(1)} %iota_compare_fusion.12, bf16[2,1024,576]{1,2,0:T(8,128)(2,1)S(1)} %copy-done, bf16[2,256,64]{1,2,0:T(8,128)(2,1)} %copy.64, bf16[2,256,512]{1,2,0:T(8,128)(2,1)} %copy.63), kind=kOutput, calls=%fused_computation.11 | convolution fusion | flops 606731776 | bytes 5050368 | tf_op jit(solution)/shard_map/rqk,rck->rqc/dot_general | solution.py:107
  36.4 0.1 fusion.31
  36.5 0.1 fusion.55
  36.7 0.2 copy.67
  36.9 0.3 fusion.69
  37.2 2.3 fusion.4
  39.4 1.1 fusion.14
  40.6 0.4 fusion.40
  41.0 0.2 fusion.17
  41.2 0.9 reshape.159
  42.1 1.5 convolution_convert_fusion.3
  43.6 2.1 fusion.70
  46.1 5.1 %collective-permute-done.1 = bf16[128,1024]{1,0:T(8,128)(2,1)S(1)} collective-permute-done((bf16[128,1024]{1,0:T(8,128)(2,1)S(1)}, bf16[128,1024]{1,0:T(8,128)(2,1)S(1)}, u32[]{:S(2)}, u32[]{:S(2)}) %collective-permute-start.1) | collective-permute-done | bytes 262176 | tf_op jit(solution)/shard_map/ppermute | solution.py:241
  51.2 0.7 collective-permute-start.2
  52.0 0.5 fusion
  52.4 7.6 %collective-permute-done.2 = bf16[128,1024]{1,0:T(8,128)(2,1)S(1)} collective-permute-done((bf16[128,1024]{1,0:T(8,128)(2,1)S(1)}, bf16[128,1024]{1,0:T(8,128)(2,1)S(1)}, u32[]{:S(2)}, u32[]{:S(2)}) %collective-permute-start.2) | collective-permute-done | bytes 262176 | tf_op jit(solution)/shard_map/ppermute | solution.py:244
  60.1 0.2 multiply_reduce_fusion
  60.4 2.7 collective-permute-done.3
  63.1 0.8 convolution_convert_fusion
  63.9 67.8 %all_to_all.10 = bf16[64,16,1024]{2,1,0:T(8,128)(2,1)} all-to-all(bf16[64,16,1024]{2,1,0:T(8,128)(2,1)S(1)} %bitcast.78), channel_id=1, replica_groups=mesh['req'=64,'tp'=4] {'req'}, dimensions={0} | all-to-all | bytes 4194304 | tf_op jit(solution)/shard_map/all_to_all | solution.py:266
  131.7 5.6 %collective-permute-start.4 = (bf16[64,16,1024]{2,1,0:T(8,128)(2,1)}, bf16[64,16,1024]{2,1,0:T(8,128)(2,1)}, u32[]{:S(2)}, u32[]{:S(2)}) collective-permute-start(bf16[64,16,1024]{2,1,0:T(8,128)(2,1)} %all_to_all.10), channel_id=1, source_target_pairs={{0,1},{1,0},{2,3},{3,2},{4,5},{5,4},{6,7},{7,6},{8,9},{9,8},{10,11... | collective-permute-start | bytes 6291464 | tf_op jit(solution)/shard_map/ppermute | solution.py:267
  137.4 1.7 fusion.65
  139.1 44.4 %collective-permute-done.4 = bf16[64,16,1024]{2,1,0:T(8,128)(2,1)} collective-permute-done((bf16[64,16,1024]{2,1,0:T(8,128)(2,1)}, bf16[64,16,1024]{2,1,0:T(8,128)(2,1)}, u32[]{:S(2)}, u32[]{:S(2)}) %collective-permute-start.4) | collective-permute-done | bytes 2097184 | tf_op jit(solution)/shard_map/ppermute | solution.py:267
  183.5 1.7 fusion.66
  185.3 2.3 fusion.8
  187.6 2.6 multiply_convert_fusion
  190.2 1.3 collective-permute-start.5
  191.5 1.2 fusion.22
  192.8 15.9 %collective-permute-done.5 = bf16[64,16,352]{2,1,0:T(8,128)(2,1)S(1)} collective-permute-done((bf16[64,16,352]{2,1,0:T(8,128)(2,1)S(1)}, bf16[64,16,352]{2,1,0:T(8,128)(2,1)S(1)}, u32[]{:S(2)}, u32[]{:S(2)}) %collective-permute-start.5) | collective-permute-done | bytes 720928 | tf_op jit(solution)/shard_map/ppermute | solution.py:278
  208.7 3.7 %add_convert_fusion = bf16[64,16,1024]{2,1,0:T(8,128)(2,1)} fusion(f32[64,16,1024]{2,1,0:T(8,128)S(1)} %fusion.22, bf16[64,16,352]{2,1,0:T(8,128)(2,1)S(1)} %collective-permute-done.5, bf16[352,1024]{1,0:T(8,128)(2,1)} %collective-permute-done), kind=kOutput, calls=%fused_computation.2 | convolution fusion | flops 740294656 | bytes 7733248 | tf_op jit(solution)/shard_map/sch,hf->scf/dot_general | solution.py:281
  212.4 6.8 %all-to-all-start.1 = ((bf16[64,16,1024]{2,1,0:T(8,128)(2,1)}), bf16[64,16,1024]{2,1,0:T(8,128)(2,1)}, u32[]{:S(2)}, u32[]{:S(2)}) async-start(bf16[64,16,1024]{2,1,0:T(8,128)(2,1)} %add_convert_fusion), calls=%async_computation.1 | async-start | bytes 4194304 | tf_op jit(solution)/shard_map/all_to_all | solution.py:285
  219.3 0.6 gather_fusion
  219.9 0.4 fusion.6
  220.4 31.3 %all-to-all-done.1 = bf16[64,16,1024]{2,1,0:T(8,128)(2,1)} async-done(((bf16[64,16,1024]{2,1,0:T(8,128)(2,1)}), bf16[64,16,1024]{2,1,0:T(8,128)(2,1)}, u32[]{:S(2)}, u32[]{:S(2)}) %all-to-all-start.1) | async-done | bytes 2097184 | tf_op jit(solution)/shard_map/all_to_all | solution.py:285
  251.6 2.0 fusion.71
  253.7 23.2 %collective-permute-start.6 = (bf16[128,512]{1,0:T(8,128)(2,1)S(1)}, bf16[128,512]{1,0:T(8,128)(2,1)S(1)}, u32[]{:S(2)}, u32[]{:S(2)}) collective-permute-start(bf16[128,512]{1,0:T(8,128)(2,1)S(1)} %dynamic-slice_convert_fusion), channel_id=1, source_target_pairs={{0,2},{1,3},{2,0},{3,1},{4,6},{5,7},{6,4},{7,5},{8,10},{9,11},{10,... | collective-permute-start | bytes 393224 | tf_op jit(solution)/shard_map/ppermute | solution.py:293
  277.0 0.8 convolution_convert_fusion.2
  277.8 5.6 %collective-permute-done.6 = bf16[128,512]{1,0:T(8,128)(2,1)S(1)} collective-permute-done((bf16[128,512]{1,0:T(8,128)(2,1)S(1)}, bf16[128,512]{1,0:T(8,128)(2,1)S(1)}, u32[]{:S(2)}, u32[]{:S(2)}) %collective-permute-start.6) | collective-permute-done | bytes 131104 | tf_op jit(solution)/shard_map/ppermute | solution.py:293
  283.4 0.7 add_convert_fusion.1
  (74 shorter events, 1.2 us)
Async XLA Ops:
  0.6 32.1 %copy-start = (bf16[2,1024,576]{1,2,0:T(8,128)(2,1)S(1)}, bf16[2,1024,576]{1,2,0:T(8,128)(2,1)}, u32[]{:S(2)}) copy-start(bf16[2,1024,576]{1,2,0:T(8,128)(2,1)} %param.21) | copy-start | bytes 7077892
  0.7 5.9 %copy-start.19 = (s32[2,64]{1,0:T(2,128)S(1)}, s32[2,64]{1,0:T(2,128)}, u32[]{:S(2)}) copy-start(s32[2,64]{1,0:T(2,128)} %param.23) | copy-start | bytes 1540
  0.7 7.4 %copy-start.16 = (s32[2]{0:T(128)S(1)}, s32[2]{0:T(128)}, u32[]{:S(2)}) copy-start(s32[2]{0:T(128)} %param.22) | copy-start | bytes 28
  3.1 5.9 %copy-start.7 = (bf16[512,512]{1,0:T(8,128)(2,1)S(1)}, bf16[512,512]{1,0:T(8,128)(2,1)}, u32[]{:S(2)}) copy-start(bf16[512,512]{1,0:T(8,128)(2,1)} %param.27) | copy-start | bytes 1572868
  3.1 5.9 %copy-start.9 = (bf16[128,512]{1,0:T(8,128)(2,1)S(1)}, bf16[128,512]{1,0:T(8,128)(2,1)}, u32[]{:S(2)}) copy-start(bf16[128,512]{1,0:T(8,128)(2,1)} %param.19) | copy-start | bytes 393220
  4.1 32.2 %collective-permute-start = (bf16[352,1024]{1,0:T(8,128)(2,1)}, bf16[352,1024]{1,0:T(8,128)(2,1)}, u32[]{:S(2)}, u32[]{:S(2)}) collective-permute-start(bf16[352,1024]{1,0:T(8,128)(2,1)} %pad_maximum_fusion), channel_id=1, source_target_pairs={{0,1},{1,0},{2,3},{3,2},{4,5},{5,4},{6,7},{7,6},{8,9},{9,8},{10,11... | collective-permute-start | bytes 2162696 | tf_op jit(solution)/shard_map/ppermute | solution.py:203
  9.4 6.9 %copy-start.12 = (s32[128,6]{0,1:T(8,128)S(1)}, s32[128,6]{0,1:T(8,128)}, u32[]{:S(2)}) copy-start(s32[128,6]{0,1:T(8,128)} %param.31) | copy-start | bytes 9220
  9.9 10.1 %copy-start.4 = (bf16[128,2048]{1,0:T(8,128)(2,1)S(1)}, bf16[128,2048]{1,0:T(8,128)(2,1)}, u32[]{:S(2)}) copy-start(bf16[128,2048]{1,0:T(8,128)(2,1)} %param.18) | copy-start | bytes 1572868
  10.9 9.1 %copy-start.6 = (bf16[2048,144]{0,1:T(8,128)(2,1)S(1)}, bf16[2048,144]{0,1:T(8,128)(2,1)}, u32[]{:S(2)}) copy-start(bf16[2048,144]{0,1:T(8,128)(2,1)} %param.25) | copy-start | bytes 1769476
  32.7 3.7 %copy-start.13 = (f32[512]{0:T(512)S(1)}, f32[512]{0:T(512)}, u32[]{:S(2)}) copy-start(f32[512]{0:T(512)} %param.26) | copy-start | bytes 6148
  32.7 4.2 %copy-start.8 = (bf16[2,256,512]{1,2,0:T(8,128)(2,1)S(1)}, bf16[2,256,512]{1,2,0:T(8,128)(2,1)}, u32[]{:S(2)}) copy-start(bf16[2,256,512]{1,2,0:T(8,128)(2,1)} %copy.63) | copy-start | bytes 1572868
  32.7 4.2 %copy-start.10 = (bf16[2,256,64]{1,2,0:T(8,128)(2,1)S(1)}, bf16[2,256,64]{1,2,0:T(8,128)(2,1)}, u32[]{:S(2)}) copy-start(bf16[2,256,64]{1,2,0:T(8,128)(2,1)} %copy.64) | copy-start | bytes 196612
  32.7 4.2 %copy-start.11 = (pred[2,256,64]{1,2,0:T(32,128)(4,1)S(1)}, pred[2,256,64]{1,2,0:T(32,128)(4,1)}, u32[]{:S(2)}) copy-start(pred[2,256,64]{1,2,0:T(32,128)(4,1)} %copy.68) | copy-start | bytes 98308
  36.8 2.6 copy-start.1
  43.6 2.3 copy-start.5
  45.7 6.1 %copy-start.15 = (f32[2048]{0:T(1024)S(1)}, f32[2048]{0:T(1024)}, u32[]{:S(2)}) copy-start(f32[2048]{0:T(1024)} %param.30) | copy-start | bytes 24580
  45.8 5.3 %collective-permute-start.1 = (bf16[128,1024]{1,0:T(8,128)(2,1)S(1)}, bf16[128,1024]{1,0:T(8,128)(2,1)S(1)}, u32[]{:S(2)}, u32[]{:S(2)}) collective-permute-start(bf16[128,1024]{1,0:T(8,128)(2,1)S(1)} %pad_maximum_fusion.4), channel_id=1, source_target_pairs={{0,1},{1,0},{2,3},{3,2},{4,5},{5,4},{6,7},{7,6},{8,9},{9,8},{10,11... | collective-permute-start | bytes 786440 | tf_op jit(solution)/shard_map/ppermute | solution.py:241
  51.2 8.9 %collective-permute-start.2 = (bf16[128,1024]{1,0:T(8,128)(2,1)S(1)}, bf16[128,1024]{1,0:T(8,128)(2,1)S(1)}, u32[]{:S(2)}, u32[]{:S(2)}) collective-permute-start(bf16[128,1024]{1,0:T(8,128)(2,1)S(1)} %fusion.28), channel_id=1, source_target_pairs={{0,2},{1,3},{2,0},{3,1},{4,6},{5,7},{6,4},{7,5},{8,10},{9,11},{10,... | collective-permute-start | bytes 786440 | tf_op jit(solution)/shard_map/ppermute | solution.py:244
  60.3 2.8 collective-permute-start.3
  131.7 51.8 %collective-permute-start.4 = (bf16[64,16,1024]{2,1,0:T(8,128)(2,1)}, bf16[64,16,1024]{2,1,0:T(8,128)(2,1)}, u32[]{:S(2)}, u32[]{:S(2)}) collective-permute-start(bf16[64,16,1024]{2,1,0:T(8,128)(2,1)} %all_to_all.10), channel_id=1, source_target_pairs={{0,1},{1,0},{2,3},{3,2},{4,5},{5,4},{6,7},{7,6},{8,9},{9,8},{10,11... | collective-permute-start | bytes 6291464 | tf_op jit(solution)/shard_map/ppermute | solution.py:267
  139.1 46.2 %copy-start.17 = (bf16[1,2048,352]{1,2,0:T(8,128)(2,1)S(1)}, bf16[1,2048,352]{1,2,0:T(8,128)(2,1)}, u32[]{:S(2)}) copy-start(bf16[1,2048,352]{1,2,0:T(8,128)(2,1)} %param.33) | copy-start | bytes 4325380
  185.3 2.4 copy-start.18
  187.6 3.9 %copy-start.2 = (bf16[352,512]{1,0:T(8,128)(2,1)S(1)}, bf16[352,512]{1,0:T(8,128)(2,1)}, u32[]{:S(2)}) copy-start(bf16[352,512]{1,0:T(8,128)(2,1)} %get-tuple-element.12) | copy-start | bytes 1081348
  187.6 3.9 %copy-start.3 = (bf16[352,512]{1,0:T(8,128)(2,1)S(1)}, bf16[352,512]{1,0:T(8,128)(2,1)}, u32[]{:S(2)}) copy-start(bf16[352,512]{1,0:T(8,128)(2,1)} %get-tuple-element.15) | copy-start | bytes 1081348
  190.2 18.4 %collective-permute-start.5 = (bf16[64,16,352]{2,1,0:T(8,128)(2,1)S(1)}, bf16[64,16,352]{2,1,0:T(8,128)(2,1)S(1)}, u32[]{:S(2)}, u32[]{:S(2)}) collective-permute-start(bf16[64,16,352]{2,1,0:T(8,128)(2,1)S(1)} %multiply_convert_fusion), channel_id=1, source_target_pairs={{0,1},{1,0},{2,3},{3,2},{4,5},{5,4},{6,7},{7,6},{8,9},{9,8},{10,11... | collective-permute-start | bytes 2162696 | tf_op jit(solution)/shard_map/ppermute | solution.py:278
  212.4 6.8 %copy-start.20 = (s32[2]{0:T(128)S(1)}, s32[2]{0:T(128)}, u32[]{:S(2)}) copy-start(s32[2]{0:T(128)} %param.24) | copy-start | bytes 28
  212.4 7.4 %copy-start.14 = (bf16[128,6]{0,1:T(8,128)(2,1)S(1)}, bf16[128,6]{0,1:T(8,128)(2,1)}, u32[]{:S(2)}) copy-start(bf16[128,6]{0,1:T(8,128)(2,1)} %param.32) | copy-start | bytes 4612
  212.4 39.2 %all-to-all-start.1 = ((bf16[64,16,1024]{2,1,0:T(8,128)(2,1)}), bf16[64,16,1024]{2,1,0:T(8,128)(2,1)}, u32[]{:S(2)}, u32[]{:S(2)}) async-start(bf16[64,16,1024]{2,1,0:T(8,128)(2,1)} %add_convert_fusion), calls=%async_computation.1 | async-start | bytes 4194304 | tf_op jit(solution)/shard_map/all_to_all | solution.py:285
  253.7 29.7 %collective-permute-start.6 = (bf16[128,512]{1,0:T(8,128)(2,1)S(1)}, bf16[128,512]{1,0:T(8,128)(2,1)S(1)}, u32[]{:S(2)}, u32[]{:S(2)}) collective-permute-start(bf16[128,512]{1,0:T(8,128)(2,1)S(1)} %dynamic-slice_convert_fusion), channel_id=1, source_target_pairs={{0,2},{1,3},{2,0},{3,1},{4,6},{5,7},{6,4},{7,5},{8,10},{9,11},{10,... | collective-permute-start | bytes 393224 | tf_op jit(solution)/shard_map/ppermute | solution.py:293

commit v3 on v2

--- a/solution.py
+++ b/solution.py
@@ -185,7 +185,6 @@
     compressed_part = jnp.dot(layer_in, kv_a, preferred_element_type=jnp.float32).astype(
         jnp.bfloat16
     )
-    compressed = lax.all_gather(compressed_part, "tp", axis=1, tiled=True)
     tp_size = lax.axis_size("tp")
     tp_index = lax.axis_index("tp")
     quarter = D // tp_size
@@ -195,6 +194,17 @@
     def features(block, first):
         return lax.dynamic_slice_in_dim(block, first * quarter, quarter, block.ndim - 1)
 
+    pair_block = jnp.where(
+        parity == 0,
+        jnp.concatenate([compressed_part, lax.ppermute(compressed_part, "tp", beside)], 1),
+        jnp.concatenate([lax.ppermute(compressed_part, "tp", beside), compressed_part], 1),
+    )
+    other_block = lax.ppermute(pair_block, "tp", [(t, t ^ 2) for t in range(tp_size)])
+    compressed = jnp.where(
+        tp_index // 2 == 0,
+        jnp.concatenate([pair_block, other_block], 1),
+        jnp.concatenate([other_block, pair_block], 1),
+    )
     down_local = w_down[0]
     down_own = jnp.concatenate([features(down_local, parity), features(down_local, parity + 2)], -1)
     down_given = jnp.concatenate(

time: 285 us -> 279 us (0.979)
  blocking collectives: 79.4 us -> 64.3 us
  starting transfers between devices: 40.3 us -> 48.7 us
  local copies, waits for them, and re-layouts: 19 us -> 11.6 us
  matrix products: 24.9 us -> 28.3 us
    all_gather x1 -> x0, blocking collectives: 11.5 us -> none  [on_device(): compressed = lax.all_gather(compressed_part, 'tp', axis=1, tiled=True)]
    all_to_all x1, blocking collectives: 67.8 us -> 64.3 us  [on_device(): lax.all_to_all(outgoing[:, slots], 'req', split_axis=0, concat_axis=0, ti...]
    ppermute x0 -> x2, starting transfers between devices: none -> 3.21 us  [the longest x1 3.2 us: on_device(): lax.ppermute(pair_block, 'tp', [(t, t ^ 2) for t in range(tp_size)])]
    concatenate x4, local copies, waits for them, and re-layouts: 4.42 us -> 1.34 us  [on_device(): jnp.concatenate([query_latent, q_pe.reshape(tok_rows, local_heads, ROPE)]...]
  transfers between devices with their start and end apart: 8 -> 10, of which waited for: 7 -> 8; matrix products, arithmetic and copies ran while one was open for 8% -> 8% of each run, Pallas kernels for 0% -> 0%
where the time goes in v3:
time: 279 us; the launch traced here: 278 us
  waiting for transfers between devices  115 us (41%)
  blocking collectives  64.3 us (23%)
  starting transfers between devices  48.7 us (17%)
  matrix products  28.3 us (10%)
  local copies, waits for them, and re-layouts  11.6 us (4%)
  other arithmetic  8.78 us (3%)
    all_to_all x1, blocking collectives, on_device(): lax.all_to_all(outgoing[:, slots], 'req', split_axis=0, concat_axis=0, ti...  64.3 us
    ppermute x1, waiting for transfers between devices, on_device(): partner_rows = lax.ppermute(own_rows, 'tp', beside)  45.4 us
    all_to_all x1, waiting for transfers between devices, on_device(): lax.all_to_all(pair_value, 'req', split_axis=0, concat_axis=0, tiled=True)  31.2 us
    ppermute x1, starting transfers between devices, on_device(): lax.ppermute(give.astype(jnp.bfloat16), 'tp', across).astype(jnp.float32)  23.3 us
    ppermute x1, waiting for transfers between devices, on_device(): partner_hidden = lax.ppermute(expert_hidden, 'tp', beside)  15.9 us
    ppermute x1, waiting for transfers between devices, on_device(): lax.ppermute(pair_sum.astype(jnp.bfloat16), 'tp', across)  10.1 us
    all_to_all x1, starting transfers between devices, on_device(): lax.all_to_all(pair_value, 'req', split_axis=0, concat_axis=0, tiled=True)  6.97 us
  transfers between devices with their start and end apart: 10, of which 8 were waited for; matrix products, arithmetic and copies ran while one was open for 8% of the time, Pallas kernels for 0%

profile of v3, /device:TPU:1, one launch (start us, length us, event | category | flops | bytes accessed | tf_op | source)
XLA Modules:
  0.0 278.0 jit_solution(8974156060240858882)
XLA Ops:
  0.7 2.5 dynamic-slice_bitcast_fusion.1
  3.2 0.9 pad_maximum_fusion
  4.1 2.5 collective-permute-start
  6.6 0.9 convolution_convert_fusion.4
  7.7 0.2 convolution_minimum_fusion.6
  7.9 0.2 convolution_minimum_fusion.5
  8.1 0.2 convolution_minimum_fusion.4
  8.3 0.2 convolution_minimum_fusion.3
  8.5 0.2 convolution_minimum_fusion.2
  8.7 0.2 convolution_minimum_fusion.1
  8.9 0.3 fusion.68
  9.2 0.3 fusion.10
  9.5 0.4 copy.62
  10.0 1.0 copy.63
  11.3 0.6 copy-done.12
  11.9 4.1 %fusion.3 = (f32[2,256]{1,0:T(2,128)}, f32[2,256,1024]{2,1,0:T(8,128)}) fusion(pred[2,1024]{1,0:T(4,128)(4,1)S(1)} %iota_compare_fusion.12, bf16[2,1024,576]{1,2,0:T(8,128)(2,1)S(1)} %copy-done, bf16[2,256,64]{1,2,0:T(8,128)(2,1)S(1)} %copy.64, bf16[2,256,512]{1,2,0:T(8,128)(2,1)} %copy.63), kind=kOutput, calls=%fused_computation.11 | convolution fusion | flops 606731776 | bytes 5050368 | tf_op jit(solution)/shard_map/rqk,rck->rqc/dot_general | solution.py:107
  16.0 0.6 broadcast_add_fusion
  16.8 0.7 eq.89
  17.5 1.7 fusion.13
  19.2 1.3 add.134
  20.7 0.7 copy.68
  21.4 1.0 copy.75
  22.4 0.7 convert_element_type.117
  23.3 0.9 maximum_select_fusion.2
  24.2 3.2 %collective-permute-start.2 = (bf16[128,288]{0,1:T(8,128)(2,1)S(1)}, bf16[128,288]{0,1:T(8,128)(2,1)S(1)}, u32[]{:S(2)}, u32[]{:S(2)}) collective-permute-start(bf16[128,288]{0,1:T(8,128)(2,1)S(1)} %maximum_select_fusion.2), channel_id=1, source_target_pairs={{0,2},{1,3},{2,0},{3,1},{4,6},{5,7},{6,4},{7,5},{8,10},{9,11},{10,... | collective-permute-start | bytes 221192 | tf_op jit(solution)/shard_map/ppermute | solution.py:202
  27.4 1.7 collective-permute-done.2
  29.3 0.8 fusion.31
  30.5 1.2 fusion.69
  31.7 2.1 fusion.4
  33.8 1.1 fusion.14
  34.9 0.4 fusion.40
  35.3 0.2 fusion.17
  35.5 0.9 reshape.159
  36.5 1.5 convolution_convert_fusion.3
  38.0 2.1 fusion.70
  40.2 1.6 collective-permute-start.3
  41.9 3.7 %collective-permute-done.3 = bf16[128,1024]{1,0:T(8,128)(2,1)S(1)} collective-permute-done((bf16[128,1024]{1,0:T(8,128)(2,1)S(1)}, bf16[128,1024]{1,0:T(8,128)(2,1)S(1)}, u32[]{:S(2)}, u32[]{:S(2)}) %collective-permute-start.3) | collective-permute-done | bytes 262176 | tf_op jit(solution)/shard_map/ppermute | solution.py:251
  45.6 3.3 %collective-permute-start.4 = (bf16[128,1024]{1,0:T(8,128)(2,1)S(1)}, bf16[128,1024]{1,0:T(8,128)(2,1)S(1)}, u32[]{:S(2)}, u32[]{:S(2)}) collective-permute-start(bf16[128,1024]{1,0:T(8,128)(2,1)S(1)} %fusion.28), channel_id=1, source_target_pairs={{0,2},{1,3},{2,0},{3,1},{4,6},{5,7},{6,4},{7,5},{8,10},{9,11},{10,... | collective-permute-start | bytes 786440 | tf_op jit(solution)/shard_map/ppermute | solution.py:254
  49.0 0.5 fusion
  49.5 10.1 %collective-permute-done.4 = bf16[128,1024]{1,0:T(8,128)(2,1)S(1)} collective-permute-done((bf16[128,1024]{1,0:T(8,128)(2,1)S(1)}, bf16[128,1024]{1,0:T(8,128)(2,1)S(1)}, u32[]{:S(2)}, u32[]{:S(2)}) %collective-permute-start.4) | collective-permute-done | bytes 262176 | tf_op jit(solution)/shard_map/ppermute | solution.py:254
  59.6 0.2 multiply_reduce_fusion
  59.8 1.2 collective-permute-start.5
  61.0 1.5 collective-permute-done.5
  62.5 0.8 convolution_convert_fusion
  63.3 64.3 %all_to_all.10 = bf16[64,16,1024]{2,1,0:T(8,128)(2,1)S(1)} all-to-all(bf16[64,16,1024]{2,1,0:T(8,128)(2,1)S(1)} %bitcast.78), channel_id=1, replica_groups=mesh['req'=64,'tp'=4] {'req'}, dimensions={0} | all-to-all | bytes 4194304 | tf_op jit(solution)/shard_map/all_to_all | solution.py:276
  127.6 5.4 %collective-permute-start.6 = (bf16[64,16,1024]{2,1,0:T(8,128)(2,1)S(1)}, bf16[64,16,1024]{2,1,0:T(8,128)(2,1)S(1)}, u32[]{:S(2)}, u32[]{:S(2)}) collective-permute-start(bf16[64,16,1024]{2,1,0:T(8,128)(2,1)S(1)} %all_to_all.10), channel_id=1, source_target_pairs={{0,1},{1,0},{2,3},{3,2},{4,5},{5,4},{6,7},{7,6},{8,9},{9,8},{10,11... | collective-permute-start | bytes 6291464 | tf_op jit(solution)/shard_map/ppermute | solution.py:277
  133.0 0.3 fusion.65
  133.3 45.4 %collective-permute-done.6 = bf16[64,16,1024]{2,1,0:T(8,128)(2,1)S(1)} collective-permute-done((bf16[64,16,1024]{2,1,0:T(8,128)(2,1)S(1)}, bf16[64,16,1024]{2,1,0:T(8,128)(2,1)S(1)}, u32[]{:S(2)}, u32[]{:S(2)}) %collective-permute-start.6) | collective-permute-done | bytes 2097184 | tf_op jit(solution)/shard_map/ppermute | solution.py:277
  178.7 0.3 fusion.66
  179.1 2.3 fusion.8
  181.4 2.6 multiply_convert_fusion
  184.0 1.3 collective-permute-start.7
  185.3 1.2 fusion.22
  186.5 15.9 %collective-permute-done.7 = bf16[64,16,352]{2,1,0:T(8,128)(2,1)S(1)} collective-permute-done((bf16[64,16,352]{2,1,0:T(8,128)(2,1)S(1)}, bf16[64,16,352]{2,1,0:T(8,128)(2,1)S(1)}, u32[]{:S(2)}, u32[]{:S(2)}) %collective-permute-start.7) | collective-permute-done | bytes 720928 | tf_op jit(solution)/shard_map/ppermute | solution.py:288
  202.4 3.7 %add_convert_fusion = bf16[64,16,1024]{2,1,0:T(8,128)(2,1)} fusion(f32[64,16,1024]{2,1,0:T(8,128)S(1)} %fusion.22, bf16[64,16,352]{2,1,0:T(8,128)(2,1)S(1)} %collective-permute-done.7, bf16[352,1024]{1,0:T(8,128)(2,1)} %collective-permute-done), kind=kOutput, calls=%fused_computation.2 | convolution fusion | flops 740294656 | bytes 7733248 | tf_op jit(solution)/shard_map/sch,hf->scf/dot_general | solution.py:291
  206.1 7.0 %all-to-all-start.1 = ((bf16[64,16,1024]{2,1,0:T(8,128)(2,1)}), bf16[64,16,1024]{2,1,0:T(8,128)(2,1)}, u32[]{:S(2)}, u32[]{:S(2)}) async-start(bf16[64,16,1024]{2,1,0:T(8,128)(2,1)} %add_convert_fusion), calls=%async_computation.1 | async-start | bytes 4194304 | tf_op jit(solution)/shard_map/all_to_all | solution.py:295
  213.1 0.6 gather_fusion
  213.7 0.4 fusion.6
  214.2 31.2 %all-to-all-done.1 = bf16[64,16,1024]{2,1,0:T(8,128)(2,1)} async-done(((bf16[64,16,1024]{2,1,0:T(8,128)(2,1)}), bf16[64,16,1024]{2,1,0:T(8,128)(2,1)}, u32[]{:S(2)}, u32[]{:S(2)}) %all-to-all-start.1) | async-done | bytes 2097184 | tf_op jit(solution)/shard_map/all_to_all | solution.py:295
  245.4 2.0 fusion.71
  247.5 23.3 %collective-permute-start.8 = (bf16[128,512]{1,0:T(8,128)(2,1)S(1)}, bf16[128,512]{1,0:T(8,128)(2,1)S(1)}, u32[]{:S(2)}, u32[]{:S(2)}) collective-permute-start(bf16[128,512]{1,0:T(8,128)(2,1)S(1)} %dynamic-slice_convert_fusion), channel_id=1, source_target_pairs={{0,2},{1,3},{2,0},{3,1},{4,6},{5,7},{6,4},{7,5},{8,10},{9,11},{10,... | collective-permute-start | bytes 393224 | tf_op jit(solution)/shard_map/ppermute | solution.py:303
  270.9 0.8 convolution_convert_fusion.2
  271.7 5.5 %collective-permute-done.8 = bf16[128,512]{1,0:T(8,128)(2,1)S(1)} collective-permute-done((bf16[128,512]{1,0:T(8,128)(2,1)S(1)}, bf16[128,512]{1,0:T(8,128)(2,1)S(1)}, u32[]{:S(2)}, u32[]{:S(2)}) %collective-permute-start.8) | collective-permute-done | bytes 131104 | tf_op jit(solution)/shard_map/ppermute | solution.py:303
  277.2 0.7 add_convert_fusion.1
  (93 shorter events, 1.9 us)
Async XLA Ops:
  0.6 11.3 %copy-start = (bf16[2,1024,576]{1,2,0:T(8,128)(2,1)S(1)}, bf16[2,1024,576]{1,2,0:T(8,128)(2,1)}, u32[]{:S(2)}) copy-start(bf16[2,1024,576]{1,2,0:T(8,128)(2,1)} %param.21) | copy-start | bytes 7077892
  0.7 5.9 %copy-start.4 = (bf16[128,2048]{1,0:T(8,128)(2,1)S(1)}, bf16[128,2048]{1,0:T(8,128)(2,1)}, u32[]{:S(2)}) copy-start(bf16[128,2048]{1,0:T(8,128)(2,1)} %param.18) | copy-start | bytes 1572868
  0.7 5.9 %copy-start.6 = (bf16[2048,144]{0,1:T(8,128)(2,1)S(1)}, bf16[2048,144]{0,1:T(8,128)(2,1)}, u32[]{:S(2)}) copy-start(bf16[2048,144]{0,1:T(8,128)(2,1)} %param.25) | copy-start | bytes 1769476
  0.7 6.9 %copy-start.23 = (s32[2]{0:T(128)S(1)}, s32[2]{0:T(128)}, u32[]{:S(2)}) copy-start(s32[2]{0:T(128)} %param.22) | copy-start | bytes 28
  0.7 6.9 %copy-start.26 = (s32[2,64]{1,0:T(2,128)S(1)}, s32[2,64]{1,0:T(2,128)}, u32[]{:S(2)}) copy-start(s32[2,64]{1,0:T(2,128)} %param.23) | copy-start | bytes 1540
  3.2 6.0 %copy-start.7 = (bf16[512,512]{1,0:T(8,128)(2,1)S(1)}, bf16[512,512]{1,0:T(8,128)(2,1)}, u32[]{:S(2)}) copy-start(bf16[512,512]{1,0:T(8,128)(2,1)} %param.27) | copy-start | bytes 1572868
  3.2 6.0 %copy-start.10 = (bf16[128,512]{1,0:T(8,128)(2,1)S(1)}, bf16[128,512]{1,0:T(8,128)(2,1)}, u32[]{:S(2)}) copy-start(bf16[128,512]{1,0:T(8,128)(2,1)} %param.19) | copy-start | bytes 393220
  4.1 25.0 %collective-permute-start = (bf16[352,1024]{1,0:T(8,128)(2,1)}, bf16[352,1024]{1,0:T(8,128)(2,1)}, u32[]{:S(2)}, u32[]{:S(2)}) collective-permute-start(bf16[352,1024]{1,0:T(8,128)(2,1)} %pad_maximum_fusion), channel_id=1, source_target_pairs={{0,1},{1,0},{2,3},{3,2},{4,5},{5,4},{6,7},{7,6},{8,9},{9,8},{10,11... | collective-permute-start | bytes 2162696 | tf_op jit(solution)/shard_map/ppermute | solution.py:213
  7.5 15.7 %collective-permute-start.1 = (bf16[128,144]{0,1:T(8,128)(2,1)}, bf16[128,144]{0,1:T(8,128)(2,1)}, u32[]{:S(2)}, u32[]{:S(2)}) collective-permute-start(bf16[128,144]{0,1:T(8,128)(2,1)} %convolution_convert_fusion.4), channel_id=1, source_target_pairs={{0,1},{1,0},{2,3},{3,2},{4,5},{5,4},{6,7},{7,6},{8,9},{9,8},{10,11... | collective-permute-start | bytes 110600 | tf_op jit(solution)/shard_map/ppermute | solution.py:199
  7.7 3.6 %copy-start.14 = (pred[2,1024]{1,0:T(4,128)(4,1)}, pred[2,1024]{1,0:T(4,128)(4,1)S(1)}, u32[]{:S(2)}) copy-start(pred[2,1024]{1,0:T(4,128)(4,1)S(1)} %iota_compare_fusion.12) | copy-start | bytes 6148
  9.2 1.8 copy-start.11
  11.3 0.6 copy-start.12
  11.9 4.7 %copy-start.16 = (s32[128,6]{0,1:T(8,128)S(1)}, s32[128,6]{0,1:T(8,128)}, u32[]{:S(2)}) copy-start(s32[128,6]{0,1:T(8,128)} %param.31) | copy-start | bytes 9220
  11.9 9.5 %copy-start.8 = (bf16[512,512]{1,0:T(8,128)(2,1)S(1)}, bf16[512,512]{1,0:T(8,128)(2,1)}, u32[]{:S(2)}) copy-start(bf16[512,512]{1,0:T(8,128)(2,1)} %param.28) | copy-start | bytes 1572868
  16.0 14.5 %copy-start.9 = (bf16[2,256,512]{1,2,0:T(8,128)(2,1)S(1)}, bf16[2,256,512]{1,2,0:T(8,128)(2,1)}, u32[]{:S(2)}) copy-start(bf16[2,256,512]{1,2,0:T(8,128)(2,1)} %copy.63) | copy-start | bytes 1572868
  17.5 13.0 %copy-start.13 = (bf16[2,256,64]{1,2,0:T(8,128)(2,1)S(1)}, bf16[2,256,64]{1,2,0:T(8,128)(2,1)}, u32[]{:S(2)}) copy-start(bf16[2,256,64]{1,2,0:T(8,128)(2,1)} %copy-done.12) | copy-start | bytes 196612
  20.6 9.5 %copy-start.22 = (f32[128]{0:T(128)S(1)}, f32[128]{0:T(128)}, u32[]{:S(2)}) copy-start(f32[128]{0:T(128)} %add.134) | copy-start | bytes 1540
  20.6 11.0 %copy-start.20 = (f32[2,256]{1,0:T(2,128)S(1)}, f32[2,256]{1,0:T(2,128)}, u32[]{:S(2)}) copy-start(f32[2,256]{1,0:T(2,128)} %get-tuple-element.30) | copy-start | bytes 6148
  20.6 11.0 %copy-start.15 = (pred[2,1024]{1,0:T(4,128)(4,1)S(1)}, pred[2,1024]{1,0:T(4,128)(4,1)}, u32[]{:S(2)}) copy-start(pred[2,1024]{1,0:T(4,128)(4,1)} %copy-done.14) | copy-start | bytes 6148
  24.2 4.9 %collective-permute-start.2 = (bf16[128,288]{0,1:T(8,128)(2,1)S(1)}, bf16[128,288]{0,1:T(8,128)(2,1)S(1)}, u32[]{:S(2)}, u32[]{:S(2)}) collective-permute-start(bf16[128,288]{0,1:T(8,128)(2,1)S(1)} %maximum_select_fusion.2), channel_id=1, source_target_pairs={{0,2},{1,3},{2,0},{3,1},{4,6},{5,7},{6,4},{7,5},{8,10},{9,11},{10,... | collective-permute-start | bytes 221192 | tf_op jit(solution)/shard_map/ppermute | solution.py:202
  30.4 3.4 %copy-start.1 = (f32[2,256,1024]{2,1,0:T(8,128)S(1)}, f32[2,256,1024]{2,1,0:T(8,128)}, u32[]{:S(2)}) copy-start(f32[2,256,1024]{2,1,0:T(8,128)} %get-tuple-element.31) | copy-start | bytes 6291460
  38.0 3.8 %copy-start.17 = (s32[128,6]{0,1:T(8,128)S(1)}, s32[128,6]{0,1:T(8,128)}, u32[]{:S(2)}) copy-start(s32[128,6]{0,1:T(8,128)} %param.31) | copy-start | bytes 9220
  38.0 3.8 %copy-start.5 = (bf16[128,2048]{1,0:T(8,128)(2,1)S(1)}, bf16[128,2048]{1,0:T(8,128)(2,1)}, u32[]{:S(2)}) copy-start(bf16[128,2048]{1,0:T(8,128)(2,1)} %param.18) | copy-start | bytes 1572868
  40.1 8.8 %copy-start.21 = (f32[2048]{0:T(1024)S(1)}, f32[2048]{0:T(1024)}, u32[]{:S(2)}) copy-start(f32[2048]{0:T(1024)} %param.30) | copy-start | bytes 24580
  40.2 5.4 %collective-permute-start.3 = (bf16[128,1024]{1,0:T(8,128)(2,1)S(1)}, bf16[128,1024]{1,0:T(8,128)(2,1)S(1)}, u32[]{:S(2)}, u32[]{:S(2)}) collective-permute-start(bf16[128,1024]{1,0:T(8,128)(2,1)S(1)} %pad_maximum_fusion.4), channel_id=1, source_target_pairs={{0,1},{1,0},{2,3},{3,2},{4,5},{5,4},{6,7},{7,6},{8,9},{9,8},{10,11... | collective-permute-start | bytes 786440 | tf_op jit(solution)/shard_map/ppermute | solution.py:251
  45.6 14.0 %collective-permute-start.4 = (bf16[128,1024]{1,0:T(8,128)(2,1)S(1)}, bf16[128,1024]{1,0:T(8,128)(2,1)S(1)}, u32[]{:S(2)}, u32[]{:S(2)}) collective-permute-start(bf16[128,1024]{1,0:T(8,128)(2,1)S(1)} %fusion.28), channel_id=1, source_target_pairs={{0,2},{1,3},{2,0},{3,1},{4,6},{5,7},{6,4},{7,5},{8,10},{9,11},{10,... | collective-permute-start | bytes 786440 | tf_op jit(solution)/shard_map/ppermute | solution.py:254
  59.8 2.7 collective-permute-start.5
  127.6 51.1 %collective-permute-start.6 = (bf16[64,16,1024]{2,1,0:T(8,128)(2,1)S(1)}, bf16[64,16,1024]{2,1,0:T(8,128)(2,1)S(1)}, u32[]{:S(2)}, u32[]{:S(2)}) collective-permute-start(bf16[64,16,1024]{2,1,0:T(8,128)(2,1)S(1)} %all_to_all.10), channel_id=1, source_target_pairs={{0,1},{1,0},{2,3},{3,2},{4,5},{5,4},{6,7},{7,6},{8,9},{9,8},{10,11... | collective-permute-start | bytes 6291464 | tf_op jit(solution)/shard_map/ppermute | solution.py:277
  133.3 45.8 %copy-start.24 = (bf16[1,2048,352]{1,2,0:T(8,128)(2,1)S(1)}, bf16[1,2048,352]{1,2,0:T(8,128)(2,1)}, u32[]{:S(2)}) copy-start(bf16[1,2048,352]{1,2,0:T(8,128)(2,1)} %param.33) | copy-start | bytes 4325380
  179.0 2.4 copy-start.25
  181.4 3.9 %copy-start.2 = (bf16[352,512]{1,0:T(8,128)(2,1)S(1)}, bf16[352,512]{1,0:T(8,128)(2,1)}, u32[]{:S(2)}) copy-start(bf16[352,512]{1,0:T(8,128)(2,1)} %get-tuple-element.12) | copy-start | bytes 1081348
  181.4 3.9 %copy-start.3 = (bf16[352,512]{1,0:T(8,128)(2,1)S(1)}, bf16[352,512]{1,0:T(8,128)(2,1)}, u32[]{:S(2)}) copy-start(bf16[352,512]{1,0:T(8,128)(2,1)} %get-tuple-element.15) | copy-start | bytes 1081348
  184.0 18.4 %collective-permute-start.7 = (bf16[64,16,352]{2,1,0:T(8,128)(2,1)S(1)}, bf16[64,16,352]{2,1,0:T(8,128)(2,1)S(1)}, u32[]{:S(2)}, u32[]{:S(2)}) collective-permute-start(bf16[64,16,352]{2,1,0:T(8,128)(2,1)S(1)} %multiply_convert_fusion), channel_id=1, source_target_pairs={{0,1},{1,0},{2,3},{3,2},{4,5},{5,4},{6,7},{7,6},{8,9},{9,8},{10,11... | collective-permute-start | bytes 2162696 | tf_op jit(solution)/shard_map/ppermute | solution.py:288
  206.1 7.0 %copy-start.27 = (s32[2]{0:T(128)S(1)}, s32[2]{0:T(128)}, u32[]{:S(2)}) copy-start(s32[2]{0:T(128)} %param.24) | copy-start | bytes 28
  206.1 7.6 %copy-start.19 = (bf16[128,6]{0,1:T(8,128)(2,1)S(1)}, bf16[128,6]{0,1:T(8,128)(2,1)}, u32[]{:S(2)}) copy-start(bf16[128,6]{0,1:T(8,128)(2,1)} %param.32) | copy-start | bytes 4612
  206.1 39.3 %all-to-all-start.1 = ((bf16[64,16,1024]{2,1,0:T(8,128)(2,1)}), bf16[64,16,1024]{2,1,0:T(8,128)(2,1)}, u32[]{:S(2)}, u32[]{:S(2)}) async-start(bf16[64,16,1024]{2,1,0:T(8,128)(2,1)} %add_convert_fusion), calls=%async_computation.1 | async-start | bytes 4194304 | tf_op jit(solution)/shard_map/all_to_all | solution.py:295
  213.1 57.8 %copy-start.18 = (f32[2,64]{1,0:T(2,128)S(1)}, f32[2,64]{1,0:T(2,128)}, u32[]{:S(2)}) copy-start(f32[2,64]{1,0:T(2,128)} %get-tuple-element.26) | copy-start | bytes 1540
  247.5 29.7 %collective-permute-start.8 = (bf16[128,512]{1,0:T(8,128)(2,1)S(1)}, bf16[128,512]{1,0:T(8,128)(2,1)S(1)}, u32[]{:S(2)}, u32[]{:S(2)}) collective-permute-start(bf16[128,512]{1,0:T(8,128)(2,1)S(1)} %dynamic-slice_convert_fusion), channel_id=1, source_target_pairs={{0,2},{1,3},{2,0},{3,1},{4,6},{5,7},{6,4},{7,5},{8,10},{9,11},{10,... | collective-permute-start | bytes 393224 | tf_op jit(solution)/shard_map/ppermute | solution.py:303

commit v4 on v3

--- a/solution.py
+++ b/solution.py
@@ -211,7 +211,21 @@
         [features(down_local, 1 - parity), features(down_local, 3 - parity)], -1
     )
     down_partner = lax.ppermute(down_given, "tp", beside)
-    down_partner, compressed = lax.optimization_barrier((down_partner, compressed))
+    def feature_rows(weight, which):
+        return jnp.concatenate(
+            [
+                lax.dynamic_slice_in_dim(weight, which * quarter, quarter, 0),
+                lax.dynamic_slice_in_dim(weight, (which + 2) * quarter, quarter, 0),
+            ],
+            0,
+        )
+
+    gate_up_local = jnp.concatenate([w_gate[0], w_up[0]], 1)
+    gate_up_own = feature_rows(gate_up_local, parity)
+    gate_up_partner = lax.ppermute(feature_rows(gate_up_local, 1 - parity), "tp", beside)
+    down_partner, gate_up_partner, compressed = lax.optimization_barrier(
+        (down_partner, gate_up_partner, compressed)
+    )
     ancestry = jax.vmap(ancestors)(parents)
     depths = jnp.sum(ancestry, -1) - 1.0
     positions = (lengths.astype(jnp.float32)[:, None] + depths).reshape(-1)
@@ -274,16 +288,15 @@
     for chunk in range(chunks):
         slots = slice(chunk * slot_step, (chunk + 1) * slot_step)
         own_rows = lax.all_to_all(outgoing[:, slots], "req", split_axis=0, concat_axis=0, tiled=True)
-        partner_rows = lax.ppermute(own_rows, "tp", beside)
-        low_own, high_own = own_rows[..., :quarter], own_rows[..., quarter:]
-        low_partner, high_partner = partner_rows[..., :quarter], partner_rows[..., quarter:]
-        row_set = jnp.where(
-            parity == 0,
-            jnp.concatenate([low_own, low_partner, high_own, high_partner], -1),
-            jnp.concatenate([low_partner, low_own, high_partner, high_own], -1),
+        own_part = jnp.einsum(
+            "scf,fh->sch", own_rows, gate_up_own, preferred_element_type=jnp.float32
         )
-        gate_act = jnp.einsum("scf,fh->sch", row_set, w_gate[0], preferred_element_type=jnp.float32)
-        up_act = jnp.einsum("scf,fh->sch", row_set, w_up[0], preferred_element_type=jnp.float32)
+        given_part = jnp.einsum(
+            "scf,fh->sch", own_rows, gate_up_partner, preferred_element_type=jnp.float32
+        ).astype(jnp.bfloat16)
+        pre_act = own_part + lax.ppermute(given_part, "tp", beside).astype(jnp.float32)
+        hidden_size = pre_act.shape[-1] // 2
+        gate_act, up_act = pre_act[..., :hidden_size], pre_act[..., hidden_size:]
         expert_hidden = (jax.nn.silu(gate_act) * up_act).astype(jnp.bfloat16)
         partner_hidden = lax.ppermute(expert_hidden, "tp", beside)
         pair_value = (

time: 279 us -> 300 us (1.075)
  waiting for transfers between devices: 115 us -> 132 us
  other arithmetic: 8.78 us -> 13.8 us
    ppermute x1, waiting for transfers between devices: 0.01 us -> 26.3 us  [on_device(): lax.ppermute(compressed_part, 'tp', beside)]
    ppermute x1 -> x2, waiting for transfers between devices: 45.4 us -> 34.5 us  [the longest x1 34.5 us: on_device(): lax.ppermute(given_part, 'tp', beside).astype(jnp.float32)]
    concatenate x0 -> x2, other arithmetic: none -> 4.56 us  [the longest x1 3.28 us: on_device(): gate_up_local = jnp.concatenate([w_gate[0], w_up[0]], 1)]
    ppermute x1 -> x2, starting transfers between devices: 5.36 us -> 7.98 us  [the longest x1 5.53 us: on_device(): lax.ppermute(given_part, 'tp', beside).astype(jnp.float32)]
  transfers between devices with their start and end apart: 10 -> 11, of which waited for: 8 -> 9; matrix products, arithmetic and copies ran while one was open for 8% -> 8% of each run, Pallas kernels for 0% -> 0%
where the time goes in v4:
time: 300 us; the launch traced here: 299 us
  waiting for transfers between devices  132 us (44%)
  blocking collectives  63.2 us (21%)
  starting transfers between devices  50.4 us (17%)
  matrix products  28.4 us (9%)
  other arithmetic  13.8 us (5%)
  local copies, waits for them, and re-layouts  10.1 us (3%)
    all_to_all x1, blocking collectives, on_device(): lax.all_to_all(outgoing[:, slots], 'req', split_axis=0, concat_axis=0, ti...  63.2 us
    ppermute x1, waiting for transfers between devices, on_device(): lax.ppermute(given_part, 'tp', beside).astype(jnp.float32)  34.5 us
    all_to_all x1, waiting for transfers between devices, on_device(): lax.all_to_all(pair_value, 'req', split_axis=0, concat_axis=0, tiled=True)  31.3 us
    ppermute x1, waiting for transfers between devices, on_device(): lax.ppermute(compressed_part, 'tp', beside)  26.3 us
    ppermute x1, starting transfers between devices, on_device(): lax.ppermute(give.astype(jnp.bfloat16), 'tp', across).astype(jnp.float32)  23.2 us
    ppermute x1, waiting for transfers between devices, on_device(): partner_hidden = lax.ppermute(expert_hidden, 'tp', beside)  15.8 us
    ppermute x1, waiting for transfers between devices, on_device(): lax.ppermute(pair_sum.astype(jnp.bfloat16), 'tp', across)  11 us
    all_to_all x1, starting transfers between devices, on_device(): lax.all_to_all(pair_value, 'req', split_axis=0, concat_axis=0, tiled=True)  7.04 us
  transfers between devices with their start and end apart: 11, of which 9 were waited for; matrix products, arithmetic and copies ran while one was open for 8% of the time, Pallas kernels for 0%

profile of v4, /device:TPU:1, one launch (start us, length us, event | category | flops | bytes accessed | tf_op | source)
XLA Modules:
  0.0 299.1 jit_solution(14055017532223907049)
XLA Ops:
  0.7 3.3 %fusion.27 = (bf16[512,704]{0,1:T(8,128)(2,1)}, bf16[512,704]{0,1:T(8,128)(2,1)S(1)}, bf16[512,704]{0,1:T(8,128)(2,1)S(1)}, bf16[512,704]{0,1:T(8,128)(2,1)}) fusion(s32[]{:T(128)S(6)} %select_n.85, bf16[2048,352]{0,1:T(8,128)(2,1)} %bitcast.88, bf16[2048,352]{0,1:T(8,128)(2,1)} %bitcast.89, s32[]{:T(128)S(6)} %select_n.88, s32[]{:T(128)S(6)} %select_n.89, ...), kind=kLoop, calls=%fused_computation.59 | loop fusion | flops 5767168 | bytes 5767184 | tf_op jit(solution)/shard_map/concatenate | solution.py:223
  4.0 1.3 pad_maximum_fusion
  5.2 2.5 collective-permute-start.1
  7.7 1.0 dynamic-slice_bitcast_fusion.1
  8.7 0.9 pad_maximum_fusion.1
  9.7 0.6 collective-permute-start
  10.2 0.9 convolution_convert_fusion.5
  11.2 0.9 collective-permute-start.2
  12.1 0.2 convolution_minimum_fusion.6
  13.3 0.3 fusion.76
  13.6 0.3 fusion.12
  13.9 0.4 copy.62
  14.5 1.0 copy.63
  15.8 0.5 copy-done.15
  16.4 0.6 copy-done.17
  17.0 4.0 %fusion.3 = (f32[2,256]{1,0:T(2,128)}, f32[2,256,1024]{2,1,0:T(8,128)}) fusion(pred[2,1024]{1,0:T(4,128)(4,1)S(1)} %iota_compare_fusion.12, bf16[2,1024,576]{1,2,0:T(8,128)(2,1)S(1)} %copy-done, bf16[2,256,64]{1,2,0:T(8,128)(2,1)S(1)} %copy.64, bf16[2,256,512]{1,2,0:T(8,128)(2,1)} %copy.63), kind=kOutput, calls=%fused_computation.19 | convolution fusion | flops 606731776 | bytes 5050368 | tf_op jit(solution)/shard_map/rqk,rck->rqc/dot_general | solution.py:107
  21.0 0.6 broadcast_add_fusion
  21.7 0.7 eq.88
  22.5 1.7 fusion.15
  24.2 1.3 add.143
  25.6 0.7 copy.68
  26.3 1.1 copy.75
  27.4 0.7 convert_element_type.123
  28.3 26.3 %collective-permute-done.2 = bf16[128,144]{0,1:T(8,128)(2,1)} collective-permute-done((bf16[128,144]{0,1:T(8,128)(2,1)}, bf16[128,144]{0,1:T(8,128)(2,1)}, u32[]{:S(2)}, u32[]{:S(2)}) %collective-permute-start.2) | collective-permute-done | bytes 36896 | tf_op jit(solution)/shard_map/ppermute | solution.py:199
  54.5 0.9 maximum_select_fusion.1
  55.4 4.0 %collective-permute-start.3 = (bf16[128,288]{0,1:T(8,128)(2,1)S(1)}, bf16[128,288]{0,1:T(8,128)(2,1)S(1)}, u32[]{:S(2)}, u32[]{:S(2)}) collective-permute-start(bf16[128,288]{0,1:T(8,128)(2,1)S(1)} %maximum_select_fusion.1), channel_id=1, source_target_pairs={{0,2},{1,3},{2,0},{3,1},{4,6},{5,7},{6,4},{7,5},{8,10},{9,11},{10,... | collective-permute-start | bytes 221192 | tf_op jit(solution)/shard_map/ppermute | solution.py:202
  59.4 1.7 collective-permute-done.3
  61.3 0.8 fusion.40
  62.5 1.2 fusion.77
  63.7 2.1 fusion.4
  65.8 1.1 fusion.16
  66.9 0.4 fusion.49
  67.3 0.2 fusion.19
  67.6 0.9 reshape.159
  68.5 1.5 convolution_convert_fusion.4
  70.0 2.1 fusion.78
  72.3 1.6 collective-permute-start.4
  74.0 3.7 %collective-permute-done.4 = bf16[128,1024]{1,0:T(8,128)(2,1)S(1)} collective-permute-done((bf16[128,1024]{1,0:T(8,128)(2,1)S(1)}, bf16[128,1024]{1,0:T(8,128)(2,1)S(1)}, u32[]{:S(2)}, u32[]{:S(2)}) %collective-permute-start.4) | collective-permute-done | bytes 262176 | tf_op jit(solution)/shard_map/ppermute | solution.py:265
  77.7 3.5 %collective-permute-start.5 = (bf16[128,1024]{1,0:T(8,128)(2,1)S(1)}, bf16[128,1024]{1,0:T(8,128)(2,1)S(1)}, u32[]{:S(2)}, u32[]{:S(2)}) collective-permute-start(bf16[128,1024]{1,0:T(8,128)(2,1)S(1)} %fusion.37), channel_id=1, source_target_pairs={{0,2},{1,3},{2,0},{3,1},{4,6},{5,7},{6,4},{7,5},{8,10},{9,11},{10,... | collective-permute-start | bytes 786440 | tf_op jit(solution)/shard_map/ppermute | solution.py:268
  81.3 0.5 fusion
  81.7 11.0 %collective-permute-done.5 = bf16[128,1024]{1,0:T(8,128)(2,1)S(1)} collective-permute-done((bf16[128,1024]{1,0:T(8,128)(2,1)S(1)}, bf16[128,1024]{1,0:T(8,128)(2,1)S(1)}, u32[]{:S(2)}, u32[]{:S(2)}) %collective-permute-start.5) | collective-permute-done | bytes 262176 | tf_op jit(solution)/shard_map/ppermute | solution.py:268
  92.7 0.2 multiply_reduce_fusion
  92.9 0.3 collective-permute-start.6
  93.2 2.2 collective-permute-done.6
  95.4 0.8 convolution_convert_fusion
  96.2 63.2 %all_to_all.10 = bf16[64,16,1024]{2,1,0:T(8,128)(2,1)S(1)} all-to-all(bf16[64,16,1024]{2,1,0:T(8,128)(2,1)S(1)} %bitcast.84), channel_id=1, replica_groups=mesh['req'=64,'tp'=4] {'req'}, dimensions={0} | all-to-all | bytes 4194304 | tf_op jit(solution)/shard_map/all_to_all | solution.py:290
  159.4 3.3 %convolution_convert_fusion.1 = bf16[64,16,704]{2,1,0:T(8,128)(2,1)S(1)} fusion(bf16[64,16,1024]{2,1,0:T(8,128)(2,1)S(1)} %all_to_all.10, bf16[1024,704]{0,1:T(8,128)(2,1)} %collective-permute-done.1), kind=kOutput, calls=%fused_computation.20 | convolution fusion | flops 1477115904 | bytes 4980736 | tf_op jit(solution)/shard_map/scf,fh->sch/dot_general | solution.py:294
  162.7 5.5 %collective-permute-start.7 = (bf16[64,16,704]{2,1,0:T(8,128)(2,1)S(1)}, bf16[64,16,704]{2,1,0:T(8,128)(2,1)S(1)}, u32[]{:S(2)}, u32[]{:S(2)}) collective-permute-start(bf16[64,16,704]{2,1,0:T(8,128)(2,1)S(1)} %convolution_convert_fusion.1), channel_id=1, source_target_pairs={{0,1},{1,0},{2,3},{3,2},{4,5},{5,4},{6,7},{7,6},{8,9},{9,8},{10,11... | collective-permute-start | bytes 4325384 | tf_op jit(solution)/shard_map/ppermute | solution.py:297
  168.2 34.5 %collective-permute-done.7 = bf16[64,16,704]{2,1,0:T(8,128)(2,1)S(1)} collective-permute-done((bf16[64,16,704]{2,1,0:T(8,128)(2,1)S(1)}, bf16[64,16,704]{2,1,0:T(8,128)(2,1)S(1)}, u32[]{:S(2)}, u32[]{:S(2)}) %collective-permute-start.7) | collective-permute-done | bytes 1441824 | tf_op jit(solution)/shard_map/ppermute | solution.py:297
  202.8 1.8 convert_add_fusion
  204.6 0.5 fusion.7
  205.1 1.3 collective-permute-start.8
  206.4 1.2 fusion.28
  207.6 15.8 %collective-permute-done.8 = bf16[64,16,352]{2,1,0:T(8,128)(2,1)S(1)} collective-permute-done((bf16[64,16,352]{2,1,0:T(8,128)(2,1)S(1)}, bf16[64,16,352]{2,1,0:T(8,128)(2,1)S(1)}, u32[]{:S(2)}, u32[]{:S(2)}) %collective-permute-start.8) | collective-permute-done | bytes 720928 | tf_op jit(solution)/shard_map/ppermute | solution.py:301
  223.5 3.7 %add_convert_fusion = bf16[64,16,1024]{2,1,0:T(8,128)(2,1)} fusion(f32[64,16,1024]{2,1,0:T(8,128)S(1)} %fusion.28, bf16[64,16,352]{2,1,0:T(8,128)(2,1)S(1)} %collective-permute-done.8, bf16[352,1024]{1,0:T(8,128)(2,1)} %collective-permute-done), kind=kOutput, calls=%fused_computation.1 | convolution fusion | flops 740294656 | bytes 7733248 | tf_op jit(solution)/shard_map/sch,hf->scf/dot_general | solution.py:304
  227.2 7.0 %all-to-all-start.1 = ((bf16[64,16,1024]{2,1,0:T(8,128)(2,1)}), bf16[64,16,1024]{2,1,0:T(8,128)(2,1)}, u32[]{:S(2)}, u32[]{:S(2)}) async-start(bf16[64,16,1024]{2,1,0:T(8,128)(2,1)} %add_convert_fusion), calls=%async_computation.1 | async-start | bytes 4194304 | tf_op jit(solution)/shard_map/all_to_all | solution.py:308
  234.3 0.6 gather_fusion
  234.9 0.4 fusion.6
  235.4 31.3 %all-to-all-done.1 = bf16[64,16,1024]{2,1,0:T(8,128)(2,1)} async-done(((bf16[64,16,1024]{2,1,0:T(8,128)(2,1)}), bf16[64,16,1024]{2,1,0:T(8,128)(2,1)}, u32[]{:S(2)}, u32[]{:S(2)}) %all-to-all-start.1) | async-done | bytes 2097184 | tf_op jit(solution)/shard_map/all_to_all | solution.py:308
  266.6 2.0 fusion.79
  268.7 23.2 %collective-permute-start.9 = (bf16[128,512]{1,0:T(8,128)(2,1)S(1)}, bf16[128,512]{1,0:T(8,128)(2,1)S(1)}, u32[]{:S(2)}, u32[]{:S(2)}) collective-permute-start(bf16[128,512]{1,0:T(8,128)(2,1)S(1)} %dynamic-slice_convert_fusion), channel_id=1, source_target_pairs={{0,2},{1,3},{2,0},{3,1},{4,6},{5,7},{6,4},{7,5},{8,10},{9,11},{10,... | collective-permute-start | bytes 393224 | tf_op jit(solution)/shard_map/ppermute | solution.py:316
  292.0 0.9 convolution_convert_fusion.3
  292.8 5.6 %collective-permute-done.9 = bf16[128,512]{1,0:T(8,128)(2,1)S(1)} collective-permute-done((bf16[128,512]{1,0:T(8,128)(2,1)S(1)}, bf16[128,512]{1,0:T(8,128)(2,1)S(1)}, u32[]{:S(2)}, u32[]{:S(2)}) %collective-permute-start.9) | collective-permute-done | bytes 131104 | tf_op jit(solution)/shard_map/ppermute | solution.py:316
  298.4 0.7 add_convert_fusion.1
  (98 shorter events, 2.8 us)
Async XLA Ops:
  0.6 16.4 %copy-start = (bf16[2,1024,576]{1,2,0:T(8,128)(2,1)S(1)}, bf16[2,1024,576]{1,2,0:T(8,128)(2,1)}, u32[]{:S(2)}) copy-start(bf16[2,1024,576]{1,2,0:T(8,128)(2,1)} %param.21) | copy-start | bytes 7077892
  3.9 3.7 %copy-start.4 = (bf16[1,352,2048]{2,1,0:T(8,128)(2,1)S(1)}, bf16[1,352,2048]{2,1,0:T(8,128)(2,1)}, u32[]{:S(2)}) copy-start(bf16[1,352,2048]{2,1,0:T(8,128)(2,1)} %param.35) | copy-start | bytes 4325380
  5.2 5.0 %copy-start.5 = (bf16[128,2048]{1,0:T(8,128)(2,1)S(1)}, bf16[128,2048]{1,0:T(8,128)(2,1)}, u32[]{:S(2)}) copy-start(bf16[128,2048]{1,0:T(8,128)(2,1)} %param.18) | copy-start | bytes 1572868
  5.2 5.0 %copy-start.9 = (bf16[2048,144]{0,1:T(8,128)(2,1)S(1)}, bf16[2048,144]{0,1:T(8,128)(2,1)}, u32[]{:S(2)}) copy-start(bf16[2048,144]{0,1:T(8,128)(2,1)} %param.25) | copy-start | bytes 1769476
  5.2 6.8 %copy-start.27 = (s32[2,64]{1,0:T(2,128)S(1)}, s32[2,64]{1,0:T(2,128)}, u32[]{:S(2)}) copy-start(s32[2,64]{1,0:T(2,128)} %param.23) | copy-start | bytes 1540
  5.2 55.9 %collective-permute-start.1 = (bf16[1024,704]{0,1:T(8,128)(2,1)}, bf16[1024,704]{0,1:T(8,128)(2,1)}, u32[]{:S(2)}, u32[]{:S(2)}) collective-permute-start(bf16[1024,704]{0,1:T(8,128)(2,1)} %pad_maximum_fusion), channel_id=1, source_target_pairs={{0,1},{1,0},{2,3},{3,2},{4,5},{5,4},{6,7},{7,6},{8,9},{9,8},{10,11... | collective-permute-start | bytes 4325384 | tf_op jit(solution)/shard_map/ppermute | solution.py:225
  8.7 4.9 %copy-start.26 = (s32[2]{0:T(128)S(1)}, s32[2]{0:T(128)}, u32[]{:S(2)}) copy-start(s32[2]{0:T(128)} %param.22) | copy-start | bytes 28
  8.7 4.9 %copy-start.10 = (bf16[512,512]{1,0:T(8,128)(2,1)S(1)}, bf16[512,512]{1,0:T(8,128)(2,1)}, u32[]{:S(2)}) copy-start(bf16[512,512]{1,0:T(8,128)(2,1)} %param.27) | copy-start | bytes 1572868
  8.7 4.9 %copy-start.13 = (bf16[128,512]{1,0:T(8,128)(2,1)S(1)}, bf16[128,512]{1,0:T(8,128)(2,1)}, u32[]{:S(2)}) copy-start(bf16[128,512]{1,0:T(8,128)(2,1)} %param.19) | copy-start | bytes 393220
  9.7 51.5 %collective-permute-start = (bf16[352,1024]{1,0:T(8,128)(2,1)}, bf16[352,1024]{1,0:T(8,128)(2,1)}, u32[]{:S(2)}, u32[]{:S(2)}) collective-permute-start(bf16[352,1024]{1,0:T(8,128)(2,1)} %pad_maximum_fusion.1), channel_id=1, source_target_pairs={{0,1},{1,0},{2,3},{3,2},{4,5},{5,4},{6,7},{7,6},{8,9},{9,8},{10,11... | collective-permute-start | bytes 2162696 | tf_op jit(solution)/shard_map/ppermute | solution.py:213
  11.2 43.3 %collective-permute-start.2 = (bf16[128,144]{0,1:T(8,128)(2,1)}, bf16[128,144]{0,1:T(8,128)(2,1)}, u32[]{:S(2)}, u32[]{:S(2)}) collective-permute-start(bf16[128,144]{0,1:T(8,128)(2,1)} %convolution_convert_fusion.5), channel_id=1, source_target_pairs={{0,1},{1,0},{2,3},{3,2},{4,5},{5,4},{6,7},{7,6},{8,9},{9,8},{10,11... | collective-permute-start | bytes 110600 | tf_op jit(solution)/shard_map/ppermute | solution.py:199
  13.6 1.9 copy-start.14
  15.8 0.6 copy-start.15
  16.4 0.6 copy-start.17
  17.0 4.6 %copy-start.19 = (s32[128,6]{0,1:T(8,128)S(1)}, s32[128,6]{0,1:T(8,128)}, u32[]{:S(2)}) copy-start(s32[128,6]{0,1:T(8,128)} %param.31) | copy-start | bytes 9220
  17.0 9.3 %copy-start.11 = (bf16[512,512]{1,0:T(8,128)(2,1)S(1)}, bf16[512,512]{1,0:T(8,128)(2,1)}, u32[]{:S(2)}) copy-start(bf16[512,512]{1,0:T(8,128)(2,1)} %param.28) | copy-start | bytes 1572868
  21.0 41.4 %copy-start.12 = (bf16[2,256,512]{1,2,0:T(8,128)(2,1)S(1)}, bf16[2,256,512]{1,2,0:T(8,128)(2,1)}, u32[]{:S(2)}) copy-start(bf16[2,256,512]{1,2,0:T(8,128)(2,1)} %copy.63) | copy-start | bytes 1572868
  22.5 40.0 %copy-start.16 = (bf16[2,256,64]{1,2,0:T(8,128)(2,1)S(1)}, bf16[2,256,64]{1,2,0:T(8,128)(2,1)}, u32[]{:S(2)}) copy-start(bf16[2,256,64]{1,2,0:T(8,128)(2,1)} %copy-done.15) | copy-start | bytes 196612
  25.5 36.6 %copy-start.25 = (f32[128]{0:T(128)S(1)}, f32[128]{0:T(128)}, u32[]{:S(2)}) copy-start(f32[128]{0:T(128)} %add.143) | copy-start | bytes 1540
  25.5 38.1 %copy-start.23 = (f32[2,256]{1,0:T(2,128)S(1)}, f32[2,256]{1,0:T(2,128)}, u32[]{:S(2)}) copy-start(f32[2,256]{1,0:T(2,128)} %get-tuple-element.32) | copy-start | bytes 6148
  25.6 38.1 %copy-start.18 = (pred[2,1024]{1,0:T(4,128)(4,1)S(1)}, pred[2,1024]{1,0:T(4,128)(4,1)}, u32[]{:S(2)}) copy-start(pred[2,1024]{1,0:T(4,128)(4,1)} %copy-done.17) | copy-start | bytes 6148
  55.4 5.7 %collective-permute-start.3 = (bf16[128,288]{0,1:T(8,128)(2,1)S(1)}, bf16[128,288]{0,1:T(8,128)(2,1)S(1)}, u32[]{:S(2)}, u32[]{:S(2)}) collective-permute-start(bf16[128,288]{0,1:T(8,128)(2,1)S(1)} %maximum_select_fusion.1), channel_id=1, source_target_pairs={{0,2},{1,3},{2,0},{3,1},{4,6},{5,7},{6,4},{7,5},{8,10},{9,11},{10,... | collective-permute-start | bytes 221192 | tf_op jit(solution)/shard_map/ppermute | solution.py:202
  62.5 3.4 %copy-start.1 = (f32[2,256,1024]{2,1,0:T(8,128)S(1)}, f32[2,256,1024]{2,1,0:T(8,128)}, u32[]{:S(2)}) copy-start(f32[2,256,1024]{2,1,0:T(8,128)} %get-tuple-element.33) | copy-start | bytes 6291460
  70.0 3.9 %copy-start.20 = (s32[128,6]{0,1:T(8,128)S(1)}, s32[128,6]{0,1:T(8,128)}, u32[]{:S(2)}) copy-start(s32[128,6]{0,1:T(8,128)} %param.31) | copy-start | bytes 9220
  70.0 3.9 %copy-start.6 = (bf16[128,2048]{1,0:T(8,128)(2,1)S(1)}, bf16[128,2048]{1,0:T(8,128)(2,1)}, u32[]{:S(2)}) copy-start(bf16[128,2048]{1,0:T(8,128)(2,1)} %param.18) | copy-start | bytes 1572868
  72.2 9.0 %copy-start.24 = (f32[2048]{0:T(1024)S(1)}, f32[2048]{0:T(1024)}, u32[]{:S(2)}) copy-start(f32[2048]{0:T(1024)} %param.30) | copy-start | bytes 24580
  72.3 5.4 %collective-permute-start.4 = (bf16[128,1024]{1,0:T(8,128)(2,1)S(1)}, bf16[128,1024]{1,0:T(8,128)(2,1)S(1)}, u32[]{:S(2)}, u32[]{:S(2)}) collective-permute-start(bf16[128,1024]{1,0:T(8,128)(2,1)S(1)} %pad_maximum_fusion.5), channel_id=1, source_target_pairs={{0,1},{1,0},{2,3},{3,2},{4,5},{5,4},{6,7},{7,6},{8,9},{9,8},{10,11... | collective-permute-start | bytes 786440 | tf_op jit(solution)/shard_map/ppermute | solution.py:265
  77.7 15.0 %collective-permute-start.5 = (bf16[128,1024]{1,0:T(8,128)(2,1)S(1)}, bf16[128,1024]{1,0:T(8,128)(2,1)S(1)}, u32[]{:S(2)}, u32[]{:S(2)}) collective-permute-start(bf16[128,1024]{1,0:T(8,128)(2,1)S(1)} %fusion.37), channel_id=1, source_target_pairs={{0,2},{1,3},{2,0},{3,1},{4,6},{5,7},{6,4},{7,5},{8,10},{9,11},{10,... | collective-permute-start | bytes 786440 | tf_op jit(solution)/shard_map/ppermute | solution.py:268
  92.9 2.5 collective-permute-start.6
  159.4 43.3 %copy-start.7 = (bf16[512,704]{0,1:T(8,128)(2,1)S(1)}, bf16[512,704]{0,1:T(8,128)(2,1)}, u32[]{:S(2)}) copy-start(bf16[512,704]{0,1:T(8,128)(2,1)} %get-tuple-element.10) | copy-start | bytes 2162692
  159.4 43.3 %copy-start.8 = (bf16[512,704]{0,1:T(8,128)(2,1)S(1)}, bf16[512,704]{0,1:T(8,128)(2,1)}, u32[]{:S(2)}) copy-start(bf16[512,704]{0,1:T(8,128)(2,1)} %get-tuple-element.13) | copy-start | bytes 2162692
  162.7 40.0 %collective-permute-start.7 = (bf16[64,16,704]{2,1,0:T(8,128)(2,1)S(1)}, bf16[64,16,704]{2,1,0:T(8,128)(2,1)S(1)}, u32[]{:S(2)}, u32[]{:S(2)}) collective-permute-start(bf16[64,16,704]{2,1,0:T(8,128)(2,1)S(1)} %convolution_convert_fusion.1), channel_id=1, source_target_pairs={{0,1},{1,0},{2,3},{3,2},{4,5},{5,4},{6,7},{7,6},{8,9},{9,8},{10,11... | collective-permute-start | bytes 4325384 | tf_op jit(solution)/shard_map/ppermute | solution.py:297
  204.6 1.8 copy-start.2
  204.6 1.8 copy-start.3
  205.1 18.4 %collective-permute-start.8 = (bf16[64,16,352]{2,1,0:T(8,128)(2,1)S(1)}, bf16[64,16,352]{2,1,0:T(8,128)(2,1)S(1)}, u32[]{:S(2)}, u32[]{:S(2)}) collective-permute-start(bf16[64,16,352]{2,1,0:T(8,128)(2,1)S(1)} %fusion.7), channel_id=1, source_target_pairs={{0,1},{1,0},{2,3},{3,2},{4,5},{5,4},{6,7},{7,6},{8,9},{9,8},{10,11... | collective-permute-start | bytes 2162696 | tf_op jit(solution)/shard_map/ppermute | solution.py:301
  227.2 7.1 %copy-start.28 = (s32[2]{0:T(128)S(1)}, s32[2]{0:T(128)}, u32[]{:S(2)}) copy-start(s32[2]{0:T(128)} %param.24) | copy-start | bytes 28
  227.2 7.7 %copy-start.22 = (bf16[128,6]{0,1:T(8,128)(2,1)S(1)}, bf16[128,6]{0,1:T(8,128)(2,1)}, u32[]{:S(2)}) copy-start(bf16[128,6]{0,1:T(8,128)(2,1)} %param.32) | copy-start | bytes 4612
  227.2 39.5 %all-to-all-start.1 = ((bf16[64,16,1024]{2,1,0:T(8,128)(2,1)}), bf16[64,16,1024]{2,1,0:T(8,128)(2,1)}, u32[]{:S(2)}, u32[]{:S(2)}) async-start(bf16[64,16,1024]{2,1,0:T(8,128)(2,1)} %add_convert_fusion), calls=%async_computation.1 | async-start | bytes 4194304 | tf_op jit(solution)/shard_map/all_to_all | solution.py:308
  234.2 57.7 %copy-start.21 = (f32[2,64]{1,0:T(2,128)S(1)}, f32[2,64]{1,0:T(2,128)}, u32[]{:S(2)}) copy-start(f32[2,64]{1,0:T(2,128)} %get-tuple-element.28) | copy-start | bytes 1540
  268.7 29.7 %collective-permute-start.9 = (bf16[128,512]{1,0:T(8,128)(2,1)S(1)}, bf16[128,512]{1,0:T(8,128)(2,1)S(1)}, u32[]{:S(2)}, u32[]{:S(2)}) collective-permute-start(bf16[128,512]{1,0:T(8,128)(2,1)S(1)} %dynamic-slice_convert_fusion), channel_id=1, source_target_pairs={{0,2},{1,3},{2,0},{3,1},{4,6},{5,7},{6,4},{7,5},{8,10},{9,11},{10,... | collective-permute-start | bytes 393224 | tf_op jit(solution)/shard_map/ppermute | solution.py:316

commit v5 on v3

--- a/solution.py
+++ b/solution.py
@@ -225,16 +225,6 @@
         preferred_element_type=jnp.float32,
     ).astype(jnp.bfloat16)
     queries = jnp.concatenate([query_latent, q_pe.reshape(tok_rows, local_heads, ROPE)], -1)
-    q_rows = queries.reshape(local_requests, tree_size * local_heads, -1)
-    mask_rows = jnp.repeat(ancestry > 0, local_heads, axis=1)
-    latent_out = attend_dense(q_rows, kv_cache, lengths, rows_by_request, mask_rows)
-    latent_out = latent_out.reshape(tok_rows, local_heads, LATENT)
-    head_out = jnp.einsum(
-        "thl,lhv->thv",
-        latent_out,
-        w_uv.reshape(LATENT, local_heads, VDIM),
-        preferred_element_type=jnp.float32,
-    ).astype(jnp.bfloat16)
     experts_all = w_gate.shape[0] * lax.axis_size("req")
     top_count = routes.shape[1]
     capacity = 4 * tok_rows * top_count // (3 * experts_all)
@@ -245,23 +235,42 @@
     def half_of(block, which):
         return jnp.concatenate([features(block, which), features(block, which + 2)], -1)
 
-    attention = jnp.dot(
-        head_out.reshape(tok_rows, local_heads * VDIM), o_proj, preferred_element_type=jnp.float32
-    )
-    pair_sum = half_of(attention, parity) + lax.ppermute(
-        half_of(attention, 1 - parity).astype(jnp.bfloat16), "tp", beside
-    ).astype(jnp.float32)
-    attention_half = pair_sum + lax.ppermute(
-        pair_sum.astype(jnp.bfloat16), "tp", across
-    ).astype(jnp.float32)
-    residual_half = half_of(layer_in, parity).astype(jnp.float32) + attention_half
-    half_squares = jnp.sum(residual_half * residual_half, -1, keepdims=True)
-    square_sum = half_squares + lax.ppermute(half_squares, "tp", beside)
-    residual_quarter = features(residual_half, upper)
+    q_rows = queries.reshape(local_requests, tree_size * local_heads, -1)
+    mask_rows = jnp.repeat(ancestry > 0, local_heads, axis=1)
     gain_half = half_of(post_gain, parity)
-    half_rows = (residual_half * lax.rsqrt(square_sum / D + epsilon) * gain_half).astype(
-        jnp.bfloat16
-    )
+    half_parts, quarter_parts = [], []
+    for request in range(local_requests):
+        picked = slice(request, request + 1)
+        tokens = slice(request * tree_size, (request + 1) * tree_size)
+        latent_out = attend_dense(
+            q_rows[picked], kv_cache[picked], lengths[picked], rows_by_request[picked],
+            mask_rows[picked],
+        ).reshape(tree_size, local_heads, LATENT)
+        head_out = jnp.einsum(
+            "thl,lhv->thv",
+            latent_out,
+            w_uv.reshape(LATENT, local_heads, VDIM),
+            preferred_element_type=jnp.float32,
+        ).astype(jnp.bfloat16)
+        attention = jnp.dot(
+            head_out.reshape(tree_size, local_heads * VDIM), o_proj,
+            preferred_element_type=jnp.float32,
+        )
+        pair_sum = half_of(attention, parity) + lax.ppermute(
+            half_of(attention, 1 - parity).astype(jnp.bfloat16), "tp", beside
+        ).astype(jnp.float32)
+        attention_half = pair_sum + lax.ppermute(
+            pair_sum.astype(jnp.bfloat16), "tp", across
+        ).astype(jnp.float32)
+        residual_half = half_of(layer_in[tokens], parity).astype(jnp.float32) + attention_half
+        half_squares = jnp.sum(residual_half * residual_half, -1, keepdims=True)
+        square_sum = half_squares + lax.ppermute(half_squares, "tp", beside)
+        quarter_parts.append(features(residual_half, upper))
+        half_parts.append(
+            (residual_half * lax.rsqrt(square_sum / D + epsilon) * gain_half).astype(jnp.bfloat16)
+        )
+    residual_quarter = jnp.concatenate(quarter_parts, 0)
+    half_rows = jnp.concatenate(half_parts, 0)
     outgoing = lax.dot_general(
         pick_table, half_rows, (((0,), (0,)), ((), ())), preferred_element_type=jnp.float32
     ).astype(jnp.bfloat16)

time: 279 us -> 288 us (1.032)
  starting transfers between devices: 48.7 us -> 66.2 us
  waiting for transfers between devices: 115 us -> 105 us
  blocking collectives: 64.3 us -> 55.1 us
  matrix products: 28.3 us -> 34.5 us
  other arithmetic: 8.78 us -> 12.4 us
    ppermute x1, starting transfers between devices: 5.36 us -> 16 us  [on_device(): partner_rows = lax.ppermute(own_rows, 'tp', beside)]
    all_to_all x1, blocking collectives: 64.3 us -> 55.1 us  [on_device(): lax.all_to_all(outgoing[:, slots], 'req', split_axis=0, concat_axis=0, ti...]
    ppermute x1 -> x2, waiting for transfers between devices: 10.1 us -> 3.18 us  [on_device(): lax.ppermute(pair_sum.astype(jnp.bfloat16), 'tp', across)]
    ppermute x1 -> x2, starting transfers between devices: 1.17 us -> 6.32 us  [on_device(): square_sum = half_squares + lax.ppermute(half_squares, 'tp', beside)]
    dot_general x1 -> x2, matrix products: 4.09 us -> 5.79 us  [attend_dense(): jnp.einsum('rqk,rck->rqc', q_rows, cache, preferred_element_type=jnp.floa...]
  transfers between devices with their start and end apart: 10 -> 13, of which waited for: 8 -> 9; matrix products, arithmetic and copies ran while one was open for 8% -> 11% of each run, Pallas kernels for 0% -> 0%
where the time goes in v5:
time: 288 us
  waiting for transfers between devices  105 us (36%)
  starting transfers between devices  66.2 us (23%)
  blocking collectives  55.1 us (19%)
  matrix products  34.5 us (12%)
  local copies, waits for them, and re-layouts  12.6 us (4%)
  other arithmetic  12.4 us (4%)
    all_to_all x1, blocking collectives, on_device(): lax.all_to_all(outgoing[:, slots], 'req', split_axis=0, concat_axis=0, ti...  55.1 us
    ppermute x1, waiting for transfers between devices, on_device(): partner_rows = lax.ppermute(own_rows, 'tp', beside)  45.4 us
    all_to_all x1, waiting for transfers between devices, on_device(): lax.all_to_all(pair_value, 'req', split_axis=0, concat_axis=0, tiled=True)  29.6 us
    ppermute x1, starting transfers between devices, on_device(): lax.ppermute(give.astype(jnp.bfloat16), 'tp', across).astype(jnp.float32)  23 us
    ppermute x1, starting transfers between devices, on_device(): partner_rows = lax.ppermute(own_rows, 'tp', beside)  16 us
    ppermute x1, waiting for transfers between devices, on_device(): partner_hidden = lax.ppermute(expert_hidden, 'tp', beside)  15.8 us
    all_to_all x1, starting transfers between devices, on_device(): lax.all_to_all(pair_value, 'req', split_axis=0, concat_axis=0, tiled=True)  6.99 us
    ppermute x1, waiting for transfers between devices, on_device(): lax.ppermute(give.astype(jnp.bfloat16), 'tp', across).astype(jnp.float32)  6.43 us
  transfers between devices with their start and end apart: 13, of which 9 were waited for; matrix products, arithmetic and copies ran while one was open for 11% of the time, Pallas kernels for 0%

profile of v5, /device:TPU:1, one launch (start us, length us, event | category | flops | bytes accessed | tf_op | source)
XLA Modules:
  0.0 287.6 jit_solution(15351596834537437893)
XLA Ops:
  0.6 2.3 convolution_convert_fusion.5
  3.0 2.5 collective-permute-start.1
  5.4 2.3 dynamic-slice_bitcast_fusion.1
  7.7 0.9 pad_maximum_fusion
  8.8 0.6 convert_element_type.141
  9.3 0.6 fusion.102
  10.0 1.2 iota_compare_fusion.13
  11.2 1.2 iota_compare_fusion.12
  12.4 0.7 fusion.101
  14.5 0.6 slice_bitcast_fusion.1
  15.5 0.4 fusion.19
  16.1 0.5 fusion
  16.7 0.7 constant_dynamic-slice_fusion.9
  17.3 0.7 constant_dynamic-slice_fusion.4
  18.0 1.4 fusion.11
  19.7 1.0 copy.83
  20.7 1.8 reshape.295
  23.1 0.6 broadcast_add_fusion
  23.7 3.6 %fusion.103 = (f32[256]{0:T(256)}, f32[256,1024]{1,0:T(8,128)}) fusion(bf16[256,576]{1,0:T(8,128)(2,1)S(1)} %reshape.300, bf16[2,1024,576]{1,2,0:T(8,128)(2,1)} %param.21, pred[1024]{0:T(1024)(128)(4,1)S(1)} %copy-done.35), kind=kOutput, calls=%fused_computation.193 | convolution fusion | flops 302776064 | bytes 2525184 | tf_op jit(solution)/shard_map/rqk,rck->rqc/dot_general | solution.py:107
  27.3 2.2 fusion.105
  29.5 0.6 pad_maximum_fusion.5
  30.5 0.9 maximum_select_fusion.2
  31.4 3.1 %collective-permute-start.2 = (bf16[128,288]{0,1:T(8,128)(2,1)S(1)}, bf16[128,288]{0,1:T(8,128)(2,1)S(1)}, u32[]{:S(2)}, u32[]{:S(2)}) collective-permute-start(bf16[128,288]{0,1:T(8,128)(2,1)S(1)} %maximum_select_fusion.2), channel_id=1, source_target_pairs={{0,2},{1,3},{2,0},{3,1},{4,6},{5,7},{6,4},{7,5},{8,10},{9,11},{10,... | collective-permute-start | bytes 221192 | tf_op jit(solution)/shard_map/ppermute | solution.py:202
  34.4 1.7 collective-permute-done.2
  36.7 1.3 fusion.104
  38.0 0.7 max.19
  39.0 2.0 fusion.12
  41.3 0.9 fusion.28
  42.2 1.4 fusion.15
  44.3 0.7 fusion.73
  45.0 0.9 fusion.9
  45.9 0.7 add.187
  46.8 1.3 fusion.21
  48.1 1.3 fusion.20
  49.4 0.5 fusion.68
  49.9 0.5 fusion.65
  50.5 1.6 collective-permute-start.3
  52.3 2.2 collective-permute-done.3
  54.5 3.1 %collective-permute-start.4 = (bf16[64,1024]{1,0:T(8,128)(2,1)S(1)}, bf16[64,1024]{1,0:T(8,128)(2,1)S(1)}, u32[]{:S(2)}, u32[]{:S(2)}) collective-permute-start(bf16[64,1024]{1,0:T(8,128)(2,1)S(1)} %fusion.57), channel_id=1, source_target_pairs={{0,2},{1,3},{2,0},{3,1},{4,6},{5,7},{6,4},{7,5},{8,10},{9,11},{10,... | collective-permute-start | bytes 393224 | tf_op jit(solution)/shard_map/ppermute | solution.py:262
  57.6 2.1 collective-permute-start.6
  59.8 0.5 collective-permute-done.4
  60.4 3.5 %collective-permute-start.7 = (f32[64,1]{0,1:T(1,128)S(1)}, f32[64,1]{0,1:T(1,128)S(1)}, u32[]{:S(2)}, u32[]{:S(2)}) collective-permute-start(f32[64,1]{0,1:T(1,128)S(1)} %bitcast.133), channel_id=1, source_target_pairs={{0,1},{1,0},{2,3},{3,2},{4,5},{5,4},{6,7},{7,6},{8,9},{9,8},{10,11... | collective-permute-start | bytes 776 | tf_op jit(solution)/shard_map/ppermute | solution.py:267
  63.9 2.7 collective-permute-done.6
  66.7 2.9 collective-permute-start.8
  69.6 0.9 collective-permute-done.8
  70.7 0.8 convolution_convert_fusion
  71.5 55.1 %all_to_all.10 = bf16[64,16,1024]{2,1,0:T(8,128)(2,1)S(1)} all-to-all(bf16[64,16,1024]{2,1,0:T(8,128)(2,1)S(1)} %bitcast.127), channel_id=1, replica_groups=mesh['req'=64,'tp'=4] {'req'}, dimensions={0} | all-to-all | bytes 4194304 | tf_op jit(solution)/shard_map/all_to_all | solution.py:285
  126.5 16.0 %collective-permute-start.9 = (bf16[64,16,1024]{2,1,0:T(8,128)(2,1)S(1)}, bf16[64,16,1024]{2,1,0:T(8,128)(2,1)S(1)}, u32[]{:S(2)}, u32[]{:S(2)}) collective-permute-start(bf16[64,16,1024]{2,1,0:T(8,128)(2,1)S(1)} %all_to_all.10), channel_id=1, source_target_pairs={{0,1},{1,0},{2,3},{3,2},{4,5},{5,4},{6,7},{7,6},{8,9},{9,8},{10,11... | collective-permute-start | bytes 6291464 | tf_op jit(solution)/shard_map/ppermute | solution.py:286
  142.9 45.4 %collective-permute-done.9 = bf16[64,16,1024]{2,1,0:T(8,128)(2,1)S(1)} collective-permute-done((bf16[64,16,1024]{2,1,0:T(8,128)(2,1)S(1)}, bf16[64,16,1024]{2,1,0:T(8,128)(2,1)S(1)}, u32[]{:S(2)}, u32[]{:S(2)}) %collective-permute-start.9) | collective-permute-done | bytes 2097184 | tf_op jit(solution)/shard_map/ppermute | solution.py:286
  188.6 2.3 fusion.5
  191.0 2.6 multiply_convert_fusion
  193.6 1.3 collective-permute-start.10
  194.9 1.2 fusion.32
  196.1 15.8 %collective-permute-done.10 = bf16[64,16,352]{2,1,0:T(8,128)(2,1)S(1)} collective-permute-done((bf16[64,16,352]{2,1,0:T(8,128)(2,1)S(1)}, bf16[64,16,352]{2,1,0:T(8,128)(2,1)S(1)}, u32[]{:S(2)}, u32[]{:S(2)}) %collective-permute-start.10) | collective-permute-done | bytes 720928 | tf_op jit(solution)/shard_map/ppermute | solution.py:297
  211.9 3.7 %add_convert_fusion = bf16[64,16,1024]{2,1,0:T(8,128)(2,1)} fusion(f32[64,16,1024]{2,1,0:T(8,128)S(1)} %fusion.32, bf16[64,16,352]{2,1,0:T(8,128)(2,1)S(1)} %collective-permute-done.10, bf16[352,1024]{1,0:T(8,128)(2,1)} %collective-permute-done), kind=kOutput, calls=%fused_computation.2 | convolution fusion | flops 740294656 | bytes 7733248 | tf_op jit(solution)/shard_map/sch,hf->scf/dot_general | solution.py:300
  215.7 7.0 %all-to-all-start.1 = ((bf16[64,16,1024]{2,1,0:T(8,128)(2,1)}), bf16[64,16,1024]{2,1,0:T(8,128)(2,1)}, u32[]{:S(2)}, u32[]{:S(2)}) async-start(bf16[64,16,1024]{2,1,0:T(8,128)(2,1)} %add_convert_fusion), calls=%async_computation.1 | async-start | bytes 4194304 | tf_op jit(solution)/shard_map/all_to_all | solution.py:304
  222.7 1.4 gather_fusion
  224.2 0.4 fusion.3
  224.8 0.9 convolution_convert_fusion.2
  225.7 29.6 %all-to-all-done.1 = bf16[64,16,1024]{2,1,0:T(8,128)(2,1)} async-done(((bf16[64,16,1024]{2,1,0:T(8,128)(2,1)}), bf16[64,16,1024]{2,1,0:T(8,128)(2,1)}, u32[]{:S(2)}, u32[]{:S(2)}) %all-to-all-start.1) | async-done | bytes 2097184 | tf_op jit(solution)/shard_map/all_to_all | solution.py:304
  255.3 2.0 fusion.107
  257.3 23.0 %collective-permute-start.11 = (bf16[128,512]{1,0:T(8,128)(2,1)S(1)}, bf16[128,512]{1,0:T(8,128)(2,1)S(1)}, u32[]{:S(2)}, u32[]{:S(2)}) collective-permute-start(bf16[128,512]{1,0:T(8,128)(2,1)S(1)} %dynamic-slice_convert_fusion), channel_id=1, source_target_pairs={{0,2},{1,3},{2,0},{3,1},{4,6},{5,7},{6,4},{7,5},{8,10},{9,11},{10,... | collective-permute-start | bytes 393224 | tf_op jit(solution)/shard_map/ppermute | solution.py:312
  280.4 6.4 %collective-permute-done.11 = bf16[128,512]{1,0:T(8,128)(2,1)S(1)} collective-permute-done((bf16[128,512]{1,0:T(8,128)(2,1)S(1)}, bf16[128,512]{1,0:T(8,128)(2,1)S(1)}, u32[]{:S(2)}, u32[]{:S(2)}) %collective-permute-start.11) | collective-permute-done | bytes 131104 | tf_op jit(solution)/shard_map/ppermute | solution.py:312
  286.8 0.7 fusion.49
  (144 shorter events, 6.8 us)
Async XLA Ops:
  0.6 48.7 %copy-start = (bf16[512,2048]{1,0:T(8,128)(2,1)S(1)}, bf16[512,2048]{1,0:T(8,128)(2,1)}, u32[]{:S(2)}) copy-start(bf16[512,2048]{1,0:T(8,128)(2,1)} %param.29) | copy-start | bytes 6291460
  3.0 5.8 %copy-start.27 = (s32[2]{0:T(128)S(1)}, s32[2]{0:T(128)}, u32[]{:S(2)}) copy-start(s32[2]{0:T(128)} %param.22) | copy-start | bytes 28
  3.0 7.0 %copy-start.5 = (bf16[128,2048]{1,0:T(8,128)(2,1)S(1)}, bf16[128,2048]{1,0:T(8,128)(2,1)}, u32[]{:S(2)}) copy-start(bf16[128,2048]{1,0:T(8,128)(2,1)} %param.18) | copy-start | bytes 1572868
  3.0 27.5 %collective-permute-start.1 = (bf16[128,144]{0,1:T(8,128)(2,1)}, bf16[128,144]{0,1:T(8,128)(2,1)}, u32[]{:S(2)}, u32[]{:S(2)}) collective-permute-start(bf16[128,144]{0,1:T(8,128)(2,1)} %convolution_convert_fusion.5), channel_id=1, source_target_pairs={{0,1},{1,0},{2,3},{3,2},{4,5},{5,4},{6,7},{7,6},{8,9},{9,8},{10,11... | collective-permute-start | bytes 110600 | tf_op jit(solution)/shard_map/ppermute | solution.py:199
  5.4 7.0 %copy-start.26 = (f32[2048]{0:T(1024)S(1)}, f32[2048]{0:T(1024)}, u32[]{:S(2)}) copy-start(f32[2048]{0:T(1024)} %param.30) | copy-start | bytes 24580
  5.4 7.7 %copy-start.32 = (s32[2,64]{1,0:T(2,128)S(1)}, s32[2,64]{1,0:T(2,128)}, u32[]{:S(2)}) copy-start(s32[2,64]{1,0:T(2,128)} %param.23) | copy-start | bytes 1540
  7.7 7.5 %copy-start.15 = (bf16[128,256]{1,0:T(8,128)(2,1)S(1)}, bf16[128,256]{1,0:T(8,128)(2,1)}, u32[]{:S(2)}) copy-start(bf16[128,256]{1,0:T(8,128)(2,1)} %param.20) | copy-start | bytes 196612
  7.7 7.6 %copy-start.21 = (s32[128,6]{0,1:T(8,128)S(1)}, s32[128,6]{0,1:T(8,128)}, u32[]{:S(2)}) copy-start(s32[128,6]{0,1:T(8,128)} %param.31) | copy-start | bytes 9220
  8.7 27.6 %collective-permute-start = (bf16[352,1024]{1,0:T(8,128)(2,1)}, bf16[352,1024]{1,0:T(8,128)(2,1)}, u32[]{:S(2)}, u32[]{:S(2)}) collective-permute-start(bf16[352,1024]{1,0:T(8,128)(2,1)} %pad_maximum_fusion), channel_id=1, source_target_pairs={{0,1},{1,0},{2,3},{3,2},{4,5},{5,4},{6,7},{7,6},{8,9},{9,8},{10,11... | collective-permute-start | bytes 2162696 | tf_op jit(solution)/shard_map/ppermute | solution.py:213
  14.5 8.4 %copy-start.10 = (f32[2,64,64]{2,1,0:T(8,128)}, f32[2,64,64]{2,1,0:T(8,128)S(1)}, u32[]{:S(2)}) copy-start(f32[2,64,64]{2,1,0:T(8,128)S(1)} %get-tuple-element.49) | copy-start | bytes 98308
  16.1 6.4 %copy-start.16 = (s32[128,6]{0,1:T(8,128)}, s32[128,6]{0,1:T(8,128)S(1)}, u32[]{:S(2)}) copy-start(s32[128,6]{0,1:T(8,128)S(1)} %multiply_add_fusion) | copy-start | bytes 9220
  19.6 3.4 %copy-start.29 = (f32[2]{0:T(128)S(1)}, f32[2]{0:T(128)}, u32[]{:S(2)}) copy-start(f32[2]{0:T(128)} %convert_element_type.141) | copy-start | bytes 28
  19.6 4.0 %copy-start.35 = (pred[1024]{0:T(1024)(128)(4,1)S(1)}, pred[1024]{0:T(1024)(128)(4,1)}, u32[]{:S(2)}) copy-start(pred[1024]{0:T(1024)(128)(4,1)} %iota_compare_fusion.12) | copy-start | bytes 3076
  22.5 4.7 %copy-start.34 = (pred[1024]{0:T(1024)(128)(4,1)S(1)}, pred[1024]{0:T(1024)(128)(4,1)}, u32[]{:S(2)}) copy-start(pred[1024]{0:T(1024)(128)(4,1)} %iota_compare_fusion.13) | copy-start | bytes 3076
  23.0 0.7 copy-start.9
  23.1 4.2 %copy-start.2 = (bf16[2,1024,576]{1,2,0:T(8,128)(2,1)S(1)}, bf16[2,1024,576]{1,2,0:T(8,128)(2,1)}, u32[]{:S(2)}) copy-start(bf16[2,1024,576]{1,2,0:T(8,128)(2,1)} %param.21) | copy-start | bytes 7077892
  27.2 2.2 copy-start.22
  27.2 2.9 %copy-start.18 = (pred[64,64]{1,0:T(8,128)(4,1)S(1)}, pred[64,64]{1,0:T(8,128)(4,1)}, u32[]{:S(2)}) copy-start(pred[64,64]{1,0:T(8,128)(4,1)} %get-tuple-element.36) | copy-start | bytes 12292
  27.3 9.1 %copy-start.24 = (f32[512]{0:T(512)S(1)}, f32[512]{0:T(512)}, u32[]{:S(2)}) copy-start(f32[512]{0:T(512)} %param.26) | copy-start | bytes 6148
  30.2 8.5 %copy-start.1 = (f32[256,1024]{1,0:T(8,128)S(1)}, f32[256,1024]{1,0:T(8,128)}, u32[]{:S(2)}) copy-start(f32[256,1024]{1,0:T(8,128)} %get-tuple-element.47) | copy-start | bytes 3145732
  31.4 4.8 %collective-permute-start.2 = (bf16[128,288]{0,1:T(8,128)(2,1)S(1)}, bf16[128,288]{0,1:T(8,128)(2,1)S(1)}, u32[]{:S(2)}, u32[]{:S(2)}) collective-permute-start(bf16[128,288]{0,1:T(8,128)(2,1)S(1)} %maximum_select_fusion.2), channel_id=1, source_target_pairs={{0,2},{1,3},{2,0},{3,1},{4,6},{5,7},{6,4},{7,5},{8,10},{9,11},{10,... | collective-permute-start | bytes 221192 | tf_op jit(solution)/shard_map/ppermute | solution.py:202
  36.6 4.4 %copy-start.8 = (bf16[256,576]{1,0:T(8,128)(2,1)S(1)}, bf16[256,576]{1,0:T(8,128)(2,1)}, u32[]{:S(2)}) copy-start(bf16[256,576]{1,0:T(8,128)(2,1)} %reshape.295) | copy-start | bytes 884740
  38.0 3.3 %copy-start.28 = (f32[256]{0:T(256)S(1)}, f32[256]{0:T(256)}, u32[]{:S(2)}) copy-start(f32[256]{0:T(256)} %get-tuple-element.52) | copy-start | bytes 3076
  39.0 3.2 %copy-start.3 = (bf16[2,1024,576]{1,2,0:T(8,128)(2,1)S(1)}, bf16[2,1024,576]{1,2,0:T(8,128)(2,1)}, u32[]{:S(2)}) copy-start(bf16[2,1024,576]{1,2,0:T(8,128)(2,1)} %param.21) | copy-start | bytes 7077892
  41.3 2.7 copy-start.19
  43.7 1.3 copy-start.4
  49.9 10.4 %copy-start.13 = (bf16[64,512]{1,0:T(8,128)(2,1)S(1)}, bf16[64,512]{1,0:T(8,128)(2,1)}, u32[]{:S(2)}) copy-start(bf16[64,512]{1,0:T(8,128)(2,1)} %get-tuple-element.30) | copy-start | bytes 196612
  49.9 10.3 %copy-start.14 = (bf16[64,512]{1,0:T(8,128)(2,1)S(1)}, bf16[64,512]{1,0:T(8,128)(2,1)}, u32[]{:S(2)}) copy-start(bf16[64,512]{1,0:T(8,128)(2,1)} %get-tuple-element.31) | copy-start | bytes 196612
  50.4 16.2 %copy-start.11 = (bf16[64,512]{1,0:T(8,128)(2,1)S(1)}, bf16[64,512]{1,0:T(8,128)(2,1)}, u32[]{:S(2)}) copy-start(bf16[64,512]{1,0:T(8,128)(2,1)} %get-tuple-element.32) | copy-start | bytes 196612
  50.4 16.2 %copy-start.12 = (bf16[64,512]{1,0:T(8,128)(2,1)S(1)}, bf16[64,512]{1,0:T(8,128)(2,1)}, u32[]{:S(2)}) copy-start(bf16[64,512]{1,0:T(8,128)(2,1)} %get-tuple-element.33) | copy-start | bytes 196612
  50.4 20.1 %copy-start.20 = (f32[1024]{0:T(1024)S(1)}, f32[1024]{0:T(1024)}, u32[]{:S(2)}) copy-start(f32[1024]{0:T(1024)} %pad_maximum_fusion.5) | copy-start | bytes 12292
  50.5 4.0 %collective-permute-start.3 = (bf16[64,1024]{1,0:T(8,128)(2,1)S(1)}, bf16[64,1024]{1,0:T(8,128)(2,1)S(1)}, u32[]{:S(2)}, u32[]{:S(2)}) collective-permute-start(bf16[64,1024]{1,0:T(8,128)(2,1)S(1)} %pad_maximum_fusion.3), channel_id=1, source_target_pairs={{0,1},{1,0},{2,3},{3,2},{4,5},{5,4},{6,7},{7,6},{8,9},{9,8},{10,11... | collective-permute-start | bytes 393224 | tf_op jit(solution)/shard_map/ppermute | solution.py:259
  52.1 5.5 %collective-permute-start.5 = (bf16[64,1024]{1,0:T(8,128)(2,1)S(1)}, bf16[64,1024]{1,0:T(8,128)(2,1)S(1)}, u32[]{:S(2)}, u32[]{:S(2)}) collective-permute-start(bf16[64,1024]{1,0:T(8,128)(2,1)S(1)} %pad_maximum_fusion.4), channel_id=1, source_target_pairs={{0,1},{1,0},{2,3},{3,2},{4,5},{5,4},{6,7},{7,6},{8,9},{9,8},{10,11... | collective-permute-start | bytes 393224 | tf_op jit(solution)/shard_map/ppermute | solution.py:259
  54.5 5.7 %collective-permute-start.4 = (bf16[64,1024]{1,0:T(8,128)(2,1)S(1)}, bf16[64,1024]{1,0:T(8,128)(2,1)S(1)}, u32[]{:S(2)}, u32[]{:S(2)}) collective-permute-start(bf16[64,1024]{1,0:T(8,128)(2,1)S(1)} %fusion.57), channel_id=1, source_target_pairs={{0,2},{1,3},{2,0},{3,1},{4,6},{5,7},{6,4},{7,5},{8,10},{9,11},{10,... | collective-permute-start | bytes 393224 | tf_op jit(solution)/shard_map/ppermute | solution.py:262
  57.6 9.0 %collective-permute-start.6 = (bf16[64,1024]{1,0:T(8,128)(2,1)S(1)}, bf16[64,1024]{1,0:T(8,128)(2,1)S(1)}, u32[]{:S(2)}, u32[]{:S(2)}) collective-permute-start(bf16[64,1024]{1,0:T(8,128)(2,1)S(1)} %fusion.56), channel_id=1, source_target_pairs={{0,2},{1,3},{2,0},{3,1},{4,6},{5,7},{6,4},{7,5},{8,10},{9,11},{10,... | collective-permute-start | bytes 393224 | tf_op jit(solution)/shard_map/ppermute | solution.py:262
  60.4 9.2 %collective-permute-start.7 = (f32[64,1]{0,1:T(1,128)S(1)}, f32[64,1]{0,1:T(1,128)S(1)}, u32[]{:S(2)}, u32[]{:S(2)}) collective-permute-start(f32[64,1]{0,1:T(1,128)S(1)} %bitcast.133), channel_id=1, source_target_pairs={{0,1},{1,0},{2,3},{3,2},{4,5},{5,4},{6,7},{7,6},{8,9},{9,8},{10,11... | collective-permute-start | bytes 776 | tf_op jit(solution)/shard_map/ppermute | solution.py:267
  66.7 3.8 %collective-permute-start.8 = (f32[64,1]{0,1:T(1,128)S(1)}, f32[64,1]{0,1:T(1,128)S(1)}, u32[]{:S(2)}, u32[]{:S(2)}) collective-permute-start(f32[64,1]{0,1:T(1,128)S(1)} %bitcast.134), channel_id=1, source_target_pairs={{0,1},{1,0},{2,3},{3,2},{4,5},{5,4},{6,7},{7,6},{8,9},{9,8},{10,11... | collective-permute-start | bytes 776 | tf_op jit(solution)/shard_map/ppermute | solution.py:267
  126.5 61.8 %collective-permute-start.9 = (bf16[64,16,1024]{2,1,0:T(8,128)(2,1)S(1)}, bf16[64,16,1024]{2,1,0:T(8,128)(2,1)S(1)}, u32[]{:S(2)}, u32[]{:S(2)}) collective-permute-start(bf16[64,16,1024]{2,1,0:T(8,128)(2,1)S(1)} %all_to_all.10), channel_id=1, source_target_pairs={{0,1},{1,0},{2,3},{3,2},{4,5},{5,4},{6,7},{7,6},{8,9},{9,8},{10,11... | collective-permute-start | bytes 6291464 | tf_op jit(solution)/shard_map/ppermute | solution.py:286
  142.9 45.7 %copy-start.30 = (bf16[1,2048,352]{1,2,0:T(8,128)(2,1)S(1)}, bf16[1,2048,352]{1,2,0:T(8,128)(2,1)}, u32[]{:S(2)}) copy-start(bf16[1,2048,352]{1,2,0:T(8,128)(2,1)} %param.33) | copy-start | bytes 4325380
  188.6 2.4 copy-start.31
  191.0 3.9 %copy-start.6 = (bf16[352,512]{1,0:T(8,128)(2,1)S(1)}, bf16[352,512]{1,0:T(8,128)(2,1)}, u32[]{:S(2)}) copy-start(bf16[352,512]{1,0:T(8,128)(2,1)} %get-tuple-element.14) | copy-start | bytes 1081348
  191.0 3.9 %copy-start.7 = (bf16[352,512]{1,0:T(8,128)(2,1)S(1)}, bf16[352,512]{1,0:T(8,128)(2,1)}, u32[]{:S(2)}) copy-start(bf16[352,512]{1,0:T(8,128)(2,1)} %get-tuple-element.17) | copy-start | bytes 1081348
  193.6 18.3 %collective-permute-start.10 = (bf16[64,16,352]{2,1,0:T(8,128)(2,1)S(1)}, bf16[64,16,352]{2,1,0:T(8,128)(2,1)S(1)}, u32[]{:S(2)}, u32[]{:S(2)}) collective-permute-start(bf16[64,16,352]{2,1,0:T(8,128)(2,1)S(1)} %multiply_convert_fusion), channel_id=1, source_target_pairs={{0,1},{1,0},{2,3},{3,2},{4,5},{5,4},{6,7},{7,6},{8,9},{9,8},{10,11... | collective-permute-start | bytes 2162696 | tf_op jit(solution)/shard_map/ppermute | solution.py:297
  215.7 7.0 %copy-start.33 = (s32[2]{0:T(128)S(1)}, s32[2]{0:T(128)}, u32[]{:S(2)}) copy-start(s32[2]{0:T(128)} %param.24) | copy-start | bytes 28
  215.7 8.5 %copy-start.17 = (s32[128,6]{0,1:T(8,128)S(1)}, s32[128,6]{0,1:T(8,128)}, u32[]{:S(2)}) copy-start(s32[128,6]{0,1:T(8,128)} %copy-done.16) | copy-start | bytes 9220
  215.7 8.5 %copy-start.25 = (bf16[128,6]{0,1:T(8,128)(2,1)S(1)}, bf16[128,6]{0,1:T(8,128)(2,1)}, u32[]{:S(2)}) copy-start(bf16[128,6]{0,1:T(8,128)(2,1)} %param.32) | copy-start | bytes 4612
  215.7 9.2 %copy-start.23 = (f32[2,64]{1,0:T(2,128)S(1)}, f32[2,64]{1,0:T(2,128)}, u32[]{:S(2)}) copy-start(f32[2,64]{1,0:T(2,128)} %get-tuple-element.42) | copy-start | bytes 1540
  215.7 39.6 %all-to-all-start.1 = ((bf16[64,16,1024]{2,1,0:T(8,128)(2,1)}), bf16[64,16,1024]{2,1,0:T(8,128)(2,1)}, u32[]{:S(2)}, u32[]{:S(2)}) async-start(bf16[64,16,1024]{2,1,0:T(8,128)(2,1)} %add_convert_fusion), calls=%async_computation.1 | async-start | bytes 4194304 | tf_op jit(solution)/shard_map/all_to_all | solution.py:304
  257.3 29.5 %collective-permute-start.11 = (bf16[128,512]{1,0:T(8,128)(2,1)S(1)}, bf16[128,512]{1,0:T(8,128)(2,1)S(1)}, u32[]{:S(2)}, u32[]{:S(2)}) collective-permute-start(bf16[128,512]{1,0:T(8,128)(2,1)S(1)} %dynamic-slice_convert_fusion), channel_id=1, source_target_pairs={{0,2},{1,3},{2,0},{3,1},{4,6},{5,7},{6,4},{7,5},{8,10},{9,11},{10,... | collective-permute-start | bytes 393224 | tf_op jit(solution)/shard_map/ppermute | solution.py:312

commit v6 on v3

--- a/solution.py
+++ b/solution.py
@@ -267,6 +267,15 @@
     ).astype(jnp.bfloat16)
     outgoing = outgoing.reshape(experts_all, capacity, 2 * quarter)
 
+    def feature_rows(weight, which):
+        return jnp.concatenate(
+            [
+                lax.dynamic_slice_in_dim(weight, which * quarter, quarter, 0),
+                lax.dynamic_slice_in_dim(weight, (which + 2) * quarter, quarter, 0),
+            ],
+            0,
+        )
+
     chunks = 1
     slot_step = capacity // chunks
     weights_by_slot = weights.reshape(tok_rows, experts_all, capacity)
@@ -275,15 +284,20 @@
         slots = slice(chunk * slot_step, (chunk + 1) * slot_step)
         own_rows = lax.all_to_all(outgoing[:, slots], "req", split_axis=0, concat_axis=0, tiled=True)
         partner_rows = lax.ppermute(own_rows, "tp", beside)
-        low_own, high_own = own_rows[..., :quarter], own_rows[..., quarter:]
-        low_partner, high_partner = partner_rows[..., :quarter], partner_rows[..., quarter:]
-        row_set = jnp.where(
-            parity == 0,
-            jnp.concatenate([low_own, low_partner, high_own, high_partner], -1),
-            jnp.concatenate([low_partner, low_own, high_partner, high_own], -1),
-        )
-        gate_act = jnp.einsum("scf,fh->sch", row_set, w_gate[0], preferred_element_type=jnp.float32)
-        up_act = jnp.einsum("scf,fh->sch", row_set, w_up[0], preferred_element_type=jnp.float32)
+        gate_act = jnp.einsum(
+            "scf,fh->sch", own_rows, feature_rows(w_gate[0], parity),
+            preferred_element_type=jnp.float32,
+        ) + jnp.einsum(
+            "scf,fh->sch", partner_rows, feature_rows(w_gate[0], 1 - parity),
+            preferred_element_type=jnp.float32,
+        )
+        up_act = jnp.einsum(
+            "scf,fh->sch", own_rows, feature_rows(w_up[0], parity),
+            preferred_element_type=jnp.float32,
+        ) + jnp.einsum(
+            "scf,fh->sch", partner_rows, feature_rows(w_up[0], 1 - parity),
+            preferred_element_type=jnp.float32,
+        )
         expert_hidden = (jax.nn.silu(gate_act) * up_act).astype(jnp.bfloat16)
         partner_hidden = lax.ppermute(expert_hidden, "tp", beside)
         pair_value = (

time: 279 us -> 276 us (0.989)
  transfers between devices with their start and end apart: 10 -> 10, of which waited for: 8 -> 9; matrix products, arithmetic and copies ran while one was open for 8% -> 8% of each run, Pallas kernels for 0% -> 0%
where the time goes in v6:
time: 276 us; the launch traced here: 275 us
  waiting for transfers between devices  115 us (42%)
  blocking collectives  63.7 us (23%)
  starting transfers between devices  48.9 us (18%)
  matrix products  28.8 us (10%)
  local copies, waits for them, and re-layouts  10.8 us (4%)
  other arithmetic  7.1 us (3%)
    all_to_all x1, blocking collectives, on_device(): lax.all_to_all(outgoing[:, slots], 'req', split_axis=0, concat_axis=0, ti...  63.7 us
    ppermute x1, waiting for transfers between devices, on_device(): partner_rows = lax.ppermute(own_rows, 'tp', beside)  42.9 us
    all_to_all x1, waiting for transfers between devices, on_device(): lax.all_to_all(pair_value, 'req', split_axis=0, concat_axis=0, tiled=True)  31.3 us
    ppermute x1, starting transfers between devices, on_device(): lax.ppermute(give.astype(jnp.bfloat16), 'tp', across).astype(jnp.float32)  23.2 us
    ppermute x1, waiting for transfers between devices, on_device(): partner_hidden = lax.ppermute(expert_hidden, 'tp', beside)  15.8 us
    ppermute x1, waiting for transfers between devices, on_device(): lax.ppermute(pair_sum.astype(jnp.bfloat16), 'tp', across)  10.8 us
    all_to_all x1, starting transfers between devices, on_device(): lax.all_to_all(pair_value, 'req', split_axis=0, concat_axis=0, tiled=True)  7.06 us
    ppermute x1, waiting for transfers between devices, on_device(): lax.ppermute(give.astype(jnp.bfloat16), 'tp', across).astype(jnp.float32)  5.58 us
  transfers between devices with their start and end apart: 10, of which 9 were waited for; matrix products, arithmetic and copies ran while one was open for 8% of the time, Pallas kernels for 0%

profile of v6, /device:TPU:1, one launch (start us, length us, event | category | flops | bytes accessed | tf_op | source)
XLA Modules:
  0.0 275.0 jit_solution(11299403419343758172)
XLA Ops:
  0.7 2.5 dynamic-slice_bitcast_fusion.1
  3.2 1.0 pad_maximum_fusion
  4.2 2.5 collective-permute-start
  6.6 0.9 convolution_convert_fusion.4
  7.7 0.2 convolution_minimum_fusion.6
  7.9 0.2 convolution_minimum_fusion.5
  8.1 0.2 convolution_minimum_fusion.4
  8.7 0.2 convolution_minimum_fusion.1
  8.9 0.3 fusion.78
  9.4 0.3 fusion.7
  9.7 0.4 copy.62
  10.3 1.0 copy.63
  11.3 4.1 %fusion.3 = (f32[2,256]{1,0:T(2,128)}, f32[2,256,1024]{2,1,0:T(8,128)}) fusion(pred[2,1024]{1,0:T(4,128)(4,1)S(1)} %iota_compare_fusion.12, bf16[2,1024,576]{1,2,0:T(8,128)(2,1)S(1)} %copy-done, bf16[2,256,64]{1,2,0:T(8,128)(2,1)S(1)} %copy.64, bf16[2,256,512]{1,2,0:T(8,128)(2,1)} %copy.63), kind=kOutput, calls=%fused_computation.10 | convolution fusion | flops 606731776 | bytes 5050368 | tf_op jit(solution)/shard_map/rqk,rck->rqc/dot_general | solution.py:107
  15.4 0.6 broadcast_add_fusion
  16.1 0.7 eq.88
  16.8 1.1 fusion.10
  18.0 0.6 convert_element_type.117
  18.6 0.8 convert_element_type.118
  19.4 0.7 copy.72
  20.1 1.0 copy.75
  21.1 0.7 add.152
  22.0 0.5 collective-permute-done.1
  22.5 0.9 maximum_select_fusion.1
  23.4 4.0 %collective-permute-start.2 = (bf16[128,288]{0,1:T(8,128)(2,1)S(1)}, bf16[128,288]{0,1:T(8,128)(2,1)S(1)}, u32[]{:S(2)}, u32[]{:S(2)}) collective-permute-start(bf16[128,288]{0,1:T(8,128)(2,1)S(1)} %maximum_select_fusion.1), channel_id=1, source_target_pairs={{0,2},{1,3},{2,0},{3,1},{4,6},{5,7},{6,4},{7,5},{8,10},{9,11},{10,... | collective-permute-start | bytes 221192 | tf_op jit(solution)/shard_map/ppermute | solution.py:202
  27.4 1.7 collective-permute-done.2
  29.3 0.8 fusion.39
  30.5 0.2 fusion.79
  30.8 2.8 %fusion.11 = f32[2,256,576]{2,1,0:T(8,128)S(1)} fusion(bf16[2,1024,576]{1,2,0:T(8,128)(2,1)S(1)} %copy-done, f32[2,256,1024]{2,1,0:T(8,128)} %get-tuple-element.35, f32[2,256]{1,0:T(2,128)S(1)} %max.7, pred[2,1024]{1,0:T(4,128)(4,1)S(1)} %copy-done.17), kind=kOutput, calls=%fused_computation.31 | convolution fusion | flops 606076928 | bytes 5640192 | tf_op jit(solution)/shard_map/rqc,rck->rqk/dot_general | solution.py:120
  33.6 0.6 fusion.4
  34.1 0.4 fusion.48
  34.6 0.2 fusion.14
  34.8 0.9 reshape.167
  35.7 1.5 convolution_convert_fusion.3
  37.3 2.1 fusion.80
  39.5 1.6 collective-permute-start.3
  41.2 3.7 %collective-permute-done.3 = bf16[128,1024]{1,0:T(8,128)(2,1)S(1)} collective-permute-done((bf16[128,1024]{1,0:T(8,128)(2,1)S(1)}, bf16[128,1024]{1,0:T(8,128)(2,1)S(1)}, u32[]{:S(2)}, u32[]{:S(2)}) %collective-permute-start.3) | collective-permute-done | bytes 262176 | tf_op jit(solution)/shard_map/ppermute | solution.py:251
  44.9 3.3 %collective-permute-start.4 = (bf16[128,1024]{1,0:T(8,128)(2,1)S(1)}, bf16[128,1024]{1,0:T(8,128)(2,1)S(1)}, u32[]{:S(2)}, u32[]{:S(2)}) collective-permute-start(bf16[128,1024]{1,0:T(8,128)(2,1)S(1)} %fusion.36), channel_id=1, source_target_pairs={{0,2},{1,3},{2,0},{3,1},{4,6},{5,7},{6,4},{7,5},{8,10},{9,11},{10,... | collective-permute-start | bytes 786440 | tf_op jit(solution)/shard_map/ppermute | solution.py:254
  48.3 0.5 fusion
  48.8 10.8 %collective-permute-done.4 = bf16[128,1024]{1,0:T(8,128)(2,1)S(1)} collective-permute-done((bf16[128,1024]{1,0:T(8,128)(2,1)S(1)}, bf16[128,1024]{1,0:T(8,128)(2,1)S(1)}, u32[]{:S(2)}, u32[]{:S(2)}) %collective-permute-start.4) | collective-permute-done | bytes 262176 | tf_op jit(solution)/shard_map/ppermute | solution.py:254
  59.6 0.2 multiply_reduce_fusion
  59.8 0.5 collective-permute-start.5
  60.3 2.2 collective-permute-done.5
  62.5 0.8 convolution_convert_fusion
  63.3 63.7 %all_to_all.10 = bf16[64,16,1024]{2,1,0:T(8,128)(2,1)S(1)} all-to-all(bf16[64,16,1024]{2,1,0:T(8,128)(2,1)S(1)} %bitcast.102), channel_id=1, replica_groups=mesh['req'=64,'tp'=4] {'req'}, dimensions={0} | all-to-all | bytes 4194304 | tf_op jit(solution)/shard_map/all_to_all | solution.py:285
  127.0 5.5 %collective-permute-start.6 = (bf16[64,16,1024]{2,1,0:T(8,128)(2,1)S(1)}, bf16[64,16,1024]{2,1,0:T(8,128)(2,1)S(1)}, u32[]{:S(2)}, u32[]{:S(2)}) collective-permute-start(bf16[64,16,1024]{2,1,0:T(8,128)(2,1)S(1)} %all_to_all.10), channel_id=1, source_target_pairs={{0,1},{1,0},{2,3},{3,2},{4,5},{5,4},{6,7},{7,6},{8,9},{9,8},{10,11... | collective-permute-start | bytes 6291464 | tf_op jit(solution)/shard_map/ppermute | solution.py:286
  132.5 0.3 dynamic-slice_bitcast_fusion.3
  132.8 1.3 fusion.25
  134.1 1.3 fusion.19
  135.4 42.9 %collective-permute-done.6 = bf16[64,16,1024]{2,1,0:T(8,128)(2,1)S(1)} collective-permute-done((bf16[64,16,1024]{2,1,0:T(8,128)(2,1)S(1)}, bf16[64,16,1024]{2,1,0:T(8,128)(2,1)S(1)}, u32[]{:S(2)}, u32[]{:S(2)}) %collective-permute-start.6) | collective-permute-done | bytes 2097184 | tf_op jit(solution)/shard_map/ppermute | solution.py:286
  178.2 1.3 fusion.22
  179.5 1.5 multiply_convert_fusion
  181.0 1.3 collective-permute-start.7
  182.3 1.2 fusion.30
  183.6 15.8 %collective-permute-done.7 = bf16[64,16,352]{2,1,0:T(8,128)(2,1)S(1)} collective-permute-done((bf16[64,16,352]{2,1,0:T(8,128)(2,1)S(1)}, bf16[64,16,352]{2,1,0:T(8,128)(2,1)S(1)}, u32[]{:S(2)}, u32[]{:S(2)}) %collective-permute-start.7) | collective-permute-done | bytes 720928 | tf_op jit(solution)/shard_map/ppermute | solution.py:302
  199.4 3.7 %add_convert_fusion = bf16[64,16,1024]{2,1,0:T(8,128)(2,1)} fusion(f32[64,16,1024]{2,1,0:T(8,128)S(1)} %fusion.30, bf16[64,16,352]{2,1,0:T(8,128)(2,1)S(1)} %collective-permute-done.7, bf16[352,1024]{1,0:T(8,128)(2,1)} %collective-permute-done), kind=kOutput, calls=%fused_computation.1 | convolution fusion | flops 740294656 | bytes 7733248 | tf_op jit(solution)/shard_map/sch,hf->scf/dot_general | solution.py:305
  203.1 7.1 %all-to-all-start.1 = ((bf16[64,16,1024]{2,1,0:T(8,128)(2,1)}), bf16[64,16,1024]{2,1,0:T(8,128)(2,1)}, u32[]{:S(2)}, u32[]{:S(2)}) async-start(bf16[64,16,1024]{2,1,0:T(8,128)(2,1)} %add_convert_fusion), calls=%async_computation.1 | async-start | bytes 4194304 | tf_op jit(solution)/shard_map/all_to_all | solution.py:309
  210.2 0.6 gather_fusion
  210.8 0.4 fusion.6
  211.3 31.3 %all-to-all-done.1 = bf16[64,16,1024]{2,1,0:T(8,128)(2,1)} async-done(((bf16[64,16,1024]{2,1,0:T(8,128)(2,1)}), bf16[64,16,1024]{2,1,0:T(8,128)(2,1)}, u32[]{:S(2)}, u32[]{:S(2)}) %all-to-all-start.1) | async-done | bytes 2097184 | tf_op jit(solution)/shard_map/all_to_all | solution.py:309
  242.6 2.0 fusion.81
  244.7 23.2 %collective-permute-start.8 = (bf16[128,512]{1,0:T(8,128)(2,1)S(1)}, bf16[128,512]{1,0:T(8,128)(2,1)S(1)}, u32[]{:S(2)}, u32[]{:S(2)}) collective-permute-start(bf16[128,512]{1,0:T(8,128)(2,1)S(1)} %dynamic-slice_convert_fusion), channel_id=1, source_target_pairs={{0,2},{1,3},{2,0},{3,1},{4,6},{5,7},{6,4},{7,5},{8,10},{9,11},{10,... | collective-permute-start | bytes 393224 | tf_op jit(solution)/shard_map/ppermute | solution.py:317
  267.9 0.8 convolution_convert_fusion.2
  268.8 5.6 %collective-permute-done.8 = bf16[128,512]{1,0:T(8,128)(2,1)S(1)} collective-permute-done((bf16[128,512]{1,0:T(8,128)(2,1)S(1)}, bf16[128,512]{1,0:T(8,128)(2,1)S(1)}, u32[]{:S(2)}, u32[]{:S(2)}) %collective-permute-start.8) | collective-permute-done | bytes 131104 | tf_op jit(solution)/shard_map/ppermute | solution.py:317
  274.3 0.7 add_convert_fusion.1
  (94 shorter events, 2.2 us)
Async XLA Ops:
  0.6 10.7 %copy-start = (bf16[2,1024,576]{1,2,0:T(8,128)(2,1)S(1)}, bf16[2,1024,576]{1,2,0:T(8,128)(2,1)}, u32[]{:S(2)}) copy-start(bf16[2,1024,576]{1,2,0:T(8,128)(2,1)} %param.21) | copy-start | bytes 7077892
  0.7 5.9 %copy-start.6 = (bf16[128,2048]{1,0:T(8,128)(2,1)S(1)}, bf16[128,2048]{1,0:T(8,128)(2,1)}, u32[]{:S(2)}) copy-start(bf16[128,2048]{1,0:T(8,128)(2,1)} %param.18) | copy-start | bytes 1572868
  0.7 5.9 %copy-start.8 = (bf16[2048,144]{0,1:T(8,128)(2,1)S(1)}, bf16[2048,144]{0,1:T(8,128)(2,1)}, u32[]{:S(2)}) copy-start(bf16[2048,144]{0,1:T(8,128)(2,1)} %param.25) | copy-start | bytes 1769476
  0.7 6.9 %copy-start.25 = (s32[2]{0:T(128)S(1)}, s32[2]{0:T(128)}, u32[]{:S(2)}) copy-start(s32[2]{0:T(128)} %param.22) | copy-start | bytes 28
  0.7 7.0 %copy-start.26 = (s32[2,64]{1,0:T(2,128)S(1)}, s32[2,64]{1,0:T(2,128)}, u32[]{:S(2)}) copy-start(s32[2,64]{1,0:T(2,128)} %param.23) | copy-start | bytes 1540
  3.2 6.0 %copy-start.13 = (bf16[128,256]{1,0:T(8,128)(2,1)S(1)}, bf16[128,256]{1,0:T(8,128)(2,1)}, u32[]{:S(2)}) copy-start(bf16[128,256]{1,0:T(8,128)(2,1)} %param.20) | copy-start | bytes 196612
  3.2 6.2 %copy-start.9 = (bf16[512,512]{1,0:T(8,128)(2,1)S(1)}, bf16[512,512]{1,0:T(8,128)(2,1)}, u32[]{:S(2)}) copy-start(bf16[512,512]{1,0:T(8,128)(2,1)} %param.27) | copy-start | bytes 1572868
  3.2 6.3 %copy-start.12 = (bf16[128,512]{1,0:T(8,128)(2,1)S(1)}, bf16[128,512]{1,0:T(8,128)(2,1)}, u32[]{:S(2)}) copy-start(bf16[128,512]{1,0:T(8,128)(2,1)} %param.19) | copy-start | bytes 393220
  4.2 25.0 %collective-permute-start = (bf16[352,1024]{1,0:T(8,128)(2,1)}, bf16[352,1024]{1,0:T(8,128)(2,1)}, u32[]{:S(2)}, u32[]{:S(2)}) collective-permute-start(bf16[352,1024]{1,0:T(8,128)(2,1)} %pad_maximum_fusion), channel_id=1, source_target_pairs={{0,1},{1,0},{2,3},{3,2},{4,5},{5,4},{6,7},{7,6},{8,9},{9,8},{10,11... | collective-permute-start | bytes 2162696 | tf_op jit(solution)/shard_map/ppermute | solution.py:213
  7.6 15.0 %collective-permute-start.1 = (bf16[128,144]{0,1:T(8,128)(2,1)}, bf16[128,144]{0,1:T(8,128)(2,1)}, u32[]{:S(2)}, u32[]{:S(2)}) collective-permute-start(bf16[128,144]{0,1:T(8,128)(2,1)} %convolution_convert_fusion.4), channel_id=1, source_target_pairs={{0,1},{1,0},{2,3},{3,2},{4,5},{5,4},{6,7},{7,6},{8,9},{9,8},{10,11... | collective-permute-start | bytes 110600 | tf_op jit(solution)/shard_map/ppermute | solution.py:199
  7.7 3.6 %copy-start.16 = (pred[2,1024]{1,0:T(4,128)(4,1)}, pred[2,1024]{1,0:T(4,128)(4,1)S(1)}, u32[]{:S(2)}) copy-start(pred[2,1024]{1,0:T(4,128)(4,1)S(1)} %iota_compare_fusion.12) | copy-start | bytes 6148
  9.4 1.9 copy-start.14
  11.3 4.7 %copy-start.18 = (s32[128,6]{0,1:T(8,128)S(1)}, s32[128,6]{0,1:T(8,128)}, u32[]{:S(2)}) copy-start(s32[128,6]{0,1:T(8,128)} %param.31) | copy-start | bytes 9220
  11.3 8.8 %copy-start.10 = (bf16[512,512]{1,0:T(8,128)(2,1)S(1)}, bf16[512,512]{1,0:T(8,128)(2,1)}, u32[]{:S(2)}) copy-start(bf16[512,512]{1,0:T(8,128)(2,1)} %param.28) | copy-start | bytes 1572868
  15.4 15.1 %copy-start.11 = (bf16[2,256,512]{1,2,0:T(8,128)(2,1)S(1)}, bf16[2,256,512]{1,2,0:T(8,128)(2,1)}, u32[]{:S(2)}) copy-start(bf16[2,256,512]{1,2,0:T(8,128)(2,1)} %copy.63) | copy-start | bytes 1572868
  20.1 10.4 %copy-start.15 = (bf16[2,256,64]{1,2,0:T(8,128)(2,1)S(1)}, bf16[2,256,64]{1,2,0:T(8,128)(2,1)}, u32[]{:S(2)}) copy-start(bf16[2,256,64]{1,2,0:T(8,128)(2,1)} %copy-done.14) | copy-start | bytes 196612
  21.8 8.9 %copy-start.23 = (f32[2,256]{1,0:T(2,128)S(1)}, f32[2,256]{1,0:T(2,128)}, u32[]{:S(2)}) copy-start(f32[2,256]{1,0:T(2,128)} %get-tuple-element.34) | copy-start | bytes 6148
  21.8 8.9 %copy-start.17 = (pred[2,1024]{1,0:T(4,128)(4,1)S(1)}, pred[2,1024]{1,0:T(4,128)(4,1)}, u32[]{:S(2)}) copy-start(pred[2,1024]{1,0:T(4,128)(4,1)} %copy-done.16) | copy-start | bytes 6148
  23.4 5.7 %collective-permute-start.2 = (bf16[128,288]{0,1:T(8,128)(2,1)S(1)}, bf16[128,288]{0,1:T(8,128)(2,1)S(1)}, u32[]{:S(2)}, u32[]{:S(2)}) collective-permute-start(bf16[128,288]{0,1:T(8,128)(2,1)S(1)} %maximum_select_fusion.1), channel_id=1, source_target_pairs={{0,2},{1,3},{2,0},{3,1},{4,6},{5,7},{6,4},{7,5},{8,10},{9,11},{10,... | collective-permute-start | bytes 221192 | tf_op jit(solution)/shard_map/ppermute | solution.py:202
  30.8 2.8 %copy-start.1 = (f32[2,256,1024]{2,1,0:T(8,128)S(1)}, f32[2,256,1024]{2,1,0:T(8,128)}, u32[]{:S(2)}) copy-start(f32[2,256,1024]{2,1,0:T(8,128)} %get-tuple-element.35) | copy-start | bytes 6291460
  37.2 3.9 %copy-start.19 = (s32[128,6]{0,1:T(8,128)S(1)}, s32[128,6]{0,1:T(8,128)}, u32[]{:S(2)}) copy-start(s32[128,6]{0,1:T(8,128)} %param.31) | copy-start | bytes 9220
  37.3 3.9 %copy-start.20 = (s32[128,6]{0,1:T(8,128)S(1)}, s32[128,6]{0,1:T(8,128)}, u32[]{:S(2)}) copy-start(s32[128,6]{0,1:T(8,128)} %copy.72) | copy-start | bytes 9220
  37.3 3.9 %copy-start.7 = (bf16[128,2048]{1,0:T(8,128)(2,1)S(1)}, bf16[128,2048]{1,0:T(8,128)(2,1)}, u32[]{:S(2)}) copy-start(bf16[128,2048]{1,0:T(8,128)(2,1)} %param.18) | copy-start | bytes 1572868
  39.4 8.8 %copy-start.24 = (f32[2048]{0:T(1024)S(1)}, f32[2048]{0:T(1024)}, u32[]{:S(2)}) copy-start(f32[2048]{0:T(1024)} %param.30) | copy-start | bytes 24580
  39.5 5.4 %collective-permute-start.3 = (bf16[128,1024]{1,0:T(8,128)(2,1)S(1)}, bf16[128,1024]{1,0:T(8,128)(2,1)S(1)}, u32[]{:S(2)}, u32[]{:S(2)}) collective-permute-start(bf16[128,1024]{1,0:T(8,128)(2,1)S(1)} %pad_maximum_fusion.4), channel_id=1, source_target_pairs={{0,1},{1,0},{2,3},{3,2},{4,5},{5,4},{6,7},{7,6},{8,9},{9,8},{10,11... | collective-permute-start | bytes 786440 | tf_op jit(solution)/shard_map/ppermute | solution.py:251
  44.9 14.7 %collective-permute-start.4 = (bf16[128,1024]{1,0:T(8,128)(2,1)S(1)}, bf16[128,1024]{1,0:T(8,128)(2,1)S(1)}, u32[]{:S(2)}, u32[]{:S(2)}) collective-permute-start(bf16[128,1024]{1,0:T(8,128)(2,1)S(1)} %fusion.36), channel_id=1, source_target_pairs={{0,2},{1,3},{2,0},{3,1},{4,6},{5,7},{6,4},{7,5},{8,10},{9,11},{10,... | collective-permute-start | bytes 786440 | tf_op jit(solution)/shard_map/ppermute | solution.py:254
  59.8 2.7 collective-permute-start.5
  63.3 69.2 %copy-start.4 = (bf16[1,2048,352]{1,2,0:T(8,128)(2,1)S(1)}, bf16[1,2048,352]{1,2,0:T(8,128)(2,1)}, u32[]{:S(2)}) copy-start(bf16[1,2048,352]{1,2,0:T(8,128)(2,1)} %param.34) | copy-start | bytes 4325380
  63.3 69.2 %copy-start.5 = (bf16[1,2048,352]{1,2,0:T(8,128)(2,1)S(1)}, bf16[1,2048,352]{1,2,0:T(8,128)(2,1)}, u32[]{:S(2)}) copy-start(bf16[1,2048,352]{1,2,0:T(8,128)(2,1)} %param.33) | copy-start | bytes 4325380
  127.0 51.2 %collective-permute-start.6 = (bf16[64,16,1024]{2,1,0:T(8,128)(2,1)S(1)}, bf16[64,16,1024]{2,1,0:T(8,128)(2,1)S(1)}, u32[]{:S(2)}, u32[]{:S(2)}) collective-permute-start(bf16[64,16,1024]{2,1,0:T(8,128)(2,1)S(1)} %all_to_all.10), channel_id=1, source_target_pairs={{0,1},{1,0},{2,3},{3,2},{4,5},{5,4},{6,7},{7,6},{8,9},{9,8},{10,11... | collective-permute-start | bytes 6291464 | tf_op jit(solution)/shard_map/ppermute | solution.py:286
  179.5 2.8 %copy-start.2 = (bf16[352,512]{1,0:T(8,128)(2,1)S(1)}, bf16[352,512]{1,0:T(8,128)(2,1)}, u32[]{:S(2)}) copy-start(bf16[352,512]{1,0:T(8,128)(2,1)} %get-tuple-element.8) | copy-start | bytes 1081348
  179.5 2.8 %copy-start.3 = (bf16[352,512]{1,0:T(8,128)(2,1)S(1)}, bf16[352,512]{1,0:T(8,128)(2,1)}, u32[]{:S(2)}) copy-start(bf16[352,512]{1,0:T(8,128)(2,1)} %get-tuple-element.11) | copy-start | bytes 1081348
  181.0 18.3 %collective-permute-start.7 = (bf16[64,16,352]{2,1,0:T(8,128)(2,1)S(1)}, bf16[64,16,352]{2,1,0:T(8,128)(2,1)S(1)}, u32[]{:S(2)}, u32[]{:S(2)}) collective-permute-start(bf16[64,16,352]{2,1,0:T(8,128)(2,1)S(1)} %multiply_convert_fusion), channel_id=1, source_target_pairs={{0,1},{1,0},{2,3},{3,2},{4,5},{5,4},{6,7},{7,6},{8,9},{9,8},{10,11... | collective-permute-start | bytes 2162696 | tf_op jit(solution)/shard_map/ppermute | solution.py:302
  203.1 7.1 %copy-start.27 = (s32[2]{0:T(128)S(1)}, s32[2]{0:T(128)}, u32[]{:S(2)}) copy-start(s32[2]{0:T(128)} %param.24) | copy-start | bytes 28
  203.1 7.7 %copy-start.22 = (bf16[128,6]{0,1:T(8,128)(2,1)S(1)}, bf16[128,6]{0,1:T(8,128)(2,1)}, u32[]{:S(2)}) copy-start(bf16[128,6]{0,1:T(8,128)(2,1)} %param.32) | copy-start | bytes 4612
  203.1 39.5 %all-to-all-start.1 = ((bf16[64,16,1024]{2,1,0:T(8,128)(2,1)}), bf16[64,16,1024]{2,1,0:T(8,128)(2,1)}, u32[]{:S(2)}, u32[]{:S(2)}) async-start(bf16[64,16,1024]{2,1,0:T(8,128)(2,1)} %add_convert_fusion), calls=%async_computation.1 | async-start | bytes 4194304 | tf_op jit(solution)/shard_map/all_to_all | solution.py:309
  210.2 57.7 %copy-start.21 = (f32[2,64]{1,0:T(2,128)S(1)}, f32[2,64]{1,0:T(2,128)}, u32[]{:S(2)}) copy-start(f32[2,64]{1,0:T(2,128)} %get-tuple-element.30) | copy-start | bytes 1540
  244.7 29.7 %collective-permute-start.8 = (bf16[128,512]{1,0:T(8,128)(2,1)S(1)}, bf16[128,512]{1,0:T(8,128)(2,1)S(1)}, u32[]{:S(2)}, u32[]{:S(2)}) collective-permute-start(bf16[128,512]{1,0:T(8,128)(2,1)S(1)} %dynamic-slice_convert_fusion), channel_id=1, source_target_pairs={{0,2},{1,3},{2,0},{3,1},{4,6},{5,7},{6,4},{7,5},{8,10},{9,11},{10,... | collective-permute-start | bytes 393224 | tf_op jit(solution)/shard_map/ppermute | solution.py:317

commit v7 on v6

--- a/solution.py
+++ b/solution.py
@@ -279,7 +279,8 @@
     chunks = 1
     slot_step = capacity // chunks
     weights_by_slot = weights.reshape(tok_rows, experts_all, capacity)
-    routed_half = jnp.zeros((tok_rows, 2 * quarter), jnp.float32)
+    routed_keep = jnp.zeros((tok_rows, quarter), jnp.float32)
+    routed_give = jnp.zeros((tok_rows, quarter), jnp.float32)
     for chunk in range(chunks):
         slots = slice(chunk * slot_step, (chunk + 1) * slot_step)
         own_rows = lax.all_to_all(outgoing[:, slots], "req", split_axis=0, concat_axis=0, tiled=True)
@@ -307,14 +308,17 @@
             )
         ).astype(jnp.bfloat16)
         shares = lax.all_to_all(pair_value, "req", split_axis=0, concat_axis=0, tiled=True)
-        routed_half = routed_half + jnp.dot(
-            weights_by_slot[:, :, slots].reshape(tok_rows, experts_all * slot_step),
-            shares.reshape(experts_all * slot_step, 2 * quarter),
-            preferred_element_type=jnp.float32,
-        )
-    keep = features(routed_half, upper)
-    give = features(routed_half, 1 - upper)
-    routed = keep + lax.ppermute(give.astype(jnp.bfloat16), "tp", across).astype(jnp.float32)
+        slot_weights = weights_by_slot[:, :, slots].reshape(tok_rows, experts_all * slot_step)
+        share_rows = shares.reshape(experts_all * slot_step, 2 * quarter)
+        routed_give = routed_give + jnp.dot(
+            slot_weights, features(share_rows, 1 - upper), preferred_element_type=jnp.float32
+        )
+        routed_keep = routed_keep + jnp.dot(
+            slot_weights, features(share_rows, upper), preferred_element_type=jnp.float32
+        )
+    routed = routed_keep + lax.ppermute(
+        routed_give.astype(jnp.bfloat16), "tp", across
+    ).astype(jnp.float32)
     layer_out = (residual_quarter + routed).astype(jnp.bfloat16)
     return (layer_out, accepted_rows)
 

time: 276 us -> 277 us (level)
  no operation moved by 1% of the time
where the time goes in v7:
time: 277 us; the launch traced here: 276 us
  waiting for transfers between devices  114 us (41%)
  blocking collectives  63.7 us (23%)
  starting transfers between devices  48.9 us (18%)
  matrix products  30.5 us (11%)
  local copies, waits for them, and re-layouts  10.8 us (4%)
  other arithmetic  6.4 us (2%)
    all_to_all x1, blocking collectives, on_device(): lax.all_to_all(outgoing[:, slots], 'req', split_axis=0, concat_axis=0, ti...  63.7 us
    ppermute x1, waiting for transfers between devices, on_device(): partner_rows = lax.ppermute(own_rows, 'tp', beside)  42.9 us
    all_to_all x1, waiting for transfers between devices, on_device(): lax.all_to_all(pair_value, 'req', split_axis=0, concat_axis=0, tiled=True)  31.3 us
    ppermute x1, starting transfers between devices, on_device(): lax.ppermute(routed_give.astype(jnp.bfloat16), 'tp', across)  23.2 us
    ppermute x1, waiting for transfers between devices, on_device(): partner_hidden = lax.ppermute(expert_hidden, 'tp', beside)  15.8 us
    ppermute x1, waiting for transfers between devices, on_device(): lax.ppermute(pair_sum.astype(jnp.bfloat16), 'tp', across)  10.8 us
    all_to_all x1, starting transfers between devices, on_device(): lax.all_to_all(pair_value, 'req', split_axis=0, concat_axis=0, tiled=True)  7.06 us
    ppermute x1, waiting for transfers between devices, on_device(): lax.ppermute(routed_give.astype(jnp.bfloat16), 'tp', across)  5.57 us
  transfers between devices with their start and end apart: 10, of which 9 were waited for; matrix products, arithmetic and copies ran while one was open for 8% of the time, Pallas kernels for 0%

profile of v7, /device:TPU:1, one launch (start us, length us, event | category | flops | bytes accessed | tf_op | source)
XLA Modules:
  0.0 276.0 jit_solution(4262083760258052676)
XLA Ops:
  0.7 2.5 dynamic-slice_bitcast_fusion.1
  3.2 1.0 pad_maximum_fusion
  4.2 2.5 collective-permute-start
  6.6 0.9 convolution_convert_fusion.5
  7.7 0.2 convolution_minimum_fusion.6
  7.9 0.2 convolution_minimum_fusion.5
  8.1 0.2 convolution_minimum_fusion.4
  8.7 0.2 convolution_minimum_fusion.1
  8.9 0.3 fusion.85
  9.4 0.3 fusion.7
  9.7 0.4 copy.62
  10.3 1.0 copy.63
  11.3 4.1 %fusion.3 = (f32[2,256]{1,0:T(2,128)}, f32[2,256,1024]{2,1,0:T(8,128)}) fusion(pred[2,1024]{1,0:T(4,128)(4,1)S(1)} %iota_compare_fusion.12, bf16[2,1024,576]{1,2,0:T(8,128)(2,1)S(1)} %copy-done, bf16[2,256,64]{1,2,0:T(8,128)(2,1)S(1)} %copy.64, bf16[2,256,512]{1,2,0:T(8,128)(2,1)} %copy.63), kind=kOutput, calls=%fused_computation.10 | convolution fusion | flops 606731776 | bytes 5050368 | tf_op jit(solution)/shard_map/rqk,rck->rqc/dot_general | solution.py:107
  15.4 0.6 broadcast_add_fusion
  16.1 0.7 eq.88
  16.9 1.1 fusion.10
  18.0 0.6 convert_element_type.117
  18.6 0.8 convert_element_type.118
  19.4 0.7 copy.72
  20.1 1.0 copy.75
  21.1 0.7 add.152
  22.0 0.5 collective-permute-done.1
  22.5 0.9 maximum_select_fusion.1
  23.4 4.0 %collective-permute-start.2 = (bf16[128,288]{0,1:T(8,128)(2,1)S(1)}, bf16[128,288]{0,1:T(8,128)(2,1)S(1)}, u32[]{:S(2)}, u32[]{:S(2)}) collective-permute-start(bf16[128,288]{0,1:T(8,128)(2,1)S(1)} %maximum_select_fusion.1), channel_id=1, source_target_pairs={{0,2},{1,3},{2,0},{3,1},{4,6},{5,7},{6,4},{7,5},{8,10},{9,11},{10,... | collective-permute-start | bytes 221192 | tf_op jit(solution)/shard_map/ppermute | solution.py:202
  27.4 1.7 collective-permute-done.2
  29.3 0.8 fusion.42
  30.5 0.2 fusion.86
  30.8 2.8 %fusion.11 = f32[2,256,576]{2,1,0:T(8,128)S(1)} fusion(bf16[2,1024,576]{1,2,0:T(8,128)(2,1)S(1)} %copy-done, f32[2,256,1024]{2,1,0:T(8,128)} %get-tuple-element.35, f32[2,256]{1,0:T(2,128)S(1)} %max.7, pred[2,1024]{1,0:T(4,128)(4,1)S(1)} %copy-done.17), kind=kOutput, calls=%fused_computation.32 | convolution fusion | flops 606076928 | bytes 5640192 | tf_op jit(solution)/shard_map/rqc,rck->rqk/dot_general | solution.py:120
  33.6 0.6 fusion.4
  34.1 0.4 fusion.51
  34.6 0.2 fusion.14
  34.8 0.9 reshape.167
  35.7 1.5 convolution_convert_fusion.3
  37.3 2.1 fusion.87
  39.5 1.6 collective-permute-start.3
  41.2 3.7 %collective-permute-done.3 = bf16[128,1024]{1,0:T(8,128)(2,1)S(1)} collective-permute-done((bf16[128,1024]{1,0:T(8,128)(2,1)S(1)}, bf16[128,1024]{1,0:T(8,128)(2,1)S(1)}, u32[]{:S(2)}, u32[]{:S(2)}) %collective-permute-start.3) | collective-permute-done | bytes 262176 | tf_op jit(solution)/shard_map/ppermute | solution.py:251
  45.0 3.3 %collective-permute-start.4 = (bf16[128,1024]{1,0:T(8,128)(2,1)S(1)}, bf16[128,1024]{1,0:T(8,128)(2,1)S(1)}, u32[]{:S(2)}, u32[]{:S(2)}) collective-permute-start(bf16[128,1024]{1,0:T(8,128)(2,1)S(1)} %fusion.39), channel_id=1, source_target_pairs={{0,2},{1,3},{2,0},{3,1},{4,6},{5,7},{6,4},{7,5},{8,10},{9,11},{10,... | collective-permute-start | bytes 786440 | tf_op jit(solution)/shard_map/ppermute | solution.py:254
  48.3 0.5 fusion
  48.8 10.8 %collective-permute-done.4 = bf16[128,1024]{1,0:T(8,128)(2,1)S(1)} collective-permute-done((bf16[128,1024]{1,0:T(8,128)(2,1)S(1)}, bf16[128,1024]{1,0:T(8,128)(2,1)S(1)}, u32[]{:S(2)}, u32[]{:S(2)}) %collective-permute-start.4) | collective-permute-done | bytes 262176 | tf_op jit(solution)/shard_map/ppermute | solution.py:254
  59.6 0.2 multiply_reduce_fusion
  59.8 0.5 collective-permute-start.5
  60.3 2.2 collective-permute-done.5
  62.5 0.8 convolution_convert_fusion
  63.3 63.7 %all_to_all.10 = bf16[64,16,1024]{2,1,0:T(8,128)(2,1)S(1)} all-to-all(bf16[64,16,1024]{2,1,0:T(8,128)(2,1)S(1)} %bitcast.102), channel_id=1, replica_groups=mesh['req'=64,'tp'=4] {'req'}, dimensions={0} | all-to-all | bytes 4194304 | tf_op jit(solution)/shard_map/all_to_all | solution.py:286
  127.0 5.5 %collective-permute-start.6 = (bf16[64,16,1024]{2,1,0:T(8,128)(2,1)S(1)}, bf16[64,16,1024]{2,1,0:T(8,128)(2,1)S(1)}, u32[]{:S(2)}, u32[]{:S(2)}) collective-permute-start(bf16[64,16,1024]{2,1,0:T(8,128)(2,1)S(1)} %all_to_all.10), channel_id=1, source_target_pairs={{0,1},{1,0},{2,3},{3,2},{4,5},{5,4},{6,7},{7,6},{8,9},{9,8},{10,11... | collective-permute-start | bytes 6291464 | tf_op jit(solution)/shard_map/ppermute | solution.py:287
  132.5 0.3 dynamic-slice_bitcast_fusion.3
  132.9 1.3 fusion.28
  134.1 1.3 fusion.22
  135.4 42.9 %collective-permute-done.6 = bf16[64,16,1024]{2,1,0:T(8,128)(2,1)S(1)} collective-permute-done((bf16[64,16,1024]{2,1,0:T(8,128)(2,1)S(1)}, bf16[64,16,1024]{2,1,0:T(8,128)(2,1)S(1)}, u32[]{:S(2)}, u32[]{:S(2)}) %collective-permute-start.6) | collective-permute-done | bytes 2097184 | tf_op jit(solution)/shard_map/ppermute | solution.py:287
  178.2 1.3 fusion.25
  179.5 1.5 multiply_convert_fusion
  181.1 1.3 collective-permute-start.7
  182.3 1.2 fusion.33
  183.6 15.8 %collective-permute-done.7 = bf16[64,16,352]{2,1,0:T(8,128)(2,1)S(1)} collective-permute-done((bf16[64,16,352]{2,1,0:T(8,128)(2,1)S(1)}, bf16[64,16,352]{2,1,0:T(8,128)(2,1)S(1)}, u32[]{:S(2)}, u32[]{:S(2)}) %collective-permute-start.7) | collective-permute-done | bytes 720928 | tf_op jit(solution)/shard_map/ppermute | solution.py:303
  199.4 3.7 %add_convert_fusion = bf16[64,16,1024]{2,1,0:T(8,128)(2,1)} fusion(f32[64,16,1024]{2,1,0:T(8,128)S(1)} %fusion.33, bf16[64,16,352]{2,1,0:T(8,128)(2,1)S(1)} %collective-permute-done.7, bf16[352,1024]{1,0:T(8,128)(2,1)} %collective-permute-done), kind=kOutput, calls=%fused_computation.1 | convolution fusion | flops 740294656 | bytes 7733248 | tf_op jit(solution)/shard_map/sch,hf->scf/dot_general | solution.py:306
  203.1 7.1 %all-to-all-start.1 = ((bf16[64,16,1024]{2,1,0:T(8,128)(2,1)}), bf16[64,16,1024]{2,1,0:T(8,128)(2,1)}, u32[]{:S(2)}, u32[]{:S(2)}) async-start(bf16[64,16,1024]{2,1,0:T(8,128)(2,1)} %add_convert_fusion), calls=%async_computation.1 | async-start | bytes 4194304 | tf_op jit(solution)/shard_map/all_to_all | solution.py:310
  210.2 0.6 gather_fusion
  210.8 0.4 fusion.6
  211.3 31.3 %all-to-all-done.1 = bf16[64,16,1024]{2,1,0:T(8,128)(2,1)} async-done(((bf16[64,16,1024]{2,1,0:T(8,128)(2,1)}), bf16[64,16,1024]{2,1,0:T(8,128)(2,1)}, u32[]{:S(2)}, u32[]{:S(2)}) %all-to-all-start.1) | async-done | bytes 2097184 | tf_op jit(solution)/shard_map/all_to_all | solution.py:310
  242.6 1.5 convolution_convert_fusion.4
  244.1 23.2 %collective-permute-start.8 = (bf16[128,512]{1,0:T(8,128)(2,1)S(1)}, bf16[128,512]{1,0:T(8,128)(2,1)S(1)}, u32[]{:S(2)}, u32[]{:S(2)}) collective-permute-start(bf16[128,512]{1,0:T(8,128)(2,1)S(1)} %convolution_convert_fusion.4), channel_id=1, source_target_pairs={{0,2},{1,3},{2,0},{3,1},{4,6},{5,7},{6,4},{7,5},{8,10},{9,11},{10,... | collective-permute-start | bytes 393224 | tf_op jit(solution)/shard_map/ppermute | solution.py:319
  267.4 0.8 convolution_convert_fusion.2
  268.2 5.6 %collective-permute-done.8 = bf16[128,512]{1,0:T(8,128)(2,1)S(1)} collective-permute-done((bf16[128,512]{1,0:T(8,128)(2,1)S(1)}, bf16[128,512]{1,0:T(8,128)(2,1)S(1)}, u32[]{:S(2)}, u32[]{:S(2)}) %collective-permute-start.8) | collective-permute-done | bytes 131104 | tf_op jit(solution)/shard_map/ppermute | solution.py:319
  273.8 2.2 add_convert_fusion.1
  (93 shorter events, 2.2 us)
Async XLA Ops:
  0.6 10.7 %copy-start = (bf16[2,1024,576]{1,2,0:T(8,128)(2,1)S(1)}, bf16[2,1024,576]{1,2,0:T(8,128)(2,1)}, u32[]{:S(2)}) copy-start(bf16[2,1024,576]{1,2,0:T(8,128)(2,1)} %param.21) | copy-start | bytes 7077892
  0.7 5.9 %copy-start.6 = (bf16[128,2048]{1,0:T(8,128)(2,1)S(1)}, bf16[128,2048]{1,0:T(8,128)(2,1)}, u32[]{:S(2)}) copy-start(bf16[128,2048]{1,0:T(8,128)(2,1)} %param.18) | copy-start | bytes 1572868
  0.7 5.9 %copy-start.8 = (bf16[2048,144]{0,1:T(8,128)(2,1)S(1)}, bf16[2048,144]{0,1:T(8,128)(2,1)}, u32[]{:S(2)}) copy-start(bf16[2048,144]{0,1:T(8,128)(2,1)} %param.25) | copy-start | bytes 1769476
  0.7 6.9 %copy-start.25 = (s32[2]{0:T(128)S(1)}, s32[2]{0:T(128)}, u32[]{:S(2)}) copy-start(s32[2]{0:T(128)} %param.22) | copy-start | bytes 28
  0.7 7.0 %copy-start.26 = (s32[2,64]{1,0:T(2,128)S(1)}, s32[2,64]{1,0:T(2,128)}, u32[]{:S(2)}) copy-start(s32[2,64]{1,0:T(2,128)} %param.23) | copy-start | bytes 1540
  3.2 6.0 %copy-start.13 = (bf16[128,256]{1,0:T(8,128)(2,1)S(1)}, bf16[128,256]{1,0:T(8,128)(2,1)}, u32[]{:S(2)}) copy-start(bf16[128,256]{1,0:T(8,128)(2,1)} %param.20) | copy-start | bytes 196612
  3.2 6.2 %copy-start.9 = (bf16[512,512]{1,0:T(8,128)(2,1)S(1)}, bf16[512,512]{1,0:T(8,128)(2,1)}, u32[]{:S(2)}) copy-start(bf16[512,512]{1,0:T(8,128)(2,1)} %param.27) | copy-start | bytes 1572868
  3.2 6.2 %copy-start.12 = (bf16[128,512]{1,0:T(8,128)(2,1)S(1)}, bf16[128,512]{1,0:T(8,128)(2,1)}, u32[]{:S(2)}) copy-start(bf16[128,512]{1,0:T(8,128)(2,1)} %param.19) | copy-start | bytes 393220
  4.2 25.0 %collective-permute-start = (bf16[352,1024]{1,0:T(8,128)(2,1)}, bf16[352,1024]{1,0:T(8,128)(2,1)}, u32[]{:S(2)}, u32[]{:S(2)}) collective-permute-start(bf16[352,1024]{1,0:T(8,128)(2,1)} %pad_maximum_fusion), channel_id=1, source_target_pairs={{0,1},{1,0},{2,3},{3,2},{4,5},{5,4},{6,7},{7,6},{8,9},{9,8},{10,11... | collective-permute-start | bytes 2162696 | tf_op jit(solution)/shard_map/ppermute | solution.py:213
  7.6 15.0 %collective-permute-start.1 = (bf16[128,144]{0,1:T(8,128)(2,1)}, bf16[128,144]{0,1:T(8,128)(2,1)}, u32[]{:S(2)}, u32[]{:S(2)}) collective-permute-start(bf16[128,144]{0,1:T(8,128)(2,1)} %convolution_convert_fusion.5), channel_id=1, source_target_pairs={{0,1},{1,0},{2,3},{3,2},{4,5},{5,4},{6,7},{7,6},{8,9},{9,8},{10,11... | collective-permute-start | bytes 110600 | tf_op jit(solution)/shard_map/ppermute | solution.py:199
  7.7 3.6 %copy-start.16 = (pred[2,1024]{1,0:T(4,128)(4,1)}, pred[2,1024]{1,0:T(4,128)(4,1)S(1)}, u32[]{:S(2)}) copy-start(pred[2,1024]{1,0:T(4,128)(4,1)S(1)} %iota_compare_fusion.12) | copy-start | bytes 6148
  9.4 1.9 copy-start.14
  11.3 4.7 %copy-start.18 = (s32[128,6]{0,1:T(8,128)S(1)}, s32[128,6]{0,1:T(8,128)}, u32[]{:S(2)}) copy-start(s32[128,6]{0,1:T(8,128)} %param.31) | copy-start | bytes 9220
  11.3 8.8 %copy-start.10 = (bf16[512,512]{1,0:T(8,128)(2,1)S(1)}, bf16[512,512]{1,0:T(8,128)(2,1)}, u32[]{:S(2)}) copy-start(bf16[512,512]{1,0:T(8,128)(2,1)} %param.28) | copy-start | bytes 1572868
  15.4 15.1 %copy-start.11 = (bf16[2,256,512]{1,2,0:T(8,128)(2,1)S(1)}, bf16[2,256,512]{1,2,0:T(8,128)(2,1)}, u32[]{:S(2)}) copy-start(bf16[2,256,512]{1,2,0:T(8,128)(2,1)} %copy.63) | copy-start | bytes 1572868
  20.1 10.4 %copy-start.15 = (bf16[2,256,64]{1,2,0:T(8,128)(2,1)S(1)}, bf16[2,256,64]{1,2,0:T(8,128)(2,1)}, u32[]{:S(2)}) copy-start(bf16[2,256,64]{1,2,0:T(8,128)(2,1)} %copy-done.14) | copy-start | bytes 196612
  21.9 8.9 %copy-start.23 = (f32[2,256]{1,0:T(2,128)S(1)}, f32[2,256]{1,0:T(2,128)}, u32[]{:S(2)}) copy-start(f32[2,256]{1,0:T(2,128)} %get-tuple-element.34) | copy-start | bytes 6148
  21.9 8.9 %copy-start.17 = (pred[2,1024]{1,0:T(4,128)(4,1)S(1)}, pred[2,1024]{1,0:T(4,128)(4,1)}, u32[]{:S(2)}) copy-start(pred[2,1024]{1,0:T(4,128)(4,1)} %copy-done.16) | copy-start | bytes 6148
  23.4 5.7 %collective-permute-start.2 = (bf16[128,288]{0,1:T(8,128)(2,1)S(1)}, bf16[128,288]{0,1:T(8,128)(2,1)S(1)}, u32[]{:S(2)}, u32[]{:S(2)}) collective-permute-start(bf16[128,288]{0,1:T(8,128)(2,1)S(1)} %maximum_select_fusion.1), channel_id=1, source_target_pairs={{0,2},{1,3},{2,0},{3,1},{4,6},{5,7},{6,4},{7,5},{8,10},{9,11},{10,... | collective-permute-start | bytes 221192 | tf_op jit(solution)/shard_map/ppermute | solution.py:202
  30.8 2.8 %copy-start.1 = (f32[2,256,1024]{2,1,0:T(8,128)S(1)}, f32[2,256,1024]{2,1,0:T(8,128)}, u32[]{:S(2)}) copy-start(f32[2,256,1024]{2,1,0:T(8,128)} %get-tuple-element.35) | copy-start | bytes 6291460
  37.3 3.9 %copy-start.19 = (s32[128,6]{0,1:T(8,128)S(1)}, s32[128,6]{0,1:T(8,128)}, u32[]{:S(2)}) copy-start(s32[128,6]{0,1:T(8,128)} %param.31) | copy-start | bytes 9220
  37.3 3.9 %copy-start.20 = (s32[128,6]{0,1:T(8,128)S(1)}, s32[128,6]{0,1:T(8,128)}, u32[]{:S(2)}) copy-start(s32[128,6]{0,1:T(8,128)} %copy.72) | copy-start | bytes 9220
  37.3 3.9 %copy-start.7 = (bf16[128,2048]{1,0:T(8,128)(2,1)S(1)}, bf16[128,2048]{1,0:T(8,128)(2,1)}, u32[]{:S(2)}) copy-start(bf16[128,2048]{1,0:T(8,128)(2,1)} %param.18) | copy-start | bytes 1572868
  39.4 8.8 %copy-start.24 = (f32[2048]{0:T(1024)S(1)}, f32[2048]{0:T(1024)}, u32[]{:S(2)}) copy-start(f32[2048]{0:T(1024)} %param.30) | copy-start | bytes 24580
  39.5 5.4 %collective-permute-start.3 = (bf16[128,1024]{1,0:T(8,128)(2,1)S(1)}, bf16[128,1024]{1,0:T(8,128)(2,1)S(1)}, u32[]{:S(2)}, u32[]{:S(2)}) collective-permute-start(bf16[128,1024]{1,0:T(8,128)(2,1)S(1)} %pad_maximum_fusion.4), channel_id=1, source_target_pairs={{0,1},{1,0},{2,3},{3,2},{4,5},{5,4},{6,7},{7,6},{8,9},{9,8},{10,11... | collective-permute-start | bytes 786440 | tf_op jit(solution)/shard_map/ppermute | solution.py:251
  45.0 14.7 %collective-permute-start.4 = (bf16[128,1024]{1,0:T(8,128)(2,1)S(1)}, bf16[128,1024]{1,0:T(8,128)(2,1)S(1)}, u32[]{:S(2)}, u32[]{:S(2)}) collective-permute-start(bf16[128,1024]{1,0:T(8,128)(2,1)S(1)} %fusion.39), channel_id=1, source_target_pairs={{0,2},{1,3},{2,0},{3,1},{4,6},{5,7},{6,4},{7,5},{8,10},{9,11},{10,... | collective-permute-start | bytes 786440 | tf_op jit(solution)/shard_map/ppermute | solution.py:254
  59.8 2.7 collective-permute-start.5
  63.3 69.2 %copy-start.4 = (bf16[1,2048,352]{1,2,0:T(8,128)(2,1)S(1)}, bf16[1,2048,352]{1,2,0:T(8,128)(2,1)}, u32[]{:S(2)}) copy-start(bf16[1,2048,352]{1,2,0:T(8,128)(2,1)} %param.34) | copy-start | bytes 4325380
  63.3 69.2 %copy-start.5 = (bf16[1,2048,352]{1,2,0:T(8,128)(2,1)S(1)}, bf16[1,2048,352]{1,2,0:T(8,128)(2,1)}, u32[]{:S(2)}) copy-start(bf16[1,2048,352]{1,2,0:T(8,128)(2,1)} %param.33) | copy-start | bytes 4325380
  127.0 51.2 %collective-permute-start.6 = (bf16[64,16,1024]{2,1,0:T(8,128)(2,1)S(1)}, bf16[64,16,1024]{2,1,0:T(8,128)(2,1)S(1)}, u32[]{:S(2)}, u32[]{:S(2)}) collective-permute-start(bf16[64,16,1024]{2,1,0:T(8,128)(2,1)S(1)} %all_to_all.10), channel_id=1, source_target_pairs={{0,1},{1,0},{2,3},{3,2},{4,5},{5,4},{6,7},{7,6},{8,9},{9,8},{10,11... | collective-permute-start | bytes 6291464 | tf_op jit(solution)/shard_map/ppermute | solution.py:287
  179.5 2.8 %copy-start.2 = (bf16[352,512]{1,0:T(8,128)(2,1)S(1)}, bf16[352,512]{1,0:T(8,128)(2,1)}, u32[]{:S(2)}) copy-start(bf16[352,512]{1,0:T(8,128)(2,1)} %get-tuple-element.8) | copy-start | bytes 1081348
  179.5 2.8 %copy-start.3 = (bf16[352,512]{1,0:T(8,128)(2,1)S(1)}, bf16[352,512]{1,0:T(8,128)(2,1)}, u32[]{:S(2)}) copy-start(bf16[352,512]{1,0:T(8,128)(2,1)} %get-tuple-element.11) | copy-start | bytes 1081348
  181.1 18.3 %collective-permute-start.7 = (bf16[64,16,352]{2,1,0:T(8,128)(2,1)S(1)}, bf16[64,16,352]{2,1,0:T(8,128)(2,1)S(1)}, u32[]{:S(2)}, u32[]{:S(2)}) collective-permute-start(bf16[64,16,352]{2,1,0:T(8,128)(2,1)S(1)} %multiply_convert_fusion), channel_id=1, source_target_pairs={{0,1},{1,0},{2,3},{3,2},{4,5},{5,4},{6,7},{7,6},{8,9},{9,8},{10,11... | collective-permute-start | bytes 2162696 | tf_op jit(solution)/shard_map/ppermute | solution.py:303
  203.1 7.1 %copy-start.27 = (s32[2]{0:T(128)S(1)}, s32[2]{0:T(128)}, u32[]{:S(2)}) copy-start(s32[2]{0:T(128)} %param.24) | copy-start | bytes 28
  203.1 7.7 %copy-start.22 = (bf16[128,6]{0,1:T(8,128)(2,1)S(1)}, bf16[128,6]{0,1:T(8,128)(2,1)}, u32[]{:S(2)}) copy-start(bf16[128,6]{0,1:T(8,128)(2,1)} %param.32) | copy-start | bytes 4612
  203.1 64.3 %copy-start.21 = (f32[2,64]{1,0:T(2,128)S(1)}, f32[2,64]{1,0:T(2,128)}, u32[]{:S(2)}) copy-start(f32[2,64]{1,0:T(2,128)} %get-tuple-element.30) | copy-start | bytes 1540
  203.1 39.5 %all-to-all-start.1 = ((bf16[64,16,1024]{2,1,0:T(8,128)(2,1)}), bf16[64,16,1024]{2,1,0:T(8,128)(2,1)}, u32[]{:S(2)}, u32[]{:S(2)}) async-start(bf16[64,16,1024]{2,1,0:T(8,128)(2,1)} %add_convert_fusion), calls=%async_computation.1 | async-start | bytes 4194304 | tf_op jit(solution)/shard_map/all_to_all | solution.py:310
  244.1 29.7 %collective-permute-start.8 = (bf16[128,512]{1,0:T(8,128)(2,1)S(1)}, bf16[128,512]{1,0:T(8,128)(2,1)S(1)}, u32[]{:S(2)}, u32[]{:S(2)}) collective-permute-start(bf16[128,512]{1,0:T(8,128)(2,1)S(1)} %convolution_convert_fusion.4), channel_id=1, source_target_pairs={{0,2},{1,3},{2,0},{3,1},{4,6},{5,7},{6,4},{7,5},{8,10},{9,11},{10,... | collective-permute-start | bytes 393224 | tf_op jit(solution)/shard_map/ppermute | solution.py:319

commit v8 on v6

--- a/solution.py
+++ b/solution.py
@@ -194,17 +194,16 @@
     def features(block, first):
         return lax.dynamic_slice_in_dim(block, first * quarter, quarter, block.ndim - 1)
 
-    pair_block = jnp.where(
-        parity == 0,
-        jnp.concatenate([compressed_part, lax.ppermute(compressed_part, "tp", beside)], 1),
-        jnp.concatenate([lax.ppermute(compressed_part, "tp", beside), compressed_part], 1),
-    )
-    other_block = lax.ppermute(pair_block, "tp", [(t, t ^ 2) for t in range(tp_size)])
-    compressed = jnp.where(
-        tp_index // 2 == 0,
-        jnp.concatenate([pair_block, other_block], 1),
-        jnp.concatenate([other_block, pair_block], 1),
-    )
+    blocks = jnp.stack(
+        [compressed_part]
+        + [
+            lax.ppermute(compressed_part, "tp", [(t, t ^ step) for t in range(tp_size)])
+            for step in range(1, tp_size)
+        ],
+        0,
+    )
+    ordered = jnp.take(blocks, jnp.arange(tp_size, dtype=jnp.int32) ^ tp_index, axis=0)
+    compressed = jnp.transpose(ordered, (1, 0, 2)).reshape(tok_rows, -1)
     down_local = w_down[0]
     down_own = jnp.concatenate([features(down_local, parity), features(down_local, parity + 2)], -1)
     down_given = jnp.concatenate(

time: 276 us -> 277 us (level)
  other arithmetic: 7.1 us -> 10 us
  transfers between devices with their start and end apart: 10 -> 11, of which waited for: 9 -> 7; matrix products, arithmetic and copies ran while one was open for 8% -> 10% of each run, Pallas kernels for 0% -> 0%
where the time goes in v8:
time: 277 us; the launch traced here: 276 us
  waiting for transfers between devices  116 us (42%)
  blocking collectives  61.9 us (22%)
  starting transfers between devices  46.2 us (17%)
  matrix products  30 us (11%)
  local copies, waits for them, and re-layouts  10.8 us (4%)
  other arithmetic  10 us (4%)
    all_to_all x1, blocking collectives, on_device(): lax.all_to_all(outgoing[:, slots], 'req', split_axis=0, concat_axis=0, ti...  61.9 us
    ppermute x1, waiting for transfers between devices, on_device(): partner_rows = lax.ppermute(own_rows, 'tp', beside)  42.9 us
    all_to_all x1, waiting for transfers between devices, on_device(): lax.all_to_all(pair_value, 'req', split_axis=0, concat_axis=0, tiled=True)  31.5 us
    ppermute x1, starting transfers between devices, on_device(): lax.ppermute(give.astype(jnp.bfloat16), 'tp', across).astype(jnp.float32)  23 us
    ppermute x1, waiting for transfers between devices, on_device(): partner_hidden = lax.ppermute(expert_hidden, 'tp', beside)  15.9 us
    ppermute x1, waiting for transfers between devices, on_device(): lax.ppermute(pair_sum.astype(jnp.bfloat16), 'tp', across)  11.5 us
    all_to_all x1, starting transfers between devices, on_device(): lax.all_to_all(pair_value, 'req', split_axis=0, concat_axis=0, tiled=True)  6.89 us
    ppermute x1, waiting for transfers between devices, on_device(): lax.ppermute(half_of(attention, 1 - parity).astype(jnp.bfloat16), 'tp', b...  5.95 us
  transfers between devices with their start and end apart: 11, of which 7 were waited for; matrix products, arithmetic and copies ran while one was open for 10% of the time, Pallas kernels for 0%

profile of v8, /device:TPU:1, one launch (start us, length us, event | category | flops | bytes accessed | tf_op | source)
XLA Modules:
  0.0 276.2 jit_solution(8969430469687786080)
XLA Ops:
  0.6 2.3 convolution_convert_fusion.4
  3.0 5.2 %collective-permute-start.3 = (bf16[128,144]{0,1:T(8,128)(2,1)}, bf16[128,144]{0,1:T(8,128)(2,1)}, u32[]{:S(2)}, u32[]{:S(2)}) collective-permute-start(bf16[128,144]{0,1:T(8,128)(2,1)} %convolution_convert_fusion.4), channel_id=1, source_target_pairs={{0,3},{1,2},{2,1},{3,0},{4,7},{5,6},{6,5},{7,4},{8,11},{9,10},{10,... | collective-permute-start | bytes 110600 | tf_op jit(solution)/shard_map/ppermute | solution.py:200
  8.1 0.3 collective-permute-start.1
  8.4 2.3 dynamic-slice_bitcast_fusion.1
  10.8 1.0 pad_maximum_fusion
  11.7 1.2 collective-permute-start
  13.3 1.0 fusion.10
  14.3 0.6 pad_clamp_fusion
  16.1 0.3 fusion.79
  16.6 0.3 fusion.7
  16.9 0.4 copy.60
  17.5 1.0 copy.61
  18.5 0.7 broadcast_add_fusion
  19.2 4.1 %fusion.3 = (f32[2,256]{1,0:T(2,128)}, f32[2,256,1024]{2,1,0:T(8,128)}) fusion(pred[2,1024]{1,0:T(4,128)(4,1)S(1)} %iota_compare_fusion.12, bf16[2,1024,576]{1,2,0:T(8,128)(2,1)S(1)} %copy-done, bf16[2,256,64]{1,2,0:T(8,128)(2,1)S(1)} %copy.62, bf16[2,256,512]{1,2,0:T(8,128)(2,1)} %copy.61), kind=kOutput, calls=%fused_computation.11 | convolution fusion | flops 606731776 | bytes 5050368 | tf_op jit(solution)/shard_map/rqk,rck->rqc/dot_general | solution.py:107
  23.2 0.5 compare_and_fusion.1
  23.8 0.5 multiply_power_fusion
  24.3 0.6 convert_element_type.117
  24.9 0.8 convert_element_type.118
  25.7 0.7 copy.70
  26.4 1.0 copy.73
  27.4 0.8 add.169
  28.4 0.8 pad_maximum_fusion.5
  29.3 0.7 gather_fusion
  30.0 0.7 broadcast_select_fusion
  30.8 0.8 fusion.39
  31.6 0.8 fusion.63
  32.6 0.2 fusion.80
  32.9 2.8 %fusion.11 = f32[2,256,576]{2,1,0:T(8,128)S(1)} fusion(bf16[2,1024,576]{1,2,0:T(8,128)(2,1)S(1)} %copy-done, f32[2,256,1024]{2,1,0:T(8,128)} %get-tuple-element.35, f32[2,256]{1,0:T(2,128)S(1)} %max.7, pred[2,1024]{1,0:T(4,128)(4,1)S(1)} %copy-done.15), kind=kOutput, calls=%fused_computation.32 | convolution fusion | flops 606076928 | bytes 5640192 | tf_op jit(solution)/shard_map/rqc,rck->rqk/dot_general | solution.py:120
  35.7 0.6 fusion.4
  36.2 0.4 fusion.48
  36.7 0.2 fusion.14
  36.9 0.9 reshape.192
  37.8 1.5 convolution_convert_fusion.3
  39.4 2.1 fusion.81
  41.6 0.4 collective-permute-start.4
  42.1 5.9 %collective-permute-done.4 = bf16[128,1024]{1,0:T(8,128)(2,1)S(1)} collective-permute-done((bf16[128,1024]{1,0:T(8,128)(2,1)S(1)}, bf16[128,1024]{1,0:T(8,128)(2,1)S(1)}, u32[]{:S(2)}, u32[]{:S(2)}) %collective-permute-start.4) | collective-permute-done | bytes 262176 | tf_op jit(solution)/shard_map/ppermute | solution.py:250
  48.1 2.2 collective-permute-start.5
  50.3 0.5 fusion
  50.8 11.5 %collective-permute-done.5 = bf16[128,1024]{1,0:T(8,128)(2,1)S(1)} collective-permute-done((bf16[128,1024]{1,0:T(8,128)(2,1)S(1)}, bf16[128,1024]{1,0:T(8,128)(2,1)S(1)}, u32[]{:S(2)}, u32[]{:S(2)}) %collective-permute-start.5) | collective-permute-done | bytes 262176 | tf_op jit(solution)/shard_map/ppermute | solution.py:253
  62.3 0.2 multiply_reduce_fusion
  62.5 0.3 collective-permute-start.6
  62.8 2.4 collective-permute-done.6
  65.2 0.8 convolution_convert_fusion
  66.0 61.9 %all_to_all.10 = bf16[64,16,1024]{2,1,0:T(8,128)(2,1)S(1)} all-to-all(bf16[64,16,1024]{2,1,0:T(8,128)(2,1)S(1)} %bitcast.111), channel_id=1, replica_groups=mesh['req'=64,'tp'=4] {'req'}, dimensions={0} | all-to-all | bytes 4194304 | tf_op jit(solution)/shard_map/all_to_all | solution.py:284
  128.0 5.7 %collective-permute-start.7 = (bf16[64,16,1024]{2,1,0:T(8,128)(2,1)S(1)}, bf16[64,16,1024]{2,1,0:T(8,128)(2,1)S(1)}, u32[]{:S(2)}, u32[]{:S(2)}) collective-permute-start(bf16[64,16,1024]{2,1,0:T(8,128)(2,1)S(1)} %all_to_all.10), channel_id=1, source_target_pairs={{0,1},{1,0},{2,3},{3,2},{4,5},{5,4},{6,7},{7,6},{8,9},{9,8},{10,11... | collective-permute-start | bytes 6291464 | tf_op jit(solution)/shard_map/ppermute | solution.py:285
  133.7 0.3 dynamic-slice_bitcast_fusion.3
  134.0 1.3 fusion.25
  135.3 1.3 fusion.19
  136.5 42.9 %collective-permute-done.7 = bf16[64,16,1024]{2,1,0:T(8,128)(2,1)S(1)} collective-permute-done((bf16[64,16,1024]{2,1,0:T(8,128)(2,1)S(1)}, bf16[64,16,1024]{2,1,0:T(8,128)(2,1)S(1)}, u32[]{:S(2)}, u32[]{:S(2)}) %collective-permute-start.7) | collective-permute-done | bytes 2097184 | tf_op jit(solution)/shard_map/ppermute | solution.py:285
  179.5 1.3 fusion.22
  180.7 1.5 multiply_convert_fusion
  182.3 1.3 collective-permute-start.8
  183.5 1.2 fusion.30
  184.8 15.9 %collective-permute-done.8 = bf16[64,16,352]{2,1,0:T(8,128)(2,1)S(1)} collective-permute-done((bf16[64,16,352]{2,1,0:T(8,128)(2,1)S(1)}, bf16[64,16,352]{2,1,0:T(8,128)(2,1)S(1)}, u32[]{:S(2)}, u32[]{:S(2)}) %collective-permute-start.8) | collective-permute-done | bytes 720928 | tf_op jit(solution)/shard_map/ppermute | solution.py:301
  200.7 3.7 %add_convert_fusion = bf16[64,16,1024]{2,1,0:T(8,128)(2,1)} fusion(f32[64,16,1024]{2,1,0:T(8,128)S(1)} %fusion.30, bf16[64,16,352]{2,1,0:T(8,128)(2,1)S(1)} %collective-permute-done.8, bf16[352,1024]{1,0:T(8,128)(2,1)} %collective-permute-done), kind=kOutput, calls=%fused_computation.2 | convolution fusion | flops 740294656 | bytes 7733248 | tf_op jit(solution)/shard_map/sch,hf->scf/dot_general | solution.py:304
  204.4 6.9 %all-to-all-start.1 = ((bf16[64,16,1024]{2,1,0:T(8,128)(2,1)}), bf16[64,16,1024]{2,1,0:T(8,128)(2,1)}, u32[]{:S(2)}, u32[]{:S(2)}) async-start(bf16[64,16,1024]{2,1,0:T(8,128)(2,1)} %add_convert_fusion), calls=%async_computation.1 | async-start | bytes 4194304 | tf_op jit(solution)/shard_map/all_to_all | solution.py:308
  211.3 0.6 gather_fusion.1
  211.9 0.4 fusion.6
  212.4 31.5 %all-to-all-done.1 = bf16[64,16,1024]{2,1,0:T(8,128)(2,1)} async-done(((bf16[64,16,1024]{2,1,0:T(8,128)(2,1)}), bf16[64,16,1024]{2,1,0:T(8,128)(2,1)}, u32[]{:S(2)}, u32[]{:S(2)}) %all-to-all-start.1) | async-done | bytes 2097184 | tf_op jit(solution)/shard_map/all_to_all | solution.py:308
  243.9 2.0 fusion.82
  246.0 23.0 %collective-permute-start.9 = (bf16[128,512]{1,0:T(8,128)(2,1)S(1)}, bf16[128,512]{1,0:T(8,128)(2,1)S(1)}, u32[]{:S(2)}, u32[]{:S(2)}) collective-permute-start(bf16[128,512]{1,0:T(8,128)(2,1)S(1)} %dynamic-slice_convert_fusion), channel_id=1, source_target_pairs={{0,2},{1,3},{2,0},{3,1},{4,6},{5,7},{6,4},{7,5},{8,10},{9,11},{10,... | collective-permute-start | bytes 393224 | tf_op jit(solution)/shard_map/ppermute | solution.py:316
  269.0 0.8 convolution_convert_fusion.2
  269.8 5.6 %collective-permute-done.9 = bf16[128,512]{1,0:T(8,128)(2,1)S(1)} collective-permute-done((bf16[128,512]{1,0:T(8,128)(2,1)S(1)}, bf16[128,512]{1,0:T(8,128)(2,1)S(1)}, u32[]{:S(2)}, u32[]{:S(2)}) %collective-permute-start.9) | collective-permute-done | bytes 131104 | tf_op jit(solution)/shard_map/ppermute | solution.py:316
  275.5 0.7 add_convert_fusion.1
  (98 shorter events, 2.9 us)
Async XLA Ops:
  0.6 18.5 %copy-start = (bf16[2,1024,576]{1,2,0:T(8,128)(2,1)S(1)}, bf16[2,1024,576]{1,2,0:T(8,128)(2,1)}, u32[]{:S(2)}) copy-start(bf16[2,1024,576]{1,2,0:T(8,128)(2,1)} %param.21) | copy-start | bytes 7077892
  3.0 25.4 %collective-permute-start.3 = (bf16[128,144]{0,1:T(8,128)(2,1)}, bf16[128,144]{0,1:T(8,128)(2,1)}, u32[]{:S(2)}, u32[]{:S(2)}) collective-permute-start(bf16[128,144]{0,1:T(8,128)(2,1)} %convolution_convert_fusion.4), channel_id=1, source_target_pairs={{0,3},{1,2},{2,1},{3,0},{4,7},{5,6},{6,5},{7,4},{8,11},{9,10},{10,... | collective-permute-start | bytes 110600 | tf_op jit(solution)/shard_map/ppermute | solution.py:200
  8.1 20.3 %collective-permute-start.2 = (bf16[128,144]{0,1:T(8,128)(2,1)}, bf16[128,144]{0,1:T(8,128)(2,1)}, u32[]{:S(2)}, u32[]{:S(2)}) collective-permute-start(bf16[128,144]{0,1:T(8,128)(2,1)} %convolution_convert_fusion.4), channel_id=1, source_target_pairs={{0,2},{1,3},{2,0},{3,1},{4,6},{5,7},{6,4},{7,5},{8,10},{9,11},{10,... | collective-permute-start | bytes 110600 | tf_op jit(solution)/shard_map/ppermute | solution.py:200
  8.1 20.3 %collective-permute-start.1 = (bf16[128,144]{0,1:T(8,128)(2,1)}, bf16[128,144]{0,1:T(8,128)(2,1)}, u32[]{:S(2)}, u32[]{:S(2)}) collective-permute-start(bf16[128,144]{0,1:T(8,128)(2,1)} %convolution_convert_fusion.4), channel_id=1, source_target_pairs={{0,1},{1,0},{2,3},{3,2},{4,5},{5,4},{6,7},{7,6},{8,9},{9,8},{10,11... | collective-permute-start | bytes 110600 | tf_op jit(solution)/shard_map/ppermute | solution.py:200
  8.4 4.5 %copy-start.24 = (s32[2]{0:T(128)S(1)}, s32[2]{0:T(128)}, u32[]{:S(2)}) copy-start(s32[2]{0:T(128)} %param.22) | copy-start | bytes 28
  8.4 4.6 %copy-start.16 = (s32[128,6]{0,1:T(8,128)S(1)}, s32[128,6]{0,1:T(8,128)}, u32[]{:S(2)}) copy-start(s32[128,6]{0,1:T(8,128)} %param.31) | copy-start | bytes 9220
  8.4 6.4 %copy-start.25 = (s32[2,64]{1,0:T(2,128)S(1)}, s32[2,64]{1,0:T(2,128)}, u32[]{:S(2)}) copy-start(s32[2,64]{1,0:T(2,128)} %param.23) | copy-start | bytes 1540
  10.8 5.6 %copy-start.11 = (bf16[128,256]{1,0:T(8,128)(2,1)S(1)}, bf16[128,256]{1,0:T(8,128)(2,1)}, u32[]{:S(2)}) copy-start(bf16[128,256]{1,0:T(8,128)(2,1)} %param.20) | copy-start | bytes 196612
  10.8 5.8 %copy-start.7 = (bf16[512,512]{1,0:T(8,128)(2,1)S(1)}, bf16[512,512]{1,0:T(8,128)(2,1)}, u32[]{:S(2)}) copy-start(bf16[512,512]{1,0:T(8,128)(2,1)} %param.27) | copy-start | bytes 1572868
  10.8 5.9 %copy-start.10 = (bf16[128,512]{1,0:T(8,128)(2,1)S(1)}, bf16[128,512]{1,0:T(8,128)(2,1)}, u32[]{:S(2)}) copy-start(bf16[128,512]{1,0:T(8,128)(2,1)} %param.19) | copy-start | bytes 393220
  11.7 18.9 %collective-permute-start = (bf16[352,1024]{1,0:T(8,128)(2,1)}, bf16[352,1024]{1,0:T(8,128)(2,1)}, u32[]{:S(2)}, u32[]{:S(2)}) collective-permute-start(bf16[352,1024]{1,0:T(8,128)(2,1)} %pad_maximum_fusion), channel_id=1, source_target_pairs={{0,1},{1,0},{2,3},{3,2},{4,5},{5,4},{6,7},{7,6},{8,9},{9,8},{10,11... | collective-permute-start | bytes 2162696 | tf_op jit(solution)/shard_map/ppermute | solution.py:212
  13.0 6.1 %copy-start.14 = (pred[2,1024]{1,0:T(4,128)(4,1)}, pred[2,1024]{1,0:T(4,128)(4,1)S(1)}, u32[]{:S(2)}) copy-start(pred[2,1024]{1,0:T(4,128)(4,1)S(1)} %iota_compare_fusion.12) | copy-start | bytes 6148
  16.6 2.5 copy-start.12
  19.1 5.2 %copy-start.20 = (f32[768]{0:T(1024)S(1)}, f32[768]{0:T(1024)}, u32[]{:S(2)}) copy-start(f32[768]{0:T(1024)} %fusion.10) | copy-start | bytes 9220
  19.1 7.3 %copy-start.8 = (bf16[512,512]{1,0:T(8,128)(2,1)S(1)}, bf16[512,512]{1,0:T(8,128)(2,1)}, u32[]{:S(2)}) copy-start(bf16[512,512]{1,0:T(8,128)(2,1)} %param.28) | copy-start | bytes 1572868
  23.2 9.3 %copy-start.9 = (bf16[2,256,512]{1,2,0:T(8,128)(2,1)S(1)}, bf16[2,256,512]{1,2,0:T(8,128)(2,1)}, u32[]{:S(2)}) copy-start(bf16[2,256,512]{1,2,0:T(8,128)(2,1)} %copy.61) | copy-start | bytes 1572868
  26.4 6.2 %copy-start.13 = (bf16[2,256,64]{1,2,0:T(8,128)(2,1)S(1)}, bf16[2,256,64]{1,2,0:T(8,128)(2,1)}, u32[]{:S(2)}) copy-start(bf16[2,256,64]{1,2,0:T(8,128)(2,1)} %copy-done.12) | copy-start | bytes 196612
  28.2 4.6 %copy-start.22 = (f32[2,256]{1,0:T(2,128)S(1)}, f32[2,256]{1,0:T(2,128)}, u32[]{:S(2)}) copy-start(f32[2,256]{1,0:T(2,128)} %get-tuple-element.34) | copy-start | bytes 6148
  28.2 4.6 %copy-start.15 = (pred[2,1024]{1,0:T(4,128)(4,1)S(1)}, pred[2,1024]{1,0:T(4,128)(4,1)}, u32[]{:S(2)}) copy-start(pred[2,1024]{1,0:T(4,128)(4,1)} %copy-done.14) | copy-start | bytes 6148
  32.9 2.8 %copy-start.1 = (f32[2,256,1024]{2,1,0:T(8,128)S(1)}, f32[2,256,1024]{2,1,0:T(8,128)}, u32[]{:S(2)}) copy-start(f32[2,256,1024]{2,1,0:T(8,128)} %get-tuple-element.35) | copy-start | bytes 6291460
  39.3 2.6 copy-start.17
  39.4 2.6 copy-start.18
  39.4 2.6 copy-start.6
  41.5 8.7 %copy-start.23 = (f32[2048]{0:T(1024)S(1)}, f32[2048]{0:T(1024)}, u32[]{:S(2)}) copy-start(f32[2048]{0:T(1024)} %param.30) | copy-start | bytes 24580
  41.6 6.4 %collective-permute-start.4 = (bf16[128,1024]{1,0:T(8,128)(2,1)S(1)}, bf16[128,1024]{1,0:T(8,128)(2,1)S(1)}, u32[]{:S(2)}, u32[]{:S(2)}) collective-permute-start(bf16[128,1024]{1,0:T(8,128)(2,1)S(1)} %pad_maximum_fusion.4), channel_id=1, source_target_pairs={{0,1},{1,0},{2,3},{3,2},{4,5},{5,4},{6,7},{7,6},{8,9},{9,8},{10,11... | collective-permute-start | bytes 786440 | tf_op jit(solution)/shard_map/ppermute | solution.py:250
  48.1 14.2 %collective-permute-start.5 = (bf16[128,1024]{1,0:T(8,128)(2,1)S(1)}, bf16[128,1024]{1,0:T(8,128)(2,1)S(1)}, u32[]{:S(2)}, u32[]{:S(2)}) collective-permute-start(bf16[128,1024]{1,0:T(8,128)(2,1)S(1)} %fusion.36), channel_id=1, source_target_pairs={{0,2},{1,3},{2,0},{3,1},{4,6},{5,7},{6,4},{7,5},{8,10},{9,11},{10,... | collective-permute-start | bytes 786440 | tf_op jit(solution)/shard_map/ppermute | solution.py:253
  62.5 2.7 collective-permute-start.6
  66.0 67.6 %copy-start.4 = (bf16[1,2048,352]{1,2,0:T(8,128)(2,1)S(1)}, bf16[1,2048,352]{1,2,0:T(8,128)(2,1)}, u32[]{:S(2)}) copy-start(bf16[1,2048,352]{1,2,0:T(8,128)(2,1)} %param.34) | copy-start | bytes 4325380
  66.0 67.6 %copy-start.5 = (bf16[1,2048,352]{1,2,0:T(8,128)(2,1)S(1)}, bf16[1,2048,352]{1,2,0:T(8,128)(2,1)}, u32[]{:S(2)}) copy-start(bf16[1,2048,352]{1,2,0:T(8,128)(2,1)} %param.33) | copy-start | bytes 4325380
  128.0 51.5 %collective-permute-start.7 = (bf16[64,16,1024]{2,1,0:T(8,128)(2,1)S(1)}, bf16[64,16,1024]{2,1,0:T(8,128)(2,1)S(1)}, u32[]{:S(2)}, u32[]{:S(2)}) collective-permute-start(bf16[64,16,1024]{2,1,0:T(8,128)(2,1)S(1)} %all_to_all.10), channel_id=1, source_target_pairs={{0,1},{1,0},{2,3},{3,2},{4,5},{5,4},{6,7},{7,6},{8,9},{9,8},{10,11... | collective-permute-start | bytes 6291464 | tf_op jit(solution)/shard_map/ppermute | solution.py:285
  180.7 2.8 %copy-start.2 = (bf16[352,512]{1,0:T(8,128)(2,1)S(1)}, bf16[352,512]{1,0:T(8,128)(2,1)}, u32[]{:S(2)}) copy-start(bf16[352,512]{1,0:T(8,128)(2,1)} %get-tuple-element.8) | copy-start | bytes 1081348
  180.7 2.8 %copy-start.3 = (bf16[352,512]{1,0:T(8,128)(2,1)S(1)}, bf16[352,512]{1,0:T(8,128)(2,1)}, u32[]{:S(2)}) copy-start(bf16[352,512]{1,0:T(8,128)(2,1)} %get-tuple-element.11) | copy-start | bytes 1081348
  182.3 18.4 %collective-permute-start.8 = (bf16[64,16,352]{2,1,0:T(8,128)(2,1)S(1)}, bf16[64,16,352]{2,1,0:T(8,128)(2,1)S(1)}, u32[]{:S(2)}, u32[]{:S(2)}) collective-permute-start(bf16[64,16,352]{2,1,0:T(8,128)(2,1)S(1)} %multiply_convert_fusion), channel_id=1, source_target_pairs={{0,1},{1,0},{2,3},{3,2},{4,5},{5,4},{6,7},{7,6},{8,9},{9,8},{10,11... | collective-permute-start | bytes 2162696 | tf_op jit(solution)/shard_map/ppermute | solution.py:301
  204.4 6.9 %copy-start.26 = (s32[2]{0:T(128)S(1)}, s32[2]{0:T(128)}, u32[]{:S(2)}) copy-start(s32[2]{0:T(128)} %param.24) | copy-start | bytes 28
  204.4 7.5 %copy-start.21 = (bf16[128,6]{0,1:T(8,128)(2,1)S(1)}, bf16[128,6]{0,1:T(8,128)(2,1)}, u32[]{:S(2)}) copy-start(bf16[128,6]{0,1:T(8,128)(2,1)} %param.32) | copy-start | bytes 4612
  204.4 39.5 %all-to-all-start.1 = ((bf16[64,16,1024]{2,1,0:T(8,128)(2,1)}), bf16[64,16,1024]{2,1,0:T(8,128)(2,1)}, u32[]{:S(2)}, u32[]{:S(2)}) async-start(bf16[64,16,1024]{2,1,0:T(8,128)(2,1)} %add_convert_fusion), calls=%async_computation.1 | async-start | bytes 4194304 | tf_op jit(solution)/shard_map/all_to_all | solution.py:308
  211.3 57.7 %copy-start.19 = (f32[2,64]{1,0:T(2,128)S(1)}, f32[2,64]{1,0:T(2,128)}, u32[]{:S(2)}) copy-start(f32[2,64]{1,0:T(2,128)} %get-tuple-element.30) | copy-start | bytes 1540
  246.0 29.4 %collective-permute-start.9 = (bf16[128,512]{1,0:T(8,128)(2,1)S(1)}, bf16[128,512]{1,0:T(8,128)(2,1)S(1)}, u32[]{:S(2)}, u32[]{:S(2)}) collective-permute-start(bf16[128,512]{1,0:T(8,128)(2,1)S(1)} %dynamic-slice_convert_fusion), channel_id=1, source_target_pairs={{0,2},{1,3},{2,0},{3,1},{4,6},{5,7},{6,4},{7,5},{8,10},{9,11},{10,... | collective-permute-start | bytes 393224 | tf_op jit(solution)/shard_map/ppermute | solution.py:316

commit v9 on v6

--- a/solution.py
+++ b/solution.py
@@ -245,12 +245,13 @@
     def half_of(block, which):
         return jnp.concatenate([features(block, which), features(block, which + 2)], -1)
 
-    attention = jnp.dot(
-        head_out.reshape(tok_rows, local_heads * VDIM), o_proj, preferred_element_type=jnp.float32
-    )
-    pair_sum = half_of(attention, parity) + lax.ppermute(
-        half_of(attention, 1 - parity).astype(jnp.bfloat16), "tp", beside
-    ).astype(jnp.float32)
+    head_rows = head_out.reshape(tok_rows, local_heads * VDIM)
+    given_attention = jnp.dot(
+        head_rows, half_of(o_proj, 1 - parity), preferred_element_type=jnp.float32
+    )
+    pair_sum = jnp.dot(
+        head_rows, half_of(o_proj, parity), preferred_element_type=jnp.float32
+    ) + lax.ppermute(given_attention.astype(jnp.bfloat16), "tp", beside).astype(jnp.float32)
     attention_half = pair_sum + lax.ppermute(
         pair_sum.astype(jnp.bfloat16), "tp", across
     ).astype(jnp.float32)

time: 276 us -> 279 us (1.011)
  local copies, waits for them, and re-layouts: 10.8 us -> 13.7 us
  transfers between devices with their start and end apart: 10 -> 10, of which waited for: 9 -> 9; matrix products, arithmetic and copies ran while one was open for 8% -> 9% of each run, Pallas kernels for 0% -> 0%
where the time goes in v9:
time: 279 us
  waiting for transfers between devices  113 us (41%)
  blocking collectives  63.2 us (23%)
  starting transfers between devices  48.9 us (18%)
  matrix products  31 us (11%)
  local copies, waits for them, and re-layouts  13.7 us (5%)
  other arithmetic  7.5 us (3%)
    all_to_all x1, blocking collectives, on_device(): lax.all_to_all(outgoing[:, slots], 'req', split_axis=0, concat_axis=0, ti...  63.2 us
    ppermute x1, waiting for transfers between devices, on_device(): partner_rows = lax.ppermute(own_rows, 'tp', beside)  42.9 us
    all_to_all x1, waiting for transfers between devices, on_device(): lax.all_to_all(pair_value, 'req', split_axis=0, concat_axis=0, tiled=True)  30.4 us
    ppermute x1, starting transfers between devices, on_device(): lax.ppermute(give.astype(jnp.bfloat16), 'tp', across).astype(jnp.float32)  23.2 us
    ppermute x1, waiting for transfers between devices, on_device(): partner_hidden = lax.ppermute(expert_hidden, 'tp', beside)  15.8 us
    ppermute x1, waiting for transfers between devices, on_device(): lax.ppermute(pair_sum.astype(jnp.bfloat16), 'tp', across)  10.3 us
    all_to_all x1, starting transfers between devices, on_device(): lax.all_to_all(pair_value, 'req', split_axis=0, concat_axis=0, tiled=True)  7.06 us
  transfers between devices with their start and end apart: 10, of which 9 were waited for; matrix products, arithmetic and copies ran while one was open for 9% of the time, Pallas kernels for 0%

profile of v9, /device:TPU:1, one launch (start us, length us, event | category | flops | bytes accessed | tf_op | source)
XLA Modules:
  0.0 278.7 jit_solution(12640910745192137044)
XLA Ops:
  0.7 2.5 dynamic-slice_bitcast_fusion.1
  3.2 0.9 pad_maximum_fusion
  4.1 2.5 collective-permute-start
  6.6 0.9 convolution_convert_fusion.5
  7.7 0.2 convolution_minimum_fusion.6
  8.9 0.3 fusion.87
  9.4 0.3 fusion.7
  9.7 0.4 copy.62
  10.3 0.2 copy.63
  10.5 0.7 broadcast_add_fusion
  11.3 3.0 %fusion.3 = (f32[2,256]{1,0:T(2,128)}, f32[2,256,1024]{2,1,0:T(8,128)}) fusion(pred[2,1024]{1,0:T(4,128)(4,1)S(1)} %iota_compare_fusion.12, bf16[2,1024,576]{1,2,0:T(8,128)(2,1)S(1)} %copy-done, bf16[2,256,64]{1,2,0:T(8,128)(2,1)S(1)} %copy.64, bf16[2,256,512]{1,2,0:T(8,128)(2,1)S(1)} %copy.63), kind=kOutput, calls=%fused_computation.10 | convolution fusion | flops 606731776 | bytes 5050368 | tf_op jit(solution)/shard_map/rqk,rck->rqc/dot_general | solution.py:107
  14.3 1.2 constant_dynamic-slice_fusion.1
  15.6 0.7 eq.88
  16.4 1.7 fusion.10
  18.1 1.0 copy.75
  19.1 0.7 add.152
  20.0 2.5 collective-permute-done.1
  22.5 0.9 maximum_select_fusion.1
  23.4 4.0 %collective-permute-start.2 = (bf16[128,288]{0,1:T(8,128)(2,1)S(1)}, bf16[128,288]{0,1:T(8,128)(2,1)S(1)}, u32[]{:S(2)}, u32[]{:S(2)}) collective-permute-start(bf16[128,288]{0,1:T(8,128)(2,1)S(1)} %maximum_select_fusion.1), channel_id=1, source_target_pairs={{0,2},{1,3},{2,0},{3,1},{4,6},{5,7},{6,4},{7,5},{8,10},{9,11},{10,... | collective-permute-start | bytes 221192 | tf_op jit(solution)/shard_map/ppermute | solution.py:202
  27.4 1.7 collective-permute-done.2
  29.3 0.8 fusion.46
  30.5 1.3 fusion.88
  31.9 2.8 fusion.11
  34.6 0.6 fusion.4
  35.2 0.4 fusion.55
  35.7 0.2 fusion.14
  35.9 1.0 reshape.167
  36.9 1.6 convolution_convert_fusion.4
  38.5 2.3 convolution_convert_fusion.2
  40.8 1.5 collective-permute-start.3
  42.3 0.7 constant_dynamic-slice_fusion.5
  43.0 0.8 convert_element_type.121
  43.7 0.9 copy.72
  44.7 1.7 collective-permute-done.3
  46.4 1.3 fusion.43
  47.7 3.3 %collective-permute-start.4 = (bf16[128,1024]{1,0:T(8,128)(2,1)S(1)}, bf16[128,1024]{1,0:T(8,128)(2,1)S(1)}, u32[]{:S(2)}, u32[]{:S(2)}) collective-permute-start(bf16[128,1024]{1,0:T(8,128)(2,1)S(1)} %get-tuple-element.38), channel_id=1, source_target_pairs={{0,2},{1,3},{2,0},{3,1},{4,6},{5,7},{6,4},{7,5},{8,10},{9,11},{10,... | collective-permute-start | bytes 786440 | tf_op jit(solution)/shard_map/ppermute | solution.py:255
  51.1 0.8 fusion.86
  51.8 0.5 fusion
  52.3 10.3 %collective-permute-done.4 = bf16[128,1024]{1,0:T(8,128)(2,1)S(1)} collective-permute-done((bf16[128,1024]{1,0:T(8,128)(2,1)S(1)}, bf16[128,1024]{1,0:T(8,128)(2,1)S(1)}, u32[]{:S(2)}, u32[]{:S(2)}) %collective-permute-start.4) | collective-permute-done | bytes 262176 | tf_op jit(solution)/shard_map/ppermute | solution.py:255
  62.7 1.2 multiply_reduce_fusion
  63.8 0.5 collective-permute-start.5
  64.3 2.2 collective-permute-done.5
  66.5 0.8 convolution_convert_fusion
  67.3 63.2 %all_to_all.10 = bf16[64,16,1024]{2,1,0:T(8,128)(2,1)S(1)} all-to-all(bf16[64,16,1024]{2,1,0:T(8,128)(2,1)S(1)} %bitcast.102), channel_id=1, replica_groups=mesh['req'=64,'tp'=4] {'req'}, dimensions={0} | all-to-all | bytes 4194304 | tf_op jit(solution)/shard_map/all_to_all | solution.py:286
  130.6 5.6 %collective-permute-start.6 = (bf16[64,16,1024]{2,1,0:T(8,128)(2,1)S(1)}, bf16[64,16,1024]{2,1,0:T(8,128)(2,1)S(1)}, u32[]{:S(2)}, u32[]{:S(2)}) collective-permute-start(bf16[64,16,1024]{2,1,0:T(8,128)(2,1)S(1)} %all_to_all.10), channel_id=1, source_target_pairs={{0,1},{1,0},{2,3},{3,2},{4,5},{5,4},{6,7},{7,6},{8,9},{9,8},{10,11... | collective-permute-start | bytes 6291464 | tf_op jit(solution)/shard_map/ppermute | solution.py:287
  136.1 0.3 dynamic-slice_bitcast_fusion.3
  136.5 1.3 fusion.32
  137.8 1.3 fusion.26
  139.0 42.9 %collective-permute-done.6 = bf16[64,16,1024]{2,1,0:T(8,128)(2,1)S(1)} collective-permute-done((bf16[64,16,1024]{2,1,0:T(8,128)(2,1)S(1)}, bf16[64,16,1024]{2,1,0:T(8,128)(2,1)S(1)}, u32[]{:S(2)}, u32[]{:S(2)}) %collective-permute-start.6) | collective-permute-done | bytes 2097184 | tf_op jit(solution)/shard_map/ppermute | solution.py:287
  181.9 1.3 fusion.29
  183.2 1.5 multiply_convert_fusion
  184.7 1.3 collective-permute-start.7
  186.0 1.2 fusion.37
  187.2 15.8 %collective-permute-done.7 = bf16[64,16,352]{2,1,0:T(8,128)(2,1)S(1)} collective-permute-done((bf16[64,16,352]{2,1,0:T(8,128)(2,1)S(1)}, bf16[64,16,352]{2,1,0:T(8,128)(2,1)S(1)}, u32[]{:S(2)}, u32[]{:S(2)}) %collective-permute-start.7) | collective-permute-done | bytes 720928 | tf_op jit(solution)/shard_map/ppermute | solution.py:303
  203.0 3.7 %add_convert_fusion = bf16[64,16,1024]{2,1,0:T(8,128)(2,1)} fusion(f32[64,16,1024]{2,1,0:T(8,128)S(1)} %fusion.37, bf16[64,16,352]{2,1,0:T(8,128)(2,1)S(1)} %collective-permute-done.7, bf16[352,1024]{1,0:T(8,128)(2,1)} %collective-permute-done), kind=kOutput, calls=%fused_computation.1 | convolution fusion | flops 740294656 | bytes 7733248 | tf_op jit(solution)/shard_map/sch,hf->scf/dot_general | solution.py:306
  206.7 7.1 %all-to-all-start.1 = ((bf16[64,16,1024]{2,1,0:T(8,128)(2,1)}), bf16[64,16,1024]{2,1,0:T(8,128)(2,1)}, u32[]{:S(2)}, u32[]{:S(2)}) async-start(bf16[64,16,1024]{2,1,0:T(8,128)(2,1)} %add_convert_fusion), calls=%async_computation.1 | async-start | bytes 4194304 | tf_op jit(solution)/shard_map/all_to_all | solution.py:310
  213.9 1.4 gather_fusion
  215.3 0.4 fusion.6
  215.9 30.4 %all-to-all-done.1 = bf16[64,16,1024]{2,1,0:T(8,128)(2,1)} async-done(((bf16[64,16,1024]{2,1,0:T(8,128)(2,1)}), bf16[64,16,1024]{2,1,0:T(8,128)(2,1)}, u32[]{:S(2)}, u32[]{:S(2)}) %all-to-all-start.1) | async-done | bytes 2097184 | tf_op jit(solution)/shard_map/all_to_all | solution.py:310
  246.2 2.0 fusion.89
  248.3 23.2 %collective-permute-start.8 = (bf16[128,512]{1,0:T(8,128)(2,1)S(1)}, bf16[128,512]{1,0:T(8,128)(2,1)S(1)}, u32[]{:S(2)}, u32[]{:S(2)}) collective-permute-start(bf16[128,512]{1,0:T(8,128)(2,1)S(1)} %dynamic-slice_convert_fusion), channel_id=1, source_target_pairs={{0,2},{1,3},{2,0},{3,1},{4,6},{5,7},{6,4},{7,5},{8,10},{9,11},{10,... | collective-permute-start | bytes 393224 | tf_op jit(solution)/shard_map/ppermute | solution.py:318
  271.6 0.8 convolution_convert_fusion.3
  272.4 5.6 %collective-permute-done.8 = bf16[128,512]{1,0:T(8,128)(2,1)S(1)} collective-permute-done((bf16[128,512]{1,0:T(8,128)(2,1)S(1)}, bf16[128,512]{1,0:T(8,128)(2,1)S(1)}, u32[]{:S(2)}, u32[]{:S(2)}) %collective-permute-start.8) | collective-permute-done | bytes 131104 | tf_op jit(solution)/shard_map/ppermute | solution.py:318
  278.0 0.7 add_convert_fusion.1
  (104 shorter events, 2.7 us)
Async XLA Ops:
  0.6 10.7 %copy-start = (bf16[2,1024,576]{1,2,0:T(8,128)(2,1)S(1)}, bf16[2,1024,576]{1,2,0:T(8,128)(2,1)}, u32[]{:S(2)}) copy-start(bf16[2,1024,576]{1,2,0:T(8,128)(2,1)} %param.21) | copy-start | bytes 7077892
  0.7 5.9 %copy-start.10 = (bf16[128,2048]{1,0:T(8,128)(2,1)S(1)}, bf16[128,2048]{1,0:T(8,128)(2,1)}, u32[]{:S(2)}) copy-start(bf16[128,2048]{1,0:T(8,128)(2,1)} %param.18) | copy-start | bytes 1572868
  0.7 5.9 %copy-start.12 = (bf16[2048,144]{0,1:T(8,128)(2,1)S(1)}, bf16[2048,144]{0,1:T(8,128)(2,1)}, u32[]{:S(2)}) copy-start(bf16[2048,144]{0,1:T(8,128)(2,1)} %param.25) | copy-start | bytes 1769476
  0.7 6.9 %copy-start.31 = (s32[2]{0:T(128)S(1)}, s32[2]{0:T(128)}, u32[]{:S(2)}) copy-start(s32[2]{0:T(128)} %param.22) | copy-start | bytes 28
  0.7 6.9 %copy-start.32 = (s32[2,64]{1,0:T(2,128)S(1)}, s32[2,64]{1,0:T(2,128)}, u32[]{:S(2)}) copy-start(s32[2,64]{1,0:T(2,128)} %param.23) | copy-start | bytes 1540
  3.2 6.0 %copy-start.20 = (bf16[128,256]{1,0:T(8,128)(2,1)S(1)}, bf16[128,256]{1,0:T(8,128)(2,1)}, u32[]{:S(2)}) copy-start(bf16[128,256]{1,0:T(8,128)(2,1)} %param.20) | copy-start | bytes 196612
  3.2 6.2 %copy-start.13 = (bf16[512,512]{1,0:T(8,128)(2,1)S(1)}, bf16[512,512]{1,0:T(8,128)(2,1)}, u32[]{:S(2)}) copy-start(bf16[512,512]{1,0:T(8,128)(2,1)} %param.27) | copy-start | bytes 1572868
  3.2 6.2 %copy-start.18 = (bf16[128,512]{1,0:T(8,128)(2,1)S(1)}, bf16[128,512]{1,0:T(8,128)(2,1)}, u32[]{:S(2)}) copy-start(bf16[128,512]{1,0:T(8,128)(2,1)} %param.19) | copy-start | bytes 393220
  4.1 25.0 %collective-permute-start = (bf16[352,1024]{1,0:T(8,128)(2,1)}, bf16[352,1024]{1,0:T(8,128)(2,1)}, u32[]{:S(2)}, u32[]{:S(2)}) collective-permute-start(bf16[352,1024]{1,0:T(8,128)(2,1)} %pad_maximum_fusion), channel_id=1, source_target_pairs={{0,1},{1,0},{2,3},{3,2},{4,5},{5,4},{6,7},{7,6},{8,9},{9,8},{10,11... | collective-permute-start | bytes 2162696 | tf_op jit(solution)/shard_map/ppermute | solution.py:213
  7.5 15.0 %collective-permute-start.1 = (bf16[128,144]{0,1:T(8,128)(2,1)}, bf16[128,144]{0,1:T(8,128)(2,1)}, u32[]{:S(2)}, u32[]{:S(2)}) collective-permute-start(bf16[128,144]{0,1:T(8,128)(2,1)} %convolution_convert_fusion.5), channel_id=1, source_target_pairs={{0,1},{1,0},{2,3},{3,2},{4,5},{5,4},{6,7},{7,6},{8,9},{9,8},{10,11... | collective-permute-start | bytes 110600 | tf_op jit(solution)/shard_map/ppermute | solution.py:199
  7.7 3.6 %copy-start.23 = (pred[2,1024]{1,0:T(4,128)(4,1)}, pred[2,1024]{1,0:T(4,128)(4,1)S(1)}, u32[]{:S(2)}) copy-start(pred[2,1024]{1,0:T(4,128)(4,1)S(1)} %iota_compare_fusion.12) | copy-start | bytes 6148
  9.2 7.2 %copy-start.17 = (f32[2,64,64]{2,1,0:T(8,128)}, f32[2,64,64]{2,1,0:T(8,128)S(1)}, u32[]{:S(2)}) copy-start(f32[2,64,64]{2,1,0:T(8,128)S(1)} %get-tuple-element.33) | copy-start | bytes 98308
  9.4 1.8 copy-start.21
  10.5 0.8 copy-start.15
  11.3 3.0 %copy-start.2 = (bf16[512,2048]{1,0:T(8,128)(2,1)S(1)}, bf16[512,2048]{1,0:T(8,128)(2,1)}, u32[]{:S(2)}) copy-start(bf16[512,2048]{1,0:T(8,128)(2,1)} %param.29) | copy-start | bytes 6291460
  14.3 1.2 copy-start.25
  14.3 3.8 %copy-start.14 = (bf16[512,512]{1,0:T(8,128)(2,1)S(1)}, bf16[512,512]{1,0:T(8,128)(2,1)}, u32[]{:S(2)}) copy-start(bf16[512,512]{1,0:T(8,128)(2,1)} %param.28) | copy-start | bytes 1572868
  16.3 14.1 %copy-start.22 = (bf16[2,256,64]{1,2,0:T(8,128)(2,1)S(1)}, bf16[2,256,64]{1,2,0:T(8,128)(2,1)}, u32[]{:S(2)}) copy-start(bf16[2,256,64]{1,2,0:T(8,128)(2,1)} %copy-done.21) | copy-start | bytes 196612
  18.1 13.7 %copy-start.30 = (f32[2,256]{1,0:T(2,128)S(1)}, f32[2,256]{1,0:T(2,128)}, u32[]{:S(2)}) copy-start(f32[2,256]{1,0:T(2,128)} %get-tuple-element.34) | copy-start | bytes 6148
  18.1 13.8 %copy-start.24 = (pred[2,1024]{1,0:T(4,128)(4,1)S(1)}, pred[2,1024]{1,0:T(4,128)(4,1)}, u32[]{:S(2)}) copy-start(pred[2,1024]{1,0:T(4,128)(4,1)} %copy-done.23) | copy-start | bytes 6148
  23.4 5.7 %collective-permute-start.2 = (bf16[128,288]{0,1:T(8,128)(2,1)S(1)}, bf16[128,288]{0,1:T(8,128)(2,1)S(1)}, u32[]{:S(2)}, u32[]{:S(2)}) collective-permute-start(bf16[128,288]{0,1:T(8,128)(2,1)S(1)} %maximum_select_fusion.1), channel_id=1, source_target_pairs={{0,2},{1,3},{2,0},{3,1},{4,6},{5,7},{6,4},{7,5},{8,10},{9,11},{10,... | collective-permute-start | bytes 221192 | tf_op jit(solution)/shard_map/ppermute | solution.py:202
  30.4 4.8 %copy-start.4 = (bf16[128,576]{1,0:T(8,128)(2,1)}, bf16[128,576]{1,0:T(8,128)(2,1)S(1)}, u32[]{:S(2)}) copy-start(bf16[128,576]{1,0:T(8,128)(2,1)S(1)} %copy.67) | copy-start | bytes 442372
  31.8 2.8 %copy-start.1 = (f32[2,256,1024]{2,1,0:T(8,128)S(1)}, f32[2,256,1024]{2,1,0:T(8,128)}, u32[]{:S(2)}) copy-start(f32[2,256,1024]{2,1,0:T(8,128)} %get-tuple-element.35) | copy-start | bytes 6291460
  35.9 7.1 %copy-start.28 = (f32[768]{0:T(1024)S(1)}, f32[768]{0:T(1024)}, u32[]{:S(2)}) copy-start(f32[768]{0:T(1024)} %fusion.10) | copy-start | bytes 9220
  36.9 5.4 %copy-start.11 = (bf16[128,2048]{1,0:T(8,128)(2,1)S(1)}, bf16[128,2048]{1,0:T(8,128)(2,1)}, u32[]{:S(2)}) copy-start(bf16[128,2048]{1,0:T(8,128)(2,1)} %param.18) | copy-start | bytes 1572868
  36.9 7.8 %copy-start.26 = (s32[128,6]{0,1:T(8,128)S(1)}, s32[128,6]{0,1:T(8,128)}, u32[]{:S(2)}) copy-start(s32[128,6]{0,1:T(8,128)} %param.31) | copy-start | bytes 9220
  36.9 9.5 %copy-start.3 = (bf16[512,512]{1,0:T(8,128)(2,1)S(1)}, bf16[512,512]{1,0:T(8,128)(2,1)}, u32[]{:S(2)}) copy-start(bf16[512,512]{1,0:T(8,128)(2,1)} %get-tuple-element.10) | copy-start | bytes 1572868
  38.5 4.5 %copy-start.19 = (bf16[4,128,128]{1,2,0:T(8,128)(2,1)}, bf16[4,128,128]{1,2,0:T(8,128)(2,1)S(1)}, u32[]{:S(2)}) copy-start(bf16[4,128,128]{1,2,0:T(8,128)(2,1)S(1)} %convolution_convert_fusion.4) | copy-start | bytes 393220
  40.8 5.6 %collective-permute-start.3 = (bf16[128,1024]{1,0:T(8,128)(2,1)}, bf16[128,1024]{1,0:T(8,128)(2,1)}, u32[]{:S(2)}, u32[]{:S(2)}) collective-permute-start(bf16[128,1024]{1,0:T(8,128)(2,1)} %convolution_convert_fusion.2), channel_id=1, source_target_pairs={{0,1},{1,0},{2,3},{3,2},{4,5},{5,4},{6,7},{7,6},{8,9},{9,8},{10,11... | collective-permute-start | bytes 786440 | tf_op jit(solution)/shard_map/ppermute | solution.py:254
  44.6 18.0 %copy-start.16 = (bf16[128,512]{1,0:T(8,128)(2,1)S(1)}, bf16[128,512]{1,0:T(8,128)(2,1)}, u32[]{:S(2)}) copy-start(bf16[128,512]{1,0:T(8,128)(2,1)} %get-tuple-element.25) | copy-start | bytes 393220
  47.7 14.9 %collective-permute-start.4 = (bf16[128,1024]{1,0:T(8,128)(2,1)S(1)}, bf16[128,1024]{1,0:T(8,128)(2,1)S(1)}, u32[]{:S(2)}, u32[]{:S(2)}) collective-permute-start(bf16[128,1024]{1,0:T(8,128)(2,1)S(1)} %get-tuple-element.38), channel_id=1, source_target_pairs={{0,2},{1,3},{2,0},{3,1},{4,6},{5,7},{6,4},{7,5},{8,10},{9,11},{10,... | collective-permute-start | bytes 786440 | tf_op jit(solution)/shard_map/ppermute | solution.py:255
  63.8 2.7 collective-permute-start.5
  67.3 68.8 %copy-start.8 = (bf16[1,2048,352]{1,2,0:T(8,128)(2,1)S(1)}, bf16[1,2048,352]{1,2,0:T(8,128)(2,1)}, u32[]{:S(2)}) copy-start(bf16[1,2048,352]{1,2,0:T(8,128)(2,1)} %param.34) | copy-start | bytes 4325380
  67.3 68.8 %copy-start.9 = (bf16[1,2048,352]{1,2,0:T(8,128)(2,1)S(1)}, bf16[1,2048,352]{1,2,0:T(8,128)(2,1)}, u32[]{:S(2)}) copy-start(bf16[1,2048,352]{1,2,0:T(8,128)(2,1)} %param.33) | copy-start | bytes 4325380
  130.6 51.3 %collective-permute-start.6 = (bf16[64,16,1024]{2,1,0:T(8,128)(2,1)S(1)}, bf16[64,16,1024]{2,1,0:T(8,128)(2,1)S(1)}, u32[]{:S(2)}, u32[]{:S(2)}) collective-permute-start(bf16[64,16,1024]{2,1,0:T(8,128)(2,1)S(1)} %all_to_all.10), channel_id=1, source_target_pairs={{0,1},{1,0},{2,3},{3,2},{4,5},{5,4},{6,7},{7,6},{8,9},{9,8},{10,11... | collective-permute-start | bytes 6291464 | tf_op jit(solution)/shard_map/ppermute | solution.py:287
  183.1 2.8 %copy-start.6 = (bf16[352,512]{1,0:T(8,128)(2,1)S(1)}, bf16[352,512]{1,0:T(8,128)(2,1)}, u32[]{:S(2)}) copy-start(bf16[352,512]{1,0:T(8,128)(2,1)} %get-tuple-element.12) | copy-start | bytes 1081348
  183.2 2.8 %copy-start.7 = (bf16[352,512]{1,0:T(8,128)(2,1)S(1)}, bf16[352,512]{1,0:T(8,128)(2,1)}, u32[]{:S(2)}) copy-start(bf16[352,512]{1,0:T(8,128)(2,1)} %get-tuple-element.15) | copy-start | bytes 1081348
  184.7 18.3 %collective-permute-start.7 = (bf16[64,16,352]{2,1,0:T(8,128)(2,1)S(1)}, bf16[64,16,352]{2,1,0:T(8,128)(2,1)S(1)}, u32[]{:S(2)}, u32[]{:S(2)}) collective-permute-start(bf16[64,16,352]{2,1,0:T(8,128)(2,1)S(1)} %multiply_convert_fusion), channel_id=1, source_target_pairs={{0,1},{1,0},{2,3},{3,2},{4,5},{5,4},{6,7},{7,6},{8,9},{9,8},{10,11... | collective-permute-start | bytes 2162696 | tf_op jit(solution)/shard_map/ppermute | solution.py:303
  206.7 7.1 %copy-start.33 = (s32[2]{0:T(128)S(1)}, s32[2]{0:T(128)}, u32[]{:S(2)}) copy-start(s32[2]{0:T(128)} %param.24) | copy-start | bytes 28
  206.7 8.6 %copy-start.29 = (bf16[128,6]{0,1:T(8,128)(2,1)S(1)}, bf16[128,6]{0,1:T(8,128)(2,1)}, u32[]{:S(2)}) copy-start(bf16[128,6]{0,1:T(8,128)(2,1)} %param.32) | copy-start | bytes 4612
  206.7 39.5 %all-to-all-start.1 = ((bf16[64,16,1024]{2,1,0:T(8,128)(2,1)}), bf16[64,16,1024]{2,1,0:T(8,128)(2,1)}, u32[]{:S(2)}, u32[]{:S(2)}) async-start(bf16[64,16,1024]{2,1,0:T(8,128)(2,1)} %add_convert_fusion), calls=%async_computation.1 | async-start | bytes 4194304 | tf_op jit(solution)/shard_map/all_to_all | solution.py:310
  213.8 57.7 %copy-start.5 = (bf16[128,576]{1,0:T(8,128)(2,1)S(1)}, bf16[128,576]{1,0:T(8,128)(2,1)}, u32[]{:S(2)}) copy-start(bf16[128,576]{1,0:T(8,128)(2,1)} %copy-done.4) | copy-start | bytes 442372
  213.8 57.7 %copy-start.27 = (f32[2,64]{1,0:T(2,128)S(1)}, f32[2,64]{1,0:T(2,128)}, u32[]{:S(2)}) copy-start(f32[2,64]{1,0:T(2,128)} %get-tuple-element.30) | copy-start | bytes 1540
  248.3 29.7 %collective-permute-start.8 = (bf16[128,512]{1,0:T(8,128)(2,1)S(1)}, bf16[128,512]{1,0:T(8,128)(2,1)S(1)}, u32[]{:S(2)}, u32[]{:S(2)}) collective-permute-start(bf16[128,512]{1,0:T(8,128)(2,1)S(1)} %dynamic-slice_convert_fusion), channel_id=1, source_target_pairs={{0,2},{1,3},{2,0},{3,1},{4,6},{5,7},{6,4},{7,5},{8,10},{9,11},{10,... | collective-permute-start | bytes 393224 | tf_op jit(solution)/shard_map/ppermute | solution.py:318
